TPU v7x, 512 devices: a whole 4x4x16 slice. The times are simulated.
512 devices in a mesh: dp: 16 (over z_hi, x), seq: 32 (over y, z_lo, core).
Axes of the slice: x: 4, y: 4, z: 16 (z_hi: 4, z_lo: 4; z = z_hi * 4 + z_lo), core: 2. Of those that a mesh axis runs over, the one named last changes fastest.
Arguments:
- binned_signals: bfloat16 [16, 16384, 768], P('dp', 'seq'), may hold values from -6 to 6
- kernel_coefficients: bfloat16 [5, 768, 768], P(None, 'dp'), may hold values from -0.09375 to 0.09375
- asking_projector: bfloat16 [768, 256], replicated, may hold values from -0.21875 to 0.21875
- lookup_projector: bfloat16 [768, 256], replicated, may hold values from -0.21875 to 0.21875
- content_projector: bfloat16 [768, 384], replicated, may hold values from -0.21875 to 0.21875
- readout_projector: bfloat16 [384, 768], replicated, may hold values from -0.3125 to 0.3125
- logit_multipliers: float32 [4], replicated, may hold values from 8 to 24
- loss_sensitivity: bfloat16 [16, 4096, 768], P('dp', 'seq'), may hold values from -0.0234375 to 0.0234375
Outputs:
- pooled: bfloat16 [16, 4096, 768], P('dp', 'seq')
- update: float32 [16, 4096, 768], P('dp', 'seq')
- query_grad: float32 [768, 256], replicated
- out_grad: float32 [384, 768], replicated
All inputs are finite; a program needn't handle non-finite values.
Results may differ from a plain program's by a relative error of at most 0.0095.
The roundings to bfloat16 on the way count: a program that leaves them out, or rounds other values in their place, can miss the bound.
Values may be sent and summed in bfloat16 or wider, within the bound.
No kernel may reach another device: no remote copies, remote signals or barrier semaphores. Data moves between devices by JAX's collectives and lax.ppermute only.
A program may use at most 128 MiB of HBM per device.

v0:
```python
import jax
import jax.numpy as jnp
from jax import lax
from jax.sharding import PartitionSpec as P

POOL = 4


norm_eps = 1e-05
head_eps = 1e-06


def padded_2(array, sides, width):
    for axis, dim in sides:
        devices, length = (lax.axis_size(axis), array.shape[dim])
        up = [(i, (i + 1) % devices) for i in range(devices - 1)]
        down = [(j, i) for i, j in up]
        last = lax.slice_in_dim(array, length - width, length, axis=dim)
        leading = lax.slice_in_dim(array, 0, width, axis=dim)
        before = lax.ppermute(last, axis, up)
        after = lax.ppermute(leading, axis, down)
        array = jnp.concatenate([before, array, after], axis=dim)
    return array


def layer_norm(values):
    centre = jnp.mean(values, axis=-1, keepdims=True)
    shifted = values - centre
    variance = jnp.mean(shifted * shifted, axis=-1, keepdims=True)
    return shifted * lax.rsqrt(variance + norm_eps)


def activate(values):
    return values * jax.nn.sigmoid(1.702 * values)


def head_norm(values, group_width):
    grouped = values.reshape(values.shape[0], -1, group_width)
    factor = lax.rsqrt(jnp.mean(grouped * grouped, axis=-1, keepdims=True) + head_eps)
    return (
        (grouped * factor).reshape(values.shape),
        jnp.broadcast_to(factor, grouped.shape).reshape(values.shape),
    )


def contract_first(former, latter):
    return lax.dot_general(
        former, latter, (((0,), (0,)), ((), ())), preferred_element_type=jnp.float32
    )


def contract_last(former, latter):
    return lax.dot_general(
        former, latter, (((1,), (1,)), ((), ())), preferred_element_type=jnp.float32
    )


def stacked_conv(padded, all_taps, length_fine):
    tap_count = all_taps.shape[0]
    windows = jnp.concatenate(
        [padded[tap_index : tap_index + length_fine] for tap_index in range(tap_count)], axis=1
    )
    flat_taps = all_taps.reshape(tap_count * all_taps.shape[1], all_taps.shape[2])
    return jnp.dot(windows, flat_taps, preferred_element_type=jnp.float32)


def on_device(
    binned_signals,
    kernel_coefficients,
    asking_projector,
    lookup_projector,
    content_projector,
    readout_projector,
    logit_multipliers,
    loss_sensitivity,
):
    incoming_tensor = binned_signals[0]
    directional_perturbations = loss_sensitivity[0]
    length_fine = incoming_tensor.shape[0]
    channels = incoming_tensor.shape[1]
    tap_count = kernel_coefficients.shape[0]
    margin = tap_count // 2
    attender_total = logit_multipliers.shape[0]
    probe_extent = asking_projector.shape[1] // attender_total
    value_width = content_projector.shape[1] // attender_total
    activated = activate(layer_norm(incoming_tensor.astype(jnp.float32))).astype(jnp.bfloat16)
    padded = padded_2(activated, (("seq", 0),), margin)
    all_taps = lax.all_gather(kernel_coefficients, "dp", axis=1, tiled=True)
    conv_sum = stacked_conv(padded, all_taps, length_fine)
    summed = incoming_tensor.astype(jnp.float32) + conv_sum
    pooled = jnp.max(summed.reshape(length_fine // POOL, POOL, channels), axis=1).astype(
        jnp.bfloat16
    )
    normed = layer_norm(pooled.astype(jnp.float32)).astype(jnp.bfloat16)
    queries = jnp.dot(normed, asking_projector, preferred_element_type=jnp.float32)
    query_hat, query_factor = head_norm(queries, probe_extent)
    query_unit = query_hat.astype(jnp.bfloat16)
    key_local = head_norm(
        jnp.dot(normed, lookup_projector, preferred_element_type=jnp.float32), probe_extent
    )[0].astype(jnp.bfloat16)
    value_local = jnp.dot(normed, content_projector, preferred_element_type=jnp.float32).astype(
        jnp.bfloat16
    )
    key_unit, values_all = (
        lax.all_gather(key_local, "seq", axis=0, tiled=True),
        lax.all_gather(value_local, "seq", axis=0, tiled=True),
    )
    heads_grad = contract_last(directional_perturbations, readout_projector).astype(jnp.bfloat16)
    outputs = []
    diffs = []
    for attender_slot in range(attender_total):
        key_lo = attender_slot * probe_extent
        value_lo = attender_slot * value_width
        query_part = query_unit[:, key_lo : key_lo + probe_extent]
        key_part = key_unit[:, key_lo : key_lo + probe_extent]
        value_part = values_all[:, value_lo : value_lo + value_width]
        attender_logit_gain = logit_multipliers[attender_slot] / probe_extent
        scores = contract_last(query_part, key_part) * attender_logit_gain
        expo = jnp.exp(scores)
        probs = expo / jnp.sum(expo, axis=1, keepdims=True)
        head_out = jnp.dot(
            probs.astype(jnp.bfloat16), value_part, preferred_element_type=jnp.float32
        )
        outputs.append(head_out)
        grad_part = heads_grad[:, value_lo : value_lo + value_width]
        prob_grad = contract_last(grad_part, value_part)
        delta = jnp.sum(grad_part.astype(jnp.float32) * head_out, axis=1, keepdims=True)
        score_grad = (probs * (prob_grad - delta)).astype(jnp.bfloat16)
        unit_grad = (
            jnp.dot(score_grad, key_part, preferred_element_type=jnp.float32) * attender_logit_gain
        )
        hat_part = query_hat[:, key_lo : key_lo + probe_extent]
        factor_part = query_factor[:, key_lo : key_lo + probe_extent]
        diffs.append(
            factor_part
            * (unit_grad - hat_part * jnp.mean(hat_part * unit_grad, axis=1, keepdims=True))
        )
    heads_low = jnp.concatenate(outputs, axis=1).astype(jnp.bfloat16)
    update = jnp.dot(heads_low, readout_projector, preferred_element_type=jnp.float32)
    query_diff = jnp.concatenate(diffs, axis=1).astype(jnp.bfloat16)
    query_local = contract_first(normed, query_diff)
    out_local = contract_first(heads_low, directional_perturbations)
    query_grad, out_grad = lax.psum((query_local, out_local), ("dp", "seq"))
    return (pooled[None], update[None], query_grad, out_grad)


def solution(mesh):
    return jax.shard_map(
        on_device,
        mesh=mesh,
        in_specs=(
            P("dp", "seq", None),
            P(None, "dp", None),
            P(),
            P(),
            P(),
            P(),
            P(),
            P("dp", "seq", None),
        ),
        out_specs=(P("dp", "seq", None), P("dp", "seq", None), P(), P()),
        check_vma=False,
    )
```

profile of v0, /device:TPU:1, one launch (start us, length us, event | category | flops | bytes accessed | tf_op | source)
XLA Modules:
  0.0 842.4 jit_solution(14659338999122518173)
XLA Ops:
  7.2 0.0 copy-start
  7.2 0.0 copy-start.1
  7.2 0.0 all-gather.4.cloned.1.call-start
  7.2 0.7 all-gather.4.cloned.1.call-update
  7.9 0.0 all-gather.6.cloned.1.call-start
  8.0 1.3 convert_reduce_fusion
  9.3 1.5 fusion.23
  10.8 0.6 fusion.22
  11.4 4.9 collective-permute-start
  16.3 5.1 collective-permute-start.1
  21.5 1.1 fusion.67
  22.6 1.1 fusion.69
  23.7 1.5 constant_dynamic-update-slice_fusion
  25.3 1.1 fusion.65
  26.4 1.2 fusion.68
  27.6 157.3 %all-gather.4.cloned.1.call-done = bf16[5,768,768]{2,1,0:T(8,128)(2,1)} async-done(((bf16[5,48,768]{2,1,0:T(8,128)(2,1)}), bf16[5,768,768]{2,1,0:T(8,128)(2,1)}) %all-gather.4.cloned.1.call-update) | async-done | bytes 5898256 | tf_op jit(solution)/shard_map/all_gather | solution.py:88
  184.9 7.1 fusion.12
  191.9 0.2 reshape.105
  192.2 0.0 copy-start.8
  192.2 1.0 reduce_max.9
  193.2 0.0 copy-start.3
  193.2 0.1 convert_reduce_fusion.1
  193.4 0.2 fusion.72
  193.6 0.3 fusion.113
  193.9 0.1 copy.19
  194.0 0.1 copy.20
  194.1 0.6 multiply_convert_fusion
  194.8 0.0 all-gather.6.cloned.1.call-update
  194.8 0.0 all-gather.8.cloned.1.call-start
  194.9 1.0 convolution_convert_fusion.1
  195.8 0.0 all-gather.8.cloned.1.call-update
  195.8 0.2 all-reduce.3.cloned.1.call-start
  196.1 0.7 fusion.112
  199.3 0.3 convolution_convert_fusion
  199.6 0.3 fusion.114
  199.9 0.1 copy.17
  200.1 0.1 copy.18
  200.2 55.3 %all-gather.6.cloned.1.call-done = bf16[4096,256]{1,0:T(8,128)(2,1)} async-done(((bf16[128,256]{1,0:T(8,128)(2,1)}), bf16[4096,256]{1,0:T(8,128)(2,1)}) %all-gather.6.cloned.1.call-update) | async-done | bytes 2097168 | tf_op jit(solution)/shard_map/all_gather | solution.py:105
  255.5 3.3 fusion.118
  258.8 1.8 fusion.117
  260.6 1.9 fusion.116
  262.6 2.3 fusion.115
  264.9 58.5 %all-gather.8.cloned.1.call-done = bf16[4096,384]{1,0:T(8,128)(2,1)} async-done(((bf16[128,384]{1,0:T(8,128)(2,1)}), bf16[4096,384]{1,0:T(8,128)(2,1)}) %all-gather.8.cloned.1.call-update) | async-done | bytes 3145744 | tf_op jit(solution)/shard_map/all_gather | solution.py:106
  323.4 3.0 fusion.36
  326.4 0.4 copy-done.23
  326.8 1.0 fusion.38
  327.9 0.5 copy-done.5
  328.4 1.0 fusion.40
  329.5 0.5 copy-done.4
  330.0 1.1 multiply_reduce_fusion.7
  331.1 3.7 fusion.31
  334.9 3.9 fusion.30
  338.8 4.1 fusion.29
  342.8 4.0 multiply_reduce_fusion.3
  346.8 0.7 broadcast_multiply_fusion.3
  347.5 0.6 broadcast_multiply_fusion.1
  348.2 1.1 fusion.80
  349.3 1.3 fusion.81
  350.6 1.3 fusion.74
  351.9 0.0 all-reduce.3.cloned.1.call-update
  351.9 1.0 convolution_bitcast_fusion
  353.0 479.7 %all-reduce.3.cloned.1.call-done = (f32[768,256]{1,0:T(8,128)}, f32[384,768]{1,0:T(8,128)}) async-done(((f32[768,256]{1,0:T(8,128)}, f32[384,768]{1,0:T(8,128)}), (f32[768,256]{1,0:T(8,128)}, f32[384,768]{1,0:T(8,128)})) %all-reduce.3.cloned.1.call-update) | async-done | bytes 1966096 | tf_op jit(solution)/shard_map/psum | solution.py:143
  832.7 2.2 copy.41
  834.8 1.0 copy.42
  (59 shorter events, 0.2 us)
Async XLA Ops:
  7.2 192.1 %copy-start = (bf16[384,768]{1,0:T(8,128)(2,1)S(1)}, bf16[384,768]{1,0:T(8,128)(2,1)}, u32[]{:S(2)}) copy-start(bf16[384,768]{1,0:T(8,128)(2,1)} %param.13) | copy-start | bytes 1769476
  7.2 3.6 copy-start.1
  7.2 177.7 %all-gather.4.cloned.1.call-start = ((), (), s32[]{:S(2)}) async-start(), calls=%async_computation | async-start | bytes 6266880 | tf_op jit(solution)/shard_map/all_gather | solution.py:88
  7.9 247.6 %all-gather.6.cloned.1.call-start = ((), (), s32[]{:S(2)}) async-start(), calls=%async_computation.1 | async-start | bytes 2162688 | tf_op jit(solution)/shard_map/all_gather | solution.py:105
  11.4 10.1 %collective-permute-start = (bf16[2,768]{1,0:T(2,128)(2,1)S(1)}, bf16[2,768]{1,0:T(2,128)(2,1)S(1)}, u32[]{:S(2)}, u32[]{:S(2)}) collective-permute-start(bf16[2,768]{1,0:T(2,128)(2,1)S(1)} %get-tuple-element.17), channel_id=1, source_target_pairs={{0,1},{1,2},{2,3},{3,4},{4,5},{5,6},{6,7},{7,8},{8,9},{9,10},{10,1... | collective-permute-start | bytes 9224 | tf_op jit(solution)/shard_map/ppermute | solution.py:20
  16.3 8.9 %collective-permute-start.1 = (bf16[2,768]{1,0:T(2,128)(2,1)S(1)}, bf16[2,768]{1,0:T(2,128)(2,1)S(1)}, u32[]{:S(2)}, u32[]{:S(2)}) collective-permute-start(bf16[2,768]{1,0:T(2,128)(2,1)S(1)} %get-tuple-element.16), channel_id=1, source_target_pairs={{1,0},{2,1},{3,2},{4,3},{5,4},{6,5},{7,6},{8,7},{9,8},{10,9},{11,1... | collective-permute-start | bytes 9224 | tf_op jit(solution)/shard_map/ppermute | solution.py:21
  191.9 1.7 copy-start.9
  192.1 2.7 copy-start.24
  192.1 3.9 copy-start.13
  192.2 7.2 copy-start.8
  193.2 156.1 %copy-start.3 = (bf16[128,768]{1,0:T(8,128)(2,1)}, bf16[128,768]{1,0:T(8,128)(2,1)S(1)}, u32[]{:S(2)}) copy-start(bf16[128,768]{1,0:T(8,128)(2,1)S(1)} %reduce_max.9) | copy-start | bytes 589828
  193.3 6.3 copy-start.10
  193.4 6.5 copy-start.11
  193.6 6.3 copy-start.14
  194.8 128.6 %all-gather.8.cloned.1.call-start = ((), (), s32[]{:S(2)}) async-start(), calls=%async_computation.2 | async-start | bytes 3244032 | tf_op jit(solution)/shard_map/all_gather | solution.py:106
  195.8 636.8 %all-reduce.3.cloned.1.call-start = ((), (), s32[]{:S(2)}) async-start(), calls=%async_computation.3 | async-start | bytes 3932160 | tf_op jit(solution)/shard_map/psum | solution.py:143
  255.5 3.3 copy-start.2
  258.8 64.6 %copy-start.21 = (f32[128]{0:T(128)}, f32[128]{0:T(128)S(1)}, u32[]{:S(2)}) copy-start(f32[128]{0:T(128)S(1)} %get-tuple-element.40) | copy-start | bytes 1540
  260.6 65.8 %copy-start.19 = (f32[128]{0:T(128)}, f32[128]{0:T(128)S(1)}, u32[]{:S(2)}) copy-start(f32[128]{0:T(128)S(1)} %get-tuple-element.38) | copy-start | bytes 1540
  262.6 65.3 %copy-start.17 = (f32[128]{0:T(128)}, f32[128]{0:T(128)S(1)}, u32[]{:S(2)}) copy-start(f32[128]{0:T(128)S(1)} %get-tuple-element.36) | copy-start | bytes 1540
  323.4 3.0 copy-start.6
  323.4 3.5 copy-start.23
  326.8 1.6 copy-start.5
  328.4 1.6 copy-start.4
  328.4 1.6 copy-start.16
  330.0 1.1 copy-start.22
  331.1 3.7 copy-start.20
  334.9 3.9 copy-start.18
  334.9 3.9 copy-start.25
  342.8 6.5 copy-start.12
  342.8 6.5 copy-start.15
  832.7 2.2 copy-start.7
Sparse Core Ops, SparseCore 0:
  11.0 173.7 all-gather.3
  194.9 60.5 all-gather.5
  258.2 65.0 all-gather.7
  352.0 480.5 all-reduce.2
where the time goes:
time: 843 us; the launch traced here: 842 us
  waiting for transfers between devices  751 us (89%)
  matrix products  43.8 us (5%)
  between operations  16.7 us (2%)
  other arithmetic  14 us (2%)
  starting transfers between devices  10.4 us (1%)
    psum x1, waiting for transfers between devices, on_device(): query_grad, out_grad = lax.psum((query_local, out_local), ('dp', 'seq'))  480 us
    all_gather x1, waiting for transfers between devices, on_device(): all_taps = lax.all_gather(kernel_coefficients, 'dp', axis=1, tiled=True)  157 us
    all_gather x1, waiting for transfers between devices, on_device(): lax.all_gather(value_local, 'seq', axis=0, tiled=True)  58.5 us
    all_gather x1, waiting for transfers between devices, on_device(): lax.all_gather(key_local, 'seq', axis=0, tiled=True)  55.3 us
  transfers between devices with their start and end apart: 6, of which 4 were waited for; matrix products, arithmetic and copies ran while one was open for 3% of the time, Pallas kernels for 0%

commit v1 on v0

--- a/solution.py
+++ b/solution.py
@@ -21,6 +21,59 @@
         after = lax.ppermute(leading, axis, down)
         array = jnp.concatenate([before, array, after], axis=dim)
     return array
+
+
+DIMS = {
+    "core": ("seq", 1, 2),
+    "zlo": ("seq", 2, 4),
+    "y": ("seq", 8, 4),
+    "x": ("dp", 1, 4),
+    "zhi": ("dp", 4, 4),
+}
+RS_ORDER = ("core", "x", "y", "zlo", "zhi")
+
+
+def coord(dim):
+    axis, stride, size = DIMS[dim]
+    return (lax.axis_index(axis) // stride) % size
+
+
+def shift(array, dim, step):
+    axis, stride, size = DIMS[dim]
+    pairs = []
+    for index in range(lax.axis_size(axis)):
+        here = (index // stride) % size
+        source = index + ((here + step) % size - here) * stride
+        pairs.append((source, index))
+    return lax.ppermute(array, axis, pairs)
+
+
+def reduce_scatter_dim(chunks, dim):
+    size = DIMS[dim][2]
+    me = coord(dim)
+    total = lax.dynamic_index_in_dim(chunks, me, 0, keepdims=False)
+    for step in range(1, size):
+        part = lax.dynamic_index_in_dim(chunks, (me - step) % size, 0, keepdims=False)
+        total = total + shift(part, dim, step)
+    return total
+
+
+def gather_dim(array, dim, ordered=True):
+    size = DIMS[dim][2]
+    stacked = jnp.stack([array] + [shift(array, dim, step) for step in range(1, size)])
+    if ordered:
+        stacked = jnp.roll(stacked, coord(dim), axis=0)
+    return stacked
+
+
+def all_reduce_flat(flat):
+    sizes = [DIMS[dim][2] for dim in RS_ORDER]
+    chunks = flat.reshape(*sizes, -1)
+    for dim in RS_ORDER:
+        chunks = reduce_scatter_dim(chunks, dim)
+    for dim in reversed(RS_ORDER):
+        chunks = gather_dim(chunks, dim)
+    return chunks.reshape(-1)
 
 
 def layer_norm(values):
@@ -85,8 +138,18 @@
     value_width = content_projector.shape[1] // attender_total
     activated = activate(layer_norm(incoming_tensor.astype(jnp.float32))).astype(jnp.bfloat16)
     padded = padded_2(activated, (("seq", 0),), margin)
-    all_taps = lax.all_gather(kernel_coefficients, "dp", axis=1, tiled=True)
-    conv_sum = stacked_conv(padded, all_taps, length_fine)
+    core = coord("core")
+    half_width = kernel_coefficients.shape[2] // 2
+    own_half = lax.dynamic_slice_in_dim(kernel_coefficients, core * half_width, half_width, axis=2)
+    own_taps = lax.all_gather(own_half, "dp", axis=1, tiled=True)
+    other_taps = shift(own_taps, "core", 1)
+    conv_own = stacked_conv(padded, own_taps, length_fine)
+    conv_other = stacked_conv(padded, other_taps, length_fine)
+    conv_sum = jnp.where(
+        core == 0,
+        jnp.concatenate([conv_own, conv_other], axis=1),
+        jnp.concatenate([conv_other, conv_own], axis=1),
+    )
     summed = incoming_tensor.astype(jnp.float32) + conv_sum
     pooled = jnp.max(summed.reshape(length_fine // POOL, POOL, channels), axis=1).astype(
         jnp.bfloat16
@@ -101,10 +164,12 @@
     value_local = jnp.dot(normed, content_projector, preferred_element_type=jnp.float32).astype(
         jnp.bfloat16
     )
-    key_unit, values_all = (
-        lax.all_gather(key_local, "seq", axis=0, tiled=True),
-        lax.all_gather(value_local, "seq", axis=0, tiled=True),
-    )
+    key_width = key_local.shape[1]
+    joined = jnp.concatenate([key_local, value_local], axis=1)
+    for dim in ("zlo", "y", "core"):
+        joined = gather_dim(joined, dim, ordered=False)
+    joined = joined.reshape(-1, joined.shape[-1])
+    key_unit, values_all = joined[:, :key_width], joined[:, key_width:]
     heads_grad = contract_last(directional_perturbations, readout_projector).astype(jnp.bfloat16)
     outputs = []
     diffs = []
@@ -140,7 +205,9 @@
     query_diff = jnp.concatenate(diffs, axis=1).astype(jnp.bfloat16)
     query_local = contract_first(normed, query_diff)
     out_local = contract_first(heads_low, directional_perturbations)
-    query_grad, out_grad = lax.psum((query_local, out_local), ("dp", "seq"))
+    flat = all_reduce_flat(jnp.concatenate([query_local.reshape(-1), out_local.reshape(-1)]))
+    query_grad = flat[: query_local.size].reshape(query_local.shape)
+    out_grad = flat[query_local.size :].reshape(out_local.shape)
     return (pooled[None], update[None], query_grad, out_grad)
 
 

time: 843 us -> 443 us (0.53)
  waiting for transfers between devices: 751 us -> 199 us
  starting transfers between devices: 10.4 us -> 129 us
  local copies, waits for them, and re-layouts: 6.01 us -> 33.9 us
  other arithmetic: 14 us -> 25.9 us
  matrix products: 43.8 us -> 35.1 us
    psum x1 -> x0, waiting for transfers between devices: 480 us -> none  [on_device(): query_grad, out_grad = lax.psum((query_local, out_local), ('dp', 'seq'))]
    all_gather x3 -> x1, waiting for transfers between devices: 271 us -> 118 us  [on_device(): own_taps = lax.all_gather(own_half, 'dp', axis=1, tiled=True)]
    ppermute x0 -> x34, starting transfers between devices: none -> 124 us  [shift(): return lax.ppermute(array, axis, pairs)]
    ppermute x0 -> x34, waiting for transfers between devices: none -> 81.4 us  [shift(): return lax.ppermute(array, axis, pairs)]
    slice x0 -> x4, local copies, waits for them, and re-layouts: none -> 10.8 us  [the longest x2 5.63 us: on_device(): out_grad = flat[query_local.size:].reshape(out_local.shape)]
  transfers between devices with their start and end apart: 6 -> 37, of which waited for: 4 -> 21; matrix products, arithmetic and copies ran while one was open for 3% -> 7% of each run, Pallas kernels for 0% -> 0%
where the time goes in v1:
time: 443 us; the launch traced here: 441 us
  waiting for transfers between devices  199 us (45%)
  starting transfers between devices  129 us (29%)
  matrix products  35.1 us (8%)
  local copies, waits for them, and re-layouts  33.9 us (8%)
  other arithmetic  25.9 us (6%)
  between operations  18.2 us (4%)
    ppermute x34, starting transfers between devices, shift(): return lax.ppermute(array, axis, pairs)  124 us
    all_gather x1, waiting for transfers between devices, on_device(): own_taps = lax.all_gather(own_half, 'dp', axis=1, tiled=True)  118 us
    ppermute x34, waiting for transfers between devices, shift(): return lax.ppermute(array, axis, pairs)  81.4 us
    dot_general x4, matrix products, on_device(): jnp.dot(score_grad, key_part, preferred_element_type=jnp.float32)  13.8 us
  transfers between devices with their start and end apart: 37, of which 21 were waited for; matrix products, arithmetic and copies ran while one was open for 7% of the time, Pallas kernels for 0%

profile of v1, /device:TPU:1, one launch (start us, length us, event | category | flops | bytes accessed | tf_op | source)
XLA Modules:
  0.0 440.9 jit_solution(8638468826108281491)
XLA Ops:
  9.0 117.8 %all-gather.2.cloned.1.call-done = bf16[5,768,384]{2,1,0:T(8,128)(2,1)} async-done(((bf16[5,48,384]{2,1,0:T(8,128)(2,1)}), bf16[5,768,384]{2,1,0:T(8,128)(2,1)}) %all-gather.2.cloned.1.call-update) | async-done | bytes 2949136 | tf_op jit(solution)/shard_map/all_gather | solution.py:144
  126.8 3.1 collective-permute-start.2
  133.3 1.9 collective-permute-start
  135.3 2.4 collective-permute-start.1
  145.3 7.6 %dot_general.77 = bf16[128,4,3840]{2,1,0:T(4,128)(2,1)} reshape(bf16[512,3840]{1,0:T(8,128)(2,1)} %fusion.65) | data formatting | bytes 7864320 | tf_op jit(solution)/shard_map/dot_general | solution.py:117
  152.9 4.4 %fusion.14 = f32[128,4,384]{2,0,1:T(8,128)S(1)} fusion(bf16[3840,384,1]{1,0,2:T(8,128)(2,1)S(1)} %bitcast.177, bf16[128,4,3840]{2,1,0:T(4,128)(2,1)} %dot_general.77), kind=kOutput, calls=%fused_computation.27 | convolution fusion | flops 1509949440 | bytes 7667712 | tf_op jit(solution)/shard_map/dot_general | solution.py:117
  157.3 4.1 fusion.12
  163.4 6.6 %collective-permute-start.3 = (bf16[128,640]{1,0:T(8,128)(2,1)S(1)}, bf16[128,640]{1,0:T(8,128)(2,1)S(1)}, u32[]{:S(2)}, u32[]{:S(2)}) collective-permute-start(bf16[128,640]{1,0:T(8,128)(2,1)S(1)} %get-tuple-element.37), channel_id=1, source_target_pairs={{2,0},{3,1},{4,2},{5,3},{6,4},{7,5},{0,6},{1,7},{10,8},{11,9},{12,... | collective-permute-start | bytes 491528 | tf_op jit(solution)/shard_map/ppermute | solution.py:48
  171.9 2.2 collective-permute-start.5
  174.1 9.5 %collective-permute-done.4 = bf16[128,640]{1,0:T(8,128)(2,1)S(1)} collective-permute-done((bf16[128,640]{1,0:T(8,128)(2,1)S(1)}, bf16[128,640]{1,0:T(8,128)(2,1)S(1)}, u32[]{:S(2)}, u32[]{:S(2)}) %collective-permute-start.4) | collective-permute-done | bytes 163872 | tf_op jit(solution)/shard_map/ppermute | solution.py:48
  183.7 2.0 collective-permute-start.6
  185.7 5.1 %collective-permute-start.7 = (bf16[4,128,640]{2,1,0:T(8,128)(2,1)S(1)}, bf16[4,128,640]{2,1,0:T(8,128)(2,1)S(1)}, u32[]{:S(2)}, u32[]{:S(2)}) collective-permute-start(bf16[4,128,640]{2,1,0:T(8,128)(2,1)S(1)} %get-tuple-element.28), channel_id=1, source_target_pairs={{16,0},{17,1},{18,2},{19,3},{20,4},{21,5},{22,6},{23,7},{24,8},{25... | collective-permute-start | bytes 1966088 | tf_op jit(solution)/shard_map/ppermute | solution.py:48
  190.9 2.0 collective-permute-start.8
  192.9 8.6 %collective-permute-done.6 = bf16[4,128,640]{2,1,0:T(8,128)(2,1)S(1)} collective-permute-done((bf16[4,128,640]{2,1,0:T(8,128)(2,1)S(1)}, bf16[4,128,640]{2,1,0:T(8,128)(2,1)S(1)}, u32[]{:S(2)}, u32[]{:S(2)}) %collective-permute-start.6) | collective-permute-done | bytes 655392 | tf_op jit(solution)/shard_map/ppermute | solution.py:48
  201.4 2.5 collective-permute-done.7
  203.9 16.2 %collective-permute-done.8 = bf16[4,128,640]{2,1,0:T(8,128)(2,1)S(1)} collective-permute-done((bf16[4,128,640]{2,1,0:T(8,128)(2,1)S(1)}, bf16[4,128,640]{2,1,0:T(8,128)(2,1)S(1)}, u32[]{:S(2)}, u32[]{:S(2)}) %collective-permute-start.8) | collective-permute-done | bytes 655392 | tf_op jit(solution)/shard_map/ppermute | solution.py:48
  221.8 2.6 collective-permute-start.9
  229.4 2.0 fusion.119
  235.7 2.3 pad_maximum_fusion
  245.3 3.7 fusion.26
  249.0 3.6 fusion.27
  252.6 3.4 fusion.28
  256.1 3.0 multiply_reduce_fusion.4
  262.4 2.8 pad_maximum_fusion.2
  265.2 2.8 reshape.154
  271.1 2.9 collective-permute-done.10
  276.6 4.2 collective-permute-start.11
  280.9 2.5 collective-permute-start.12
  283.3 2.4 collective-permute-start.13
  285.8 6.0 %collective-permute-done.11 = f32[4,4,4,960]{3,2,1,0:T(4,128)S(1)} collective-permute-done((f32[4,4,4,960]{3,2,1,0:T(4,128)S(1)}, f32[4,4,4,960]{3,2,1,0:T(4,128)S(1)}, u32[]{:S(2)}, u32[]{:S(2)}) %collective-permute-start.11) | collective-permute-done | bytes 245792 | tf_op jit(solution)/shard_map/ppermute | solution.py:48
  291.8 6.3 %collective-permute-done.13 = f32[4,4,4,960]{3,2,1,0:T(4,128)S(1)} collective-permute-done((f32[4,4,4,960]{3,2,1,0:T(4,128)S(1)}, f32[4,4,4,960]{3,2,1,0:T(4,128)S(1)}, u32[]{:S(2)}, u32[]{:S(2)}) %collective-permute-start.13) | collective-permute-done | bytes 245792 | tf_op jit(solution)/shard_map/ppermute | solution.py:48
  299.2 2.2 collective-permute-start.14
  301.5 4.9 %collective-permute-start.15 = (f32[4,4,960]{2,1,0:T(4,128)S(1)}, f32[4,4,960]{2,1,0:T(4,128)S(1)}, u32[]{:S(2)}, u32[]{:S(2)}) collective-permute-start(f32[4,4,960]{2,1,0:T(4,128)S(1)} %get-tuple-element.31), channel_id=1, source_target_pairs={{16,0},{17,1},{18,2},{19,3},{20,4},{21,5},{22,6},{23,7},{24,8},{25... | collective-permute-start | bytes 184328 | tf_op jit(solution)/shard_map/ppermute | solution.py:48
  306.4 2.4 collective-permute-start.16
  308.9 3.7 collective-permute-done.16
  312.6 3.1 collective-permute-start.17
  315.7 4.5 %collective-permute-start.18 = (f32[4,960]{1,0:T(4,128)S(1)}, f32[4,960]{1,0:T(4,128)S(1)}, u32[]{:S(2)}, u32[]{:S(2)}) collective-permute-start(f32[4,960]{1,0:T(4,128)S(1)} %get-tuple-element.40), channel_id=1, source_target_pairs={{4,0},{5,1},{6,2},{7,3},{0,4},{1,5},{2,6},{3,7},{12,8},{13,9},{14,... | collective-permute-start | bytes 46088 | tf_op jit(solution)/shard_map/ppermute | solution.py:48
  320.3 3.4 collective-permute-start.19
  323.8 2.8 collective-permute-done.19
  326.6 4.4 %collective-permute-start.20 = (f32[960]{0:T(1024)S(1)}, f32[960]{0:T(1024)S(1)}, u32[]{:S(2)}, u32[]{:S(2)}) collective-permute-start(f32[960]{0:T(1024)S(1)} %bitcast.176), channel_id=1, source_target_pairs={{128,0},{160,32},{192,64},{224,96},{256,128},{288,160},{320,192},{... | collective-permute-start | bytes 11528 | tf_op jit(solution)/shard_map/ppermute | solution.py:48
  331.0 7.6 %collective-permute-start.21 = (f32[960]{0:T(1024)S(1)}, f32[960]{0:T(1024)S(1)}, u32[]{:S(2)}, u32[]{:S(2)}) collective-permute-start(f32[960]{0:T(1024)S(1)} %bitcast.175), channel_id=1, source_target_pairs={{256,0},{288,32},{320,64},{352,96},{384,128},{416,160},{448,192},{... | collective-permute-start | bytes 11528 | tf_op jit(solution)/shard_map/ppermute | solution.py:48
  338.6 3.8 collective-permute-start.22
  344.1 3.1 collective-permute-done.22
  347.2 4.2 collective-permute-start.23
  351.3 6.3 %collective-permute-start.24 = (f32[960]{0:T(1024)S(1)}, f32[960]{0:T(1024)S(1)}, u32[]{:S(2)}, u32[]{:S(2)}) collective-permute-start(f32[960]{0:T(1024)S(1)} %add_add_fusion), channel_id=1, source_target_pairs={{256,0},{288,32},{320,64},{352,96},{384,128},{416,160},{448,192},{... | collective-permute-start | bytes 11528 | tf_op jit(solution)/shard_map/ppermute | solution.py:48
  357.7 4.8 %collective-permute-start.25 = (f32[960]{0:T(1024)S(1)}, f32[960]{0:T(1024)S(1)}, u32[]{:S(2)}, u32[]{:S(2)}) collective-permute-start(f32[960]{0:T(1024)S(1)} %add_add_fusion), channel_id=1, source_target_pairs={{384,0},{416,32},{448,64},{480,96},{0,128},{32,160},{64,192},{96,2... | collective-permute-start | bytes 11528 | tf_op jit(solution)/shard_map/ppermute | solution.py:48
  366.0 1.9 collective-permute-start.26
  368.0 2.7 collective-permute-start.27
  370.8 2.5 collective-permute-start.28
  373.4 3.7 collective-permute-done.28
  379.1 3.0 collective-permute-start.30
  382.2 2.6 collective-permute-start.31
  385.7 2.8 collective-permute-done.31
  388.7 1.9 collective-permute-start.32
  390.6 2.4 collective-permute-start.33
  393.1 2.8 collective-permute-start.34
  396.0 3.2 collective-permute-done.33
  399.3 2.8 collective-permute-done.34
  403.4 14.2 %collective-permute-start.35 = (f32[4,4,4,4,960]{4,3,2,1,0:T(4,128)}, f32[4,4,4,4,960]{4,3,2,1,0:T(4,128)}, u32[]{:S(2)}, u32[]{:S(2)}) collective-permute-start(f32[4,4,4,4,960]{4,3,2,1,0:T(4,128)} %constant_dynamic-slice_fusion), channel_id=1, source_target_pairs={{1,0},{0,1},{3,2},{2,3},{5,4},{4,5},{7,6},{6,7},{9,8},{8,9},{11,10... | collective-permute-start | bytes 2949128 | tf_op jit(solution)/shard_map/ppermute | solution.py:48
  420.2 3.0 fusion.18
  423.2 3.3 slice.168
  426.5 3.1 slice.166
  429.6 2.4 slice.201
  432.0 2.1 slice.200
  (173 shorter events, 54.7 us)
Async XLA Ops:
  7.2 220.4 %copy-start = (bf16[384,768]{1,0:T(8,128)(2,1)S(1)}, bf16[384,768]{1,0:T(8,128)(2,1)}, u32[]{:S(2)}) copy-start(bf16[384,768]{1,0:T(8,128)(2,1)} %param.13) | copy-start | bytes 1769476
  7.2 125.5 %copy-start.1 = (bf16[1,512,768]{2,1,0:T(8,128)(2,1)S(1)}, bf16[1,512,768]{2,1,0:T(8,128)(2,1)}, u32[]{:S(2)}) copy-start(bf16[1,512,768]{2,1,0:T(8,128)(2,1)} %param.8) | copy-start | bytes 2359300
  7.2 119.6 %all-gather.2.cloned.1.call-start = ((), (), s32[]{:S(2)}) async-start(), calls=%async_computation | async-start | bytes 3133440 | tf_op jit(solution)/shard_map/all_gather | solution.py:144
  126.8 30.5 %collective-permute-start.2 = (bf16[5,768,384]{2,1,0:T(8,128)(2,1)}, bf16[5,768,384]{2,1,0:T(8,128)(2,1)}, u32[]{:S(2)}, u32[]{:S(2)}) collective-permute-start(bf16[5,768,384]{2,1,0:T(8,128)(2,1)} %all-gather.2.cloned.1.call-done), channel_id=1, source_target_pairs={{1,0},{0,1},{3,2},{2,3},{5,4},{4,5},{7,6},{6,7},{9,8},{8,9},{11,10... | collective-permute-start | bytes 8847368 | tf_op jit(solution)/shard_map/ppermute | solution.py:48
  133.3 5.9 %collective-permute-start = (bf16[2,768]{1,0:T(2,128)(2,1)S(1)}, bf16[2,768]{1,0:T(2,128)(2,1)S(1)}, u32[]{:S(2)}, u32[]{:S(2)}) collective-permute-start(bf16[2,768]{1,0:T(2,128)(2,1)S(1)} %get-tuple-element.26), channel_id=1, source_target_pairs={{0,1},{1,2},{2,3},{3,4},{4,5},{5,6},{6,7},{7,8},{8,9},{9,10},{10,1... | collective-permute-start | bytes 9224 | tf_op jit(solution)/shard_map/ppermute | solution.py:20
  135.3 7.7 %collective-permute-start.1 = (bf16[2,768]{1,0:T(2,128)(2,1)S(1)}, bf16[2,768]{1,0:T(2,128)(2,1)S(1)}, u32[]{:S(2)}, u32[]{:S(2)}) collective-permute-start(bf16[2,768]{1,0:T(2,128)(2,1)S(1)} %get-tuple-element.25), channel_id=1, source_target_pairs={{1,0},{2,1},{3,2},{4,3},{5,4},{6,5},{7,6},{8,7},{9,8},{10,9},{11,1... | collective-permute-start | bytes 9224 | tf_op jit(solution)/shard_map/ppermute | solution.py:21
  145.3 7.6 %copy-start.26 = (bf16[5,768,384]{2,1,0:T(8,128)(2,1)S(1)}, bf16[5,768,384]{2,1,0:T(8,128)(2,1)}, u32[]{:S(2)}) copy-start(bf16[5,768,384]{2,1,0:T(8,128)(2,1)} %all-gather.2.cloned.1.call-done) | copy-start | bytes 8847364
  152.9 4.5 %copy-start.6 = (bf16[128,4,3840]{2,1,0:T(4,128)(2,1)S(1)}, bf16[128,4,3840]{2,1,0:T(4,128)(2,1)}, u32[]{:S(2)}) copy-start(bf16[128,4,3840]{2,1,0:T(4,128)(2,1)} %dot_general.77) | copy-start | bytes 11796484
  157.3 4.2 copy-start.4
  161.5 1.0 copy-start.12
  161.5 1.5 copy-start.27
  162.1 98.3 %copy-start.3 = (bf16[128,768]{1,0:T(8,128)(2,1)}, bf16[128,768]{1,0:T(8,128)(2,1)S(1)}, u32[]{:S(2)}) copy-start(bf16[128,768]{1,0:T(8,128)(2,1)S(1)} %fusion.20) | copy-start | bytes 589828
  163.4 10.7 %collective-permute-start.3 = (bf16[128,640]{1,0:T(8,128)(2,1)S(1)}, bf16[128,640]{1,0:T(8,128)(2,1)S(1)}, u32[]{:S(2)}, u32[]{:S(2)}) collective-permute-start(bf16[128,640]{1,0:T(8,128)(2,1)S(1)} %get-tuple-element.37), channel_id=1, source_target_pairs={{2,0},{3,1},{4,2},{5,3},{6,4},{7,5},{0,6},{1,7},{10,8},{11,9},{12,... | collective-permute-start | bytes 491528 | tf_op jit(solution)/shard_map/ppermute | solution.py:48
  170.0 13.6 %collective-permute-start.4 = (bf16[128,640]{1,0:T(8,128)(2,1)S(1)}, bf16[128,640]{1,0:T(8,128)(2,1)S(1)}, u32[]{:S(2)}, u32[]{:S(2)}) collective-permute-start(bf16[128,640]{1,0:T(8,128)(2,1)S(1)} %get-tuple-element.37), channel_id=1, source_target_pairs={{4,0},{5,1},{6,2},{7,3},{0,4},{1,5},{2,6},{3,7},{12,8},{13,9},{14,... | collective-permute-start | bytes 491528 | tf_op jit(solution)/shard_map/ppermute | solution.py:48
  171.9 11.7 %collective-permute-start.5 = (bf16[128,640]{1,0:T(8,128)(2,1)S(1)}, bf16[128,640]{1,0:T(8,128)(2,1)S(1)}, u32[]{:S(2)}, u32[]{:S(2)}) collective-permute-start(bf16[128,640]{1,0:T(8,128)(2,1)S(1)} %get-tuple-element.37), channel_id=1, source_target_pairs={{6,0},{7,1},{0,2},{1,3},{2,4},{3,5},{4,6},{5,7},{14,8},{15,9},{8,1... | collective-permute-start | bytes 491528 | tf_op jit(solution)/shard_map/ppermute | solution.py:48
  183.7 17.7 %collective-permute-start.6 = (bf16[4,128,640]{2,1,0:T(8,128)(2,1)S(1)}, bf16[4,128,640]{2,1,0:T(8,128)(2,1)S(1)}, u32[]{:S(2)}, u32[]{:S(2)}) collective-permute-start(bf16[4,128,640]{2,1,0:T(8,128)(2,1)S(1)} %get-tuple-element.28), channel_id=1, source_target_pairs={{8,0},{9,1},{10,2},{11,3},{12,4},{13,5},{14,6},{15,7},{16,8},{17,9... | collective-permute-start | bytes 1966088 | tf_op jit(solution)/shard_map/ppermute | solution.py:48
  185.7 18.2 %collective-permute-start.7 = (bf16[4,128,640]{2,1,0:T(8,128)(2,1)S(1)}, bf16[4,128,640]{2,1,0:T(8,128)(2,1)S(1)}, u32[]{:S(2)}, u32[]{:S(2)}) collective-permute-start(bf16[4,128,640]{2,1,0:T(8,128)(2,1)S(1)} %get-tuple-element.28), channel_id=1, source_target_pairs={{16,0},{17,1},{18,2},{19,3},{20,4},{21,5},{22,6},{23,7},{24,8},{25... | collective-permute-start | bytes 1966088 | tf_op jit(solution)/shard_map/ppermute | solution.py:48
  190.9 29.2 %collective-permute-start.8 = (bf16[4,128,640]{2,1,0:T(8,128)(2,1)S(1)}, bf16[4,128,640]{2,1,0:T(8,128)(2,1)S(1)}, u32[]{:S(2)}, u32[]{:S(2)}) collective-permute-start(bf16[4,128,640]{2,1,0:T(8,128)(2,1)S(1)} %get-tuple-element.28), channel_id=1, source_target_pairs={{24,0},{25,1},{26,2},{27,3},{28,4},{29,5},{30,6},{31,7},{0,8},{1,9... | collective-permute-start | bytes 1966088 | tf_op jit(solution)/shard_map/ppermute | solution.py:48
  220.1 4.3 copy-start.25
  221.8 13.9 %collective-permute-start.9 = (bf16[4,4,128,640]{3,2,1,0:T(8,128)(2,1)}, bf16[4,4,128,640]{3,2,1,0:T(8,128)(2,1)}, u32[]{:S(2)}, u32[]{:S(2)}) collective-permute-start(bf16[4,4,128,640]{3,2,1,0:T(8,128)(2,1)} %get-tuple-element.21), channel_id=1, source_target_pairs={{1,0},{0,1},{3,2},{2,3},{5,4},{4,5},{7,6},{6,7},{9,8},{8,9},{11,10... | collective-permute-start | bytes 7864328 | tf_op jit(solution)/shard_map/ppermute | solution.py:48
  238.0 6.1 %copy-start.2 = (bf16[2,4,4,128,640]{4,3,2,1,0:T(8,128)(2,1)}, bf16[2,4,4,128,640]{4,3,2,1,0:T(8,128)(2,1)S(1)}, u32[]{:S(2)}) copy-start(bf16[2,4,4,128,640]{4,3,2,1,0:T(8,128)(2,1)S(1)} %pad_maximum_fusion) | copy-start | bytes 15728644
  239.2 1.7 copy-start.7
  239.7 2.2 copy-start.8
  240.4 2.6 copy-start.9
  243.0 1.1 copy-start.13
  245.3 16.8 %copy-start.14 = (bf16[128,96]{0,1:T(8,128)(2,1)}, bf16[128,96]{0,1:T(8,128)(2,1)S(1)}, u32[]{:S(2)}) copy-start(bf16[128,96]{0,1:T(8,128)(2,1)S(1)} %get-tuple-element.41) | copy-start | bytes 73732
  245.3 16.8 %copy-start.16 = (bf16[128,96]{0,1:T(8,128)(2,1)}, bf16[128,96]{0,1:T(8,128)(2,1)S(1)}, u32[]{:S(2)}) copy-start(bf16[128,96]{0,1:T(8,128)(2,1)S(1)} %get-tuple-element.42) | copy-start | bytes 73732
  249.0 7.0 %copy-start.22 = (f32[128,64]{1,0:T(8,128)}, f32[128,64]{1,0:T(8,128)S(1)}, u32[]{:S(2)}) copy-start(f32[128,64]{1,0:T(8,128)S(1)} %fusion.26) | copy-start | bytes 98308
  252.6 3.5 copy-start.23
  252.6 3.5 copy-start.10
  256.0 3.1 copy-start.24
  259.1 2.9 copy-start.11
  259.1 2.9 copy-start.18
  259.1 2.9 copy-start.20
  269.1 4.9 %collective-permute-start.10 = (f32[4,4,4,4,960]{4,3,2,1,0:T(4,128)}, f32[4,4,4,4,960]{4,3,2,1,0:T(4,128)}, u32[]{:S(2)}, u32[]{:S(2)}) collective-permute-start(f32[4,4,4,4,960]{4,3,2,1,0:T(4,128)} %dynamic-slice_bitcast_fusion), channel_id=1, source_target_pairs={{1,0},{0,1},{3,2},{2,3},{5,4},{4,5},{7,6},{6,7},{9,8},{8,9},{11,10... | collective-permute-start | bytes 2949128 | tf_op jit(solution)/shard_map/ppermute | solution.py:48
  276.6 15.2 %collective-permute-start.11 = (f32[4,4,4,960]{3,2,1,0:T(4,128)S(1)}, f32[4,4,4,960]{3,2,1,0:T(4,128)S(1)}, u32[]{:S(2)}, u32[]{:S(2)}) collective-permute-start(f32[4,4,4,960]{3,2,1,0:T(4,128)S(1)} %get-tuple-element.22), channel_id=1, source_target_pairs={{32,0},{64,32},{96,64},{0,96},{160,128},{192,160},{224,192},{128,2... | collective-permute-start | bytes 737288 | tf_op jit(solution)/shard_map/ppermute | solution.py:48
  280.9 11.0 %collective-permute-start.12 = (f32[4,4,4,960]{3,2,1,0:T(4,128)S(1)}, f32[4,4,4,960]{3,2,1,0:T(4,128)S(1)}, u32[]{:S(2)}, u32[]{:S(2)}) collective-permute-start(f32[4,4,4,960]{3,2,1,0:T(4,128)S(1)} %get-tuple-element.24), channel_id=1, source_target_pairs={{64,0},{96,32},{0,64},{32,96},{192,128},{224,160},{128,192},{160,2... | collective-permute-start | bytes 737288 | tf_op jit(solution)/shard_map/ppermute | solution.py:48
  283.3 14.8 %collective-permute-start.13 = (f32[4,4,4,960]{3,2,1,0:T(4,128)S(1)}, f32[4,4,4,960]{3,2,1,0:T(4,128)S(1)}, u32[]{:S(2)}, u32[]{:S(2)}) collective-permute-start(f32[4,4,4,960]{3,2,1,0:T(4,128)S(1)} %get-tuple-element.23), channel_id=1, source_target_pairs={{96,0},{0,32},{32,64},{64,96},{224,128},{128,160},{160,192},{192,2... | collective-permute-start | bytes 737288 | tf_op jit(solution)/shard_map/ppermute | solution.py:48
  299.2 9.7 %collective-permute-start.14 = (f32[4,4,960]{2,1,0:T(4,128)S(1)}, f32[4,4,960]{2,1,0:T(4,128)S(1)}, u32[]{:S(2)}, u32[]{:S(2)}) collective-permute-start(f32[4,4,960]{2,1,0:T(4,128)S(1)} %get-tuple-element.29), channel_id=1, source_target_pairs={{8,0},{9,1},{10,2},{11,3},{12,4},{13,5},{14,6},{15,7},{16,8},{17,9... | collective-permute-start | bytes 184328 | tf_op jit(solution)/shard_map/ppermute | solution.py:48
  301.5 7.4 %collective-permute-start.15 = (f32[4,4,960]{2,1,0:T(4,128)S(1)}, f32[4,4,960]{2,1,0:T(4,128)S(1)}, u32[]{:S(2)}, u32[]{:S(2)}) collective-permute-start(f32[4,4,960]{2,1,0:T(4,128)S(1)} %get-tuple-element.31), channel_id=1, source_target_pairs={{16,0},{17,1},{18,2},{19,3},{20,4},{21,5},{22,6},{23,7},{24,8},{25... | collective-permute-start | bytes 184328 | tf_op jit(solution)/shard_map/ppermute | solution.py:48
  306.4 6.2 %collective-permute-start.16 = (f32[4,4,960]{2,1,0:T(4,128)S(1)}, f32[4,4,960]{2,1,0:T(4,128)S(1)}, u32[]{:S(2)}, u32[]{:S(2)}) collective-permute-start(f32[4,4,960]{2,1,0:T(4,128)S(1)} %get-tuple-element.30), channel_id=1, source_target_pairs={{24,0},{25,1},{26,2},{27,3},{28,4},{29,5},{30,6},{31,7},{0,8},{1,9... | collective-permute-start | bytes 184328 | tf_op jit(solution)/shard_map/ppermute | solution.py:48
  312.6 11.1 %collective-permute-start.17 = (f32[4,960]{1,0:T(4,128)S(1)}, f32[4,960]{1,0:T(4,128)S(1)}, u32[]{:S(2)}, u32[]{:S(2)}) collective-permute-start(f32[4,960]{1,0:T(4,128)S(1)} %get-tuple-element.38), channel_id=1, source_target_pairs={{2,0},{3,1},{4,2},{5,3},{6,4},{7,5},{0,6},{1,7},{10,8},{11,9},{12,... | collective-permute-start | bytes 46088 | tf_op jit(solution)/shard_map/ppermute | solution.py:48
  315.7 8.0 %collective-permute-start.18 = (f32[4,960]{1,0:T(4,128)S(1)}, f32[4,960]{1,0:T(4,128)S(1)}, u32[]{:S(2)}, u32[]{:S(2)}) collective-permute-start(f32[4,960]{1,0:T(4,128)S(1)} %get-tuple-element.40), channel_id=1, source_target_pairs={{4,0},{5,1},{6,2},{7,3},{0,4},{1,5},{2,6},{3,7},{12,8},{13,9},{14,... | collective-permute-start | bytes 46088 | tf_op jit(solution)/shard_map/ppermute | solution.py:48
  320.3 6.3 %collective-permute-start.19 = (f32[4,960]{1,0:T(4,128)S(1)}, f32[4,960]{1,0:T(4,128)S(1)}, u32[]{:S(2)}, u32[]{:S(2)}) collective-permute-start(f32[4,960]{1,0:T(4,128)S(1)} %get-tuple-element.39), channel_id=1, source_target_pairs={{6,0},{7,1},{0,2},{1,3},{2,4},{3,5},{4,6},{5,7},{14,8},{15,9},{8,1... | collective-permute-start | bytes 46088 | tf_op jit(solution)/shard_map/ppermute | solution.py:48
  326.6 15.9 %collective-permute-start.20 = (f32[960]{0:T(1024)S(1)}, f32[960]{0:T(1024)S(1)}, u32[]{:S(2)}, u32[]{:S(2)}) collective-permute-start(f32[960]{0:T(1024)S(1)} %bitcast.176), channel_id=1, source_target_pairs={{128,0},{160,32},{192,64},{224,96},{256,128},{288,160},{320,192},{... | collective-permute-start | bytes 11528 | tf_op jit(solution)/shard_map/ppermute | solution.py:48
  331.0 13.1 %collective-permute-start.21 = (f32[960]{0:T(1024)S(1)}, f32[960]{0:T(1024)S(1)}, u32[]{:S(2)}, u32[]{:S(2)}) collective-permute-start(f32[960]{0:T(1024)S(1)} %bitcast.175), channel_id=1, source_target_pairs={{256,0},{288,32},{320,64},{352,96},{384,128},{416,160},{448,192},{... | collective-permute-start | bytes 11528 | tf_op jit(solution)/shard_map/ppermute | solution.py:48
  338.6 8.6 %collective-permute-start.22 = (f32[960]{0:T(1024)S(1)}, f32[960]{0:T(1024)S(1)}, u32[]{:S(2)}, u32[]{:S(2)}) collective-permute-start(f32[960]{0:T(1024)S(1)} %bitcast.174), channel_id=1, source_target_pairs={{384,0},{416,32},{448,64},{480,96},{0,128},{32,160},{64,192},{96,2... | collective-permute-start | bytes 11528 | tf_op jit(solution)/shard_map/ppermute | solution.py:48
  347.2 15.3 %collective-permute-start.23 = (f32[960]{0:T(1024)S(1)}, f32[960]{0:T(1024)S(1)}, u32[]{:S(2)}, u32[]{:S(2)}) collective-permute-start(f32[960]{0:T(1024)S(1)} %add_add_fusion), channel_id=1, source_target_pairs={{128,0},{160,32},{192,64},{224,96},{256,128},{288,160},{320,192},{... | collective-permute-start | bytes 11528 | tf_op jit(solution)/shard_map/ppermute | solution.py:48
  351.3 13.1 %collective-permute-start.24 = (f32[960]{0:T(1024)S(1)}, f32[960]{0:T(1024)S(1)}, u32[]{:S(2)}, u32[]{:S(2)}) collective-permute-start(f32[960]{0:T(1024)S(1)} %add_add_fusion), channel_id=1, source_target_pairs={{256,0},{288,32},{320,64},{352,96},{384,128},{416,160},{448,192},{... | collective-permute-start | bytes 11528 | tf_op jit(solution)/shard_map/ppermute | solution.py:48
  357.7 8.3 %collective-permute-start.25 = (f32[960]{0:T(1024)S(1)}, f32[960]{0:T(1024)S(1)}, u32[]{:S(2)}, u32[]{:S(2)}) collective-permute-start(f32[960]{0:T(1024)S(1)} %add_add_fusion), channel_id=1, source_target_pairs={{384,0},{416,32},{448,64},{480,96},{0,128},{32,160},{64,192},{96,2... | collective-permute-start | bytes 11528 | tf_op jit(solution)/shard_map/ppermute | solution.py:48
  366.0 7.3 %collective-permute-start.26 = (f32[4,960]{1,0:T(4,128)S(1)}, f32[4,960]{1,0:T(4,128)S(1)}, u32[]{:S(2)}, u32[]{:S(2)}) collective-permute-start(f32[4,960]{1,0:T(4,128)S(1)} %get-tuple-element.17), channel_id=1, source_target_pairs={{2,0},{3,1},{4,2},{5,3},{6,4},{7,5},{0,6},{1,7},{10,8},{11,9},{12,... | collective-permute-start | bytes 46088 | tf_op jit(solution)/shard_map/ppermute | solution.py:48
  368.0 5.4 %collective-permute-start.27 = (f32[4,960]{1,0:T(4,128)S(1)}, f32[4,960]{1,0:T(4,128)S(1)}, u32[]{:S(2)}, u32[]{:S(2)}) collective-permute-start(f32[4,960]{1,0:T(4,128)S(1)} %get-tuple-element.17), channel_id=1, source_target_pairs={{4,0},{5,1},{6,2},{7,3},{0,4},{1,5},{2,6},{3,7},{12,8},{13,9},{14,... | collective-permute-start | bytes 46088 | tf_op jit(solution)/shard_map/ppermute | solution.py:48
  370.8 6.4 %collective-permute-start.28 = (f32[4,960]{1,0:T(4,128)S(1)}, f32[4,960]{1,0:T(4,128)S(1)}, u32[]{:S(2)}, u32[]{:S(2)}) collective-permute-start(f32[4,960]{1,0:T(4,128)S(1)} %get-tuple-element.17), channel_id=1, source_target_pairs={{6,0},{7,1},{0,2},{1,3},{2,4},{3,5},{4,6},{5,7},{14,8},{15,9},{8,1... | collective-permute-start | bytes 46088 | tf_op jit(solution)/shard_map/ppermute | solution.py:48
  377.2 7.6 %collective-permute-start.29 = (f32[4,4,960]{2,1,0:T(4,128)S(1)}, f32[4,4,960]{2,1,0:T(4,128)S(1)}, u32[]{:S(2)}, u32[]{:S(2)}) collective-permute-start(f32[4,4,960]{2,1,0:T(4,128)S(1)} %get-tuple-element.15), channel_id=1, source_target_pairs={{8,0},{9,1},{10,2},{11,3},{12,4},{13,5},{14,6},{15,7},{16,8},{17,9... | collective-permute-start | bytes 184328 | tf_op jit(solution)/shard_map/ppermute | solution.py:48
  379.1 6.5 %collective-permute-start.30 = (f32[4,4,960]{2,1,0:T(4,128)S(1)}, f32[4,4,960]{2,1,0:T(4,128)S(1)}, u32[]{:S(2)}, u32[]{:S(2)}) collective-permute-start(f32[4,4,960]{2,1,0:T(4,128)S(1)} %get-tuple-element.15), channel_id=1, source_target_pairs={{16,0},{17,1},{18,2},{19,3},{20,4},{21,5},{22,6},{23,7},{24,8},{25... | collective-permute-start | bytes 184328 | tf_op jit(solution)/shard_map/ppermute | solution.py:48
  382.2 6.3 %collective-permute-start.31 = (f32[4,4,960]{2,1,0:T(4,128)S(1)}, f32[4,4,960]{2,1,0:T(4,128)S(1)}, u32[]{:S(2)}, u32[]{:S(2)}) collective-permute-start(f32[4,4,960]{2,1,0:T(4,128)S(1)} %get-tuple-element.15), channel_id=1, source_target_pairs={{24,0},{25,1},{26,2},{27,3},{28,4},{29,5},{30,6},{31,7},{0,8},{1,9... | collective-permute-start | bytes 184328 | tf_op jit(solution)/shard_map/ppermute | solution.py:48
  388.7 7.3 %collective-permute-start.32 = (f32[4,4,4,960]{3,2,1,0:T(4,128)S(1)}, f32[4,4,4,960]{3,2,1,0:T(4,128)S(1)}, u32[]{:S(2)}, u32[]{:S(2)}) collective-permute-start(f32[4,4,4,960]{3,2,1,0:T(4,128)S(1)} %get-tuple-element.13), channel_id=1, source_target_pairs={{32,0},{64,32},{96,64},{0,96},{160,128},{192,160},{224,192},{128,2... | collective-permute-start | bytes 737288 | tf_op jit(solution)/shard_map/ppermute | solution.py:48
  390.6 8.6 %collective-permute-start.33 = (f32[4,4,4,960]{3,2,1,0:T(4,128)S(1)}, f32[4,4,4,960]{3,2,1,0:T(4,128)S(1)}, u32[]{:S(2)}, u32[]{:S(2)}) collective-permute-start(f32[4,4,4,960]{3,2,1,0:T(4,128)S(1)} %get-tuple-element.13), channel_id=1, source_target_pairs={{64,0},{96,32},{0,64},{32,96},{192,128},{224,160},{128,192},{160,2... | collective-permute-start | bytes 737288 | tf_op jit(solution)/shard_map/ppermute | solution.py:48
  393.1 9.0 %collective-permute-start.34 = (f32[4,4,4,960]{3,2,1,0:T(4,128)S(1)}, f32[4,4,4,960]{3,2,1,0:T(4,128)S(1)}, u32[]{:S(2)}, u32[]{:S(2)}) collective-permute-start(f32[4,4,4,960]{3,2,1,0:T(4,128)S(1)} %get-tuple-element.13), channel_id=1, source_target_pairs={{96,0},{0,32},{32,64},{64,96},{224,128},{128,160},{160,192},{192,2... | collective-permute-start | bytes 737288 | tf_op jit(solution)/shard_map/ppermute | solution.py:48
  402.1 15.5 %copy-start.15 = (bf16[128,96]{0,1:T(8,128)(2,1)S(1)}, bf16[128,96]{0,1:T(8,128)(2,1)}, u32[]{:S(2)}) copy-start(bf16[128,96]{0,1:T(8,128)(2,1)} %copy-done.14) | copy-start | bytes 73732
  402.1 15.5 %copy-start.17 = (bf16[128,96]{0,1:T(8,128)(2,1)S(1)}, bf16[128,96]{0,1:T(8,128)(2,1)}, u32[]{:S(2)}) copy-start(bf16[128,96]{0,1:T(8,128)(2,1)} %copy-done.16) | copy-start | bytes 73732
  402.1 15.5 %copy-start.19 = (bf16[128,96]{0,1:T(8,128)(2,1)S(1)}, bf16[128,96]{0,1:T(8,128)(2,1)}, u32[]{:S(2)}) copy-start(bf16[128,96]{0,1:T(8,128)(2,1)} %get-tuple-element.43) | copy-start | bytes 73732
  402.2 15.5 %copy-start.21 = (bf16[128,96]{0,1:T(8,128)(2,1)S(1)}, bf16[128,96]{0,1:T(8,128)(2,1)}, u32[]{:S(2)}) copy-start(bf16[128,96]{0,1:T(8,128)(2,1)} %get-tuple-element.44) | copy-start | bytes 73732
  403.4 16.8 %collective-permute-start.35 = (f32[4,4,4,4,960]{4,3,2,1,0:T(4,128)}, f32[4,4,4,4,960]{4,3,2,1,0:T(4,128)}, u32[]{:S(2)}, u32[]{:S(2)}) collective-permute-start(f32[4,4,4,4,960]{4,3,2,1,0:T(4,128)} %constant_dynamic-slice_fusion), channel_id=1, source_target_pairs={{1,0},{0,1},{3,2},{2,3},{5,4},{4,5},{7,6},{6,7},{9,8},{8,9},{11,10... | collective-permute-start | bytes 2949128 | tf_op jit(solution)/shard_map/ppermute | solution.py:48
  (1 other events, 1.0 us)
Sparse Core Ops, SparseCore 0:
  11.6 115.1 all-gather.1

commit v2 on v1

--- a/solution.py
+++ b/solution.py
@@ -30,7 +30,8 @@
     "x": ("dp", 1, 4),
     "zhi": ("dp", 4, 4),
 }
-RS_ORDER = ("core", "x", "y", "zlo", "zhi")
+RS_ORDER = ("core", "x", "y")
+SUM_ORDER = ("zlo", "zhi")
 
 
 def coord(dim):
@@ -66,11 +67,29 @@
     return stacked
 
 
+def swap_y_pair(array):
+    axis, stride, _ = DIMS["y"]
+    pairs = []
+    for index in range(lax.axis_size(axis)):
+        here = (index // stride) % 4
+        pairs.append((index + ((here ^ 1) - here) * stride, index))
+    return lax.ppermute(array, axis, pairs)
+
+
+def sum_in_order(stacked):
+    total = stacked[0]
+    for index in range(1, stacked.shape[0]):
+        total = total + stacked[index]
+    return total
+
+
 def all_reduce_flat(flat):
     sizes = [DIMS[dim][2] for dim in RS_ORDER]
     chunks = flat.reshape(*sizes, -1)
     for dim in RS_ORDER:
         chunks = reduce_scatter_dim(chunks, dim)
+    for dim in SUM_ORDER:
+        chunks = sum_in_order(gather_dim(chunks, dim))
     for dim in reversed(RS_ORDER):
         chunks = gather_dim(chunks, dim)
     return chunks.reshape(-1)
@@ -139,16 +158,33 @@
     activated = activate(layer_norm(incoming_tensor.astype(jnp.float32))).astype(jnp.bfloat16)
     padded = padded_2(activated, (("seq", 0),), margin)
     core = coord("core")
-    half_width = kernel_coefficients.shape[2] // 2
-    own_half = lax.dynamic_slice_in_dim(kernel_coefficients, core * half_width, half_width, axis=2)
-    own_taps = lax.all_gather(own_half, "dp", axis=1, tiled=True)
-    other_taps = shift(own_taps, "core", 1)
-    conv_own = stacked_conv(padded, own_taps, length_fine)
-    conv_other = stacked_conv(padded, other_taps, length_fine)
+    low_bit = coord("y") % 2
+    quarter = kernel_coefficients.shape[2] // 4
+    own_part = lax.dynamic_slice_in_dim(
+        kernel_coefficients, (2 * core + low_bit) * quarter, quarter, axis=2
+    )
+    own_taps = lax.all_gather(own_part, "dp", axis=1, tiled=True)
+    pair_taps = swap_y_pair(own_taps)
+    near_taps = jnp.concatenate([own_taps, pair_taps], axis=2)
+    far_taps = jnp.concatenate(
+        [shift(own_taps, "core", 1), shift(pair_taps, "core", 1)], axis=2
+    )
+    conv_near = stacked_conv(padded, near_taps, length_fine)
+    conv_far = stacked_conv(padded, far_taps, length_fine)
+
+    def in_order(pieces_conv):
+        first, second = pieces_conv[:, :quarter], pieces_conv[:, quarter:]
+        return jnp.where(
+            low_bit == 0,
+            jnp.concatenate([first, second], axis=1),
+            jnp.concatenate([second, first], axis=1),
+        )
+
+    conv_near, conv_far = in_order(conv_near), in_order(conv_far)
     conv_sum = jnp.where(
         core == 0,
-        jnp.concatenate([conv_own, conv_other], axis=1),
-        jnp.concatenate([conv_other, conv_own], axis=1),
+        jnp.concatenate([conv_near, conv_far], axis=1),
+        jnp.concatenate([conv_far, conv_near], axis=1),
     )
     summed = incoming_tensor.astype(jnp.float32) + conv_sum
     pooled = jnp.max(summed.reshape(length_fine // POOL, POOL, channels), axis=1).astype(

time: 443 us -> 438 us (0.989)
  starting transfers between devices: 129 us -> 97 us
  local copies, waits for them, and re-layouts: 33.9 us -> 44.1 us
  other arithmetic: 25.9 us -> 33.9 us
  waiting for transfers between devices: 199 us -> 204 us
    ppermute x34 -> x29, starting transfers between devices: 124 us -> 90 us  [shift(): return lax.ppermute(array, axis, pairs)]
    ppermute x0 -> x1, waiting for transfers between devices: none -> 20.7 us  [swap_y_pair(): return lax.ppermute(array, axis, pairs)]
    all_gather x1, waiting for transfers between devices: 118 us -> 100 us  [on_device(): own_taps = lax.all_gather(own_part, 'dp', axis=1, tiled=True)]
    ppermute x0 -> x3, local copies, waits for them, and re-layouts: none -> 11.5 us  [the longest x2 7.76 us: shift(): return lax.ppermute(array, axis, pairs)]
    dot_general x1 -> x0, local copies, waits for them, and re-layouts: 7.59 us -> none  [stacked_conv(): return jnp.dot(windows, flat_taps, preferred_element_type=jnp.float32)]
    concatenate x0 -> x2, other arithmetic: none -> 5.19 us  [the longest x1 2.6 us: on_device(): near_taps = jnp.concatenate([own_taps, pair_taps], axis=2)]
    concatenate x0 -> x2, local copies, waits for them, and re-layouts: none -> 4.66 us  [on_device(): jnp.concatenate([conv_near, conv_far], axis=1)]
    ppermute x34 -> x29, waiting for transfers between devices: 81.4 us -> 83.4 us  [shift(): return lax.ppermute(array, axis, pairs)]
  transfers between devices with their start and end apart: 37 -> 33, of which waited for: 21 -> 21; matrix products, arithmetic and copies ran while one was open for 7% -> 8% of each run, Pallas kernels for 0% -> 0%
where the time goes in v2:
time: 438 us; the launch traced here: 434 us
  waiting for transfers between devices  204 us (47%)
  starting transfers between devices  97 us (22%)
  local copies, waits for them, and re-layouts  44.1 us (10%)
  matrix products  36.1 us (8%)
  other arithmetic  33.9 us (8%)
  between operations  18.3 us (4%)
    all_gather x1, waiting for transfers between devices, on_device(): own_taps = lax.all_gather(own_part, 'dp', axis=1, tiled=True)  100 us
    ppermute x29, starting transfers between devices, shift(): return lax.ppermute(array, axis, pairs)  90 us
    ppermute x29, waiting for transfers between devices, shift(): return lax.ppermute(array, axis, pairs)  83.4 us
    ppermute x1, waiting for transfers between devices, swap_y_pair(): return lax.ppermute(array, axis, pairs)  20.7 us
    dot_general x4, matrix products, on_device(): jnp.dot(score_grad, key_part, preferred_element_type=jnp.float32)  13.7 us
  transfers between devices with their start and end apart: 33, of which 21 were waited for; matrix products, arithmetic and copies ran while one was open for 8% of the time, Pallas kernels for 0%

profile of v2, /device:TPU:1, one launch (start us, length us, event | category | flops | bytes accessed | tf_op | source)
XLA Modules:
  0.0 433.7 jit_solution(1971660256799998697)
XLA Ops:
  9.1 100.0 %all-gather.2.cloned.1.call-done = bf16[5,768,192]{2,1,0:T(8,128)(2,1)} async-done(((bf16[5,48,192]{2,1,0:T(8,128)(2,1)}), bf16[5,768,192]{2,1,0:T(8,128)(2,1)}) %all-gather.2.cloned.1.call-update) | async-done | bytes 1474576 | tf_op jit(solution)/shard_map/all_gather | solution.py:166
  109.2 3.8 copy.49
  113.0 2.7 collective-permute-start.2
  116.2 2.8 collective-permute-start.3
  121.6 2.4 collective-permute-start.1
  127.8 20.7 %collective-permute-done.2 = bf16[5,768,192]{1,2,0:T(8,128)(2,1)} collective-permute-done((bf16[5,768,192]{1,2,0:T(8,128)(2,1)}, bf16[5,768,192]{1,2,0:T(8,128)(2,1)}, u32[]{:S(2)}, u32[]{:S(2)}) %collective-permute-start.2) | collective-permute-done | bytes 1474592 | tf_op jit(solution)/shard_map/ppermute | solution.py:76
  148.5 3.6 collective-permute-start.4
  156.0 3.8 copy.50
  159.7 3.9 copy.53
  163.6 2.6 pad_maximum_fusion.1
  166.2 3.9 fusion.144
  171.0 3.9 copy.54
  174.9 2.6 pad_maximum_fusion.2
  177.5 3.9 fusion.145
  183.9 2.4 concatenate.79
  187.4 2.3 concatenate.82
  189.8 2.9 fusion.16
  198.8 5.2 %collective-permute-start.5 = (bf16[128,640]{1,0:T(8,128)(2,1)S(1)}, bf16[128,640]{1,0:T(8,128)(2,1)S(1)}, u32[]{:S(2)}, u32[]{:S(2)}) collective-permute-start(bf16[128,640]{1,0:T(8,128)(2,1)S(1)} %get-tuple-element.39), channel_id=1, source_target_pairs={{2,0},{3,1},{4,2},{5,3},{6,4},{7,5},{0,6},{1,7},{10,8},{11,9},{12,... | collective-permute-start | bytes 491528 | tf_op jit(solution)/shard_map/ppermute | solution.py:49
  204.0 4.2 collective-permute-done.6
  208.2 3.4 collective-permute-done.5
  211.7 4.0 collective-permute-start.8
  215.8 2.4 collective-permute-start.9
  218.2 2.6 collective-permute-start.10
  220.8 9.0 %collective-permute-done.8 = bf16[4,128,640]{2,1,0:T(8,128)(2,1)S(1)} collective-permute-done((bf16[4,128,640]{2,1,0:T(8,128)(2,1)S(1)}, bf16[4,128,640]{2,1,0:T(8,128)(2,1)S(1)}, u32[]{:S(2)}, u32[]{:S(2)}) %collective-permute-start.8) | collective-permute-done | bytes 655392 | tf_op jit(solution)/shard_map/ppermute | solution.py:49
  229.8 5.0 %collective-permute-done.9 = bf16[4,128,640]{2,1,0:T(8,128)(2,1)S(1)} collective-permute-done((bf16[4,128,640]{2,1,0:T(8,128)(2,1)S(1)}, bf16[4,128,640]{2,1,0:T(8,128)(2,1)S(1)}, u32[]{:S(2)}, u32[]{:S(2)}) %collective-permute-start.9) | collective-permute-done | bytes 655392 | tf_op jit(solution)/shard_map/ppermute | solution.py:49
  234.8 15.1 %collective-permute-done.10 = bf16[4,128,640]{2,1,0:T(8,128)(2,1)S(1)} collective-permute-done((bf16[4,128,640]{2,1,0:T(8,128)(2,1)S(1)}, bf16[4,128,640]{2,1,0:T(8,128)(2,1)S(1)}, u32[]{:S(2)}, u32[]{:S(2)}) %collective-permute-start.10) | collective-permute-done | bytes 655392 | tf_op jit(solution)/shard_map/ppermute | solution.py:49
  251.6 2.9 collective-permute-start.11
  266.0 2.3 pad_maximum_fusion
  275.6 3.7 fusion.22
  279.3 3.5 fusion.23
  282.9 3.4 fusion.24
  286.4 3.0 multiply_reduce_fusion.4
  292.7 2.7 pad_maximum_fusion.4
  295.5 2.2 reshape.158
  299.7 2.6 collective-permute-done.12
  303.9 4.3 collective-permute-start.13
  308.2 2.5 collective-permute-start.14
  310.7 2.5 collective-permute-start.15
  313.2 5.2 %collective-permute-done.13 = f32[4,15360]{1,0:T(4,128)S(1)} collective-permute-done((f32[4,15360]{1,0:T(4,128)S(1)}, f32[4,15360]{1,0:T(4,128)S(1)}, u32[]{:S(2)}, u32[]{:S(2)}) %collective-permute-start.13) | collective-permute-done | bytes 245792 | tf_op jit(solution)/shard_map/ppermute | solution.py:49
  318.7 6.0 %collective-permute-done.15 = f32[4,15360]{1,0:T(4,128)S(1)} collective-permute-done((f32[4,15360]{1,0:T(4,128)S(1)}, f32[4,15360]{1,0:T(4,128)S(1)}, u32[]{:S(2)}, u32[]{:S(2)}) %collective-permute-start.15) | collective-permute-done | bytes 245792 | tf_op jit(solution)/shard_map/ppermute | solution.py:49
  325.1 2.2 collective-permute-start.16
  327.3 2.4 collective-permute-start.17
  329.7 2.5 collective-permute-start.18
  333.8 2.5 collective-permute-done.18
  336.3 2.5 collective-permute-start.19
  338.8 2.9 collective-permute-start.20
  341.7 2.9 collective-permute-start.21
  344.7 3.9 collective-permute-done.21
  350.2 4.3 collective-permute-start.22
  354.5 6.5 %collective-permute-start.23 = (f32[15360]{0:T(1024)S(1)}, f32[15360]{0:T(1024)S(1)}, u32[]{:S(2)}, u32[]{:S(2)}) collective-permute-start(f32[15360]{0:T(1024)S(1)} %bitcast.124), channel_id=1, source_target_pairs={{256,0},{288,32},{320,64},{352,96},{384,128},{416,160},{448,192},{... | collective-permute-start | bytes 184328 | tf_op jit(solution)/shard_map/ppermute | solution.py:49
  361.0 4.6 %collective-permute-start.24 = (f32[15360]{0:T(1024)S(1)}, f32[15360]{0:T(1024)S(1)}, u32[]{:S(2)}, u32[]{:S(2)}) collective-permute-start(f32[15360]{0:T(1024)S(1)} %bitcast.125), channel_id=1, source_target_pairs={{384,0},{416,32},{448,64},{480,96},{0,128},{32,160},{64,192},{96,2... | collective-permute-start | bytes 184328 | tf_op jit(solution)/shard_map/ppermute | solution.py:49
  365.7 2.6 collective-permute-done.23
  368.3 7.2 %collective-permute-done.24 = f32[15360]{0:T(1024)S(1)} collective-permute-done((f32[15360]{0:T(1024)S(1)}, f32[15360]{0:T(1024)S(1)}, u32[]{:S(2)}, u32[]{:S(2)}) %collective-permute-start.24) | collective-permute-done | bytes 61472 | tf_op jit(solution)/shard_map/ppermute | solution.py:49
  379.0 3.1 collective-permute-start.26
  382.1 2.2 collective-permute-start.27
  385.5 2.8 collective-permute-done.27
  393.4 4.8 %collective-permute-start.29 = (f32[4,15360]{1,0:T(4,128)S(1)}, f32[4,15360]{1,0:T(4,128)S(1)}, u32[]{:S(2)}, u32[]{:S(2)}) collective-permute-start(f32[4,15360]{1,0:T(4,128)S(1)} %get-tuple-element.14), channel_id=1, source_target_pairs={{64,0},{96,32},{0,64},{32,96},{192,128},{224,160},{128,192},{160,2... | collective-permute-start | bytes 737288 | tf_op jit(solution)/shard_map/ppermute | solution.py:49
  398.1 2.8 collective-permute-start.30
  401.8 8.3 %collective-permute-done.30 = f32[4,15360]{1,0:T(4,128)S(1)} collective-permute-done((f32[4,15360]{1,0:T(4,128)S(1)}, f32[4,15360]{1,0:T(4,128)S(1)}, u32[]{:S(2)}, u32[]{:S(2)}) %collective-permute-start.30) | collective-permute-done | bytes 245792 | tf_op jit(solution)/shard_map/ppermute | solution.py:49
  410.4 4.0 collective-permute-start.31
  417.6 2.3 slice.218
  419.9 2.3 slice.216
  422.2 2.4 slice.263
  424.6 2.1 slice.262
  (158 shorter events, 65.6 us)
Async XLA Ops:
  7.2 250.7 %copy-start = (bf16[384,768]{1,0:T(8,128)(2,1)S(1)}, bf16[384,768]{1,0:T(8,128)(2,1)}, u32[]{:S(2)}) copy-start(bf16[384,768]{1,0:T(8,128)(2,1)} %param.15) | copy-start | bytes 1769476
  7.2 108.5 %copy-start.1 = (bf16[1,512,768]{2,1,0:T(8,128)(2,1)S(1)}, bf16[1,512,768]{2,1,0:T(8,128)(2,1)}, u32[]{:S(2)}) copy-start(bf16[1,512,768]{2,1,0:T(8,128)(2,1)} %param.10) | copy-start | bytes 2359300
  7.2 102.0 %all-gather.2.cloned.1.call-start = ((), (), s32[]{:S(2)}) async-start(), calls=%async_computation | async-start | bytes 2088960 | tf_op jit(solution)/shard_map/all_gather | solution.py:166
  113.0 35.5 %collective-permute-start.2 = (bf16[5,768,192]{1,2,0:T(8,128)(2,1)}, bf16[5,768,192]{1,2,0:T(8,128)(2,1)}, u32[]{:S(2)}, u32[]{:S(2)}) collective-permute-start(bf16[5,768,192]{1,2,0:T(8,128)(2,1)} %copy.49), channel_id=1, source_target_pairs={{8,0},{9,1},{10,2},{11,3},{12,4},{13,5},{14,6},{15,7},{0,8},{1,9},... | collective-permute-start | bytes 4423688 | tf_op jit(solution)/shard_map/ppermute | solution.py:76
  116.2 43.5 %collective-permute-start.3 = (bf16[5,768,192]{1,2,0:T(8,128)(2,1)}, bf16[5,768,192]{1,2,0:T(8,128)(2,1)}, u32[]{:S(2)}, u32[]{:S(2)}) collective-permute-start(bf16[5,768,192]{1,2,0:T(8,128)(2,1)} %copy.49), channel_id=1, source_target_pairs={{1,0},{0,1},{3,2},{2,3},{5,4},{4,5},{7,6},{6,7},{9,8},{8,9},{11,10... | collective-permute-start | bytes 4423688 | tf_op jit(solution)/shard_map/ppermute | solution.py:49
  119.6 5.9 %collective-permute-start = (bf16[2,768]{1,0:T(2,128)(2,1)S(1)}, bf16[2,768]{1,0:T(2,128)(2,1)S(1)}, u32[]{:S(2)}, u32[]{:S(2)}) collective-permute-start(bf16[2,768]{1,0:T(2,128)(2,1)S(1)} %get-tuple-element.27), channel_id=1, source_target_pairs={{0,1},{1,2},{2,3},{3,4},{4,5},{5,6},{6,7},{7,8},{8,9},{9,10},{10,1... | collective-permute-start | bytes 9224 | tf_op jit(solution)/shard_map/ppermute | solution.py:20
  121.6 32.0 %collective-permute-start.1 = (bf16[2,768]{1,0:T(2,128)(2,1)S(1)}, bf16[2,768]{1,0:T(2,128)(2,1)S(1)}, u32[]{:S(2)}, u32[]{:S(2)}) collective-permute-start(bf16[2,768]{1,0:T(2,128)(2,1)S(1)} %get-tuple-element.26), channel_id=1, source_target_pairs={{1,0},{2,1},{3,2},{4,3},{5,4},{6,5},{7,6},{8,7},{9,8},{10,9},{11,1... | collective-permute-start | bytes 9224 | tf_op jit(solution)/shard_map/ppermute | solution.py:21
  148.5 22.5 %collective-permute-start.4 = (bf16[5,768,192]{1,2,0:T(8,128)(2,1)}, bf16[5,768,192]{1,2,0:T(8,128)(2,1)}, u32[]{:S(2)}, u32[]{:S(2)}) collective-permute-start(bf16[5,768,192]{1,2,0:T(8,128)(2,1)} %collective-permute-done.2), channel_id=1, source_target_pairs={{1,0},{0,1},{3,2},{2,3},{5,4},{4,5},{7,6},{6,7},{9,8},{8,9},{11,10... | collective-permute-start | bytes 4423688 | tf_op jit(solution)/shard_map/ppermute | solution.py:49
  159.7 3.9 copy-start.3
  171.0 3.9 copy-start.4
  177.5 4.0 copy-start.12
  177.5 4.0 copy-start.13
  182.8 3.5 copy-start.7
  183.9 5.8 %copy-start.6 = (f32[128,4,768]{2,1,0:T(4,128)S(1)}, f32[128,4,768]{2,1,0:T(4,128)}, u32[]{:S(2)}) copy-start(f32[128,4,768]{2,1,0:T(4,128)} %reshape.159) | copy-start | bytes 4718596
  187.4 2.3 copy-start.8
  189.8 3.2 copy-start.16
  192.6 98.0 %copy-start.5 = (bf16[128,768]{1,0:T(8,128)(2,1)}, bf16[128,768]{1,0:T(8,128)(2,1)S(1)}, u32[]{:S(2)}) copy-start(bf16[128,768]{1,0:T(8,128)(2,1)S(1)} %fusion.16) | copy-start | bytes 589828
  194.9 13.2 %collective-permute-start.6 = (bf16[128,640]{1,0:T(8,128)(2,1)S(1)}, bf16[128,640]{1,0:T(8,128)(2,1)S(1)}, u32[]{:S(2)}, u32[]{:S(2)}) collective-permute-start(bf16[128,640]{1,0:T(8,128)(2,1)S(1)} %get-tuple-element.39), channel_id=1, source_target_pairs={{4,0},{5,1},{6,2},{7,3},{0,4},{1,5},{2,6},{3,7},{12,8},{13,9},{14,... | collective-permute-start | bytes 491528 | tf_op jit(solution)/shard_map/ppermute | solution.py:49
  196.9 11.3 %collective-permute-start.7 = (bf16[128,640]{1,0:T(8,128)(2,1)S(1)}, bf16[128,640]{1,0:T(8,128)(2,1)S(1)}, u32[]{:S(2)}, u32[]{:S(2)}) collective-permute-start(bf16[128,640]{1,0:T(8,128)(2,1)S(1)} %get-tuple-element.39), channel_id=1, source_target_pairs={{6,0},{7,1},{0,2},{1,3},{2,4},{3,5},{4,6},{5,7},{14,8},{15,9},{8,1... | collective-permute-start | bytes 491528 | tf_op jit(solution)/shard_map/ppermute | solution.py:49
  198.8 12.8 %collective-permute-start.5 = (bf16[128,640]{1,0:T(8,128)(2,1)S(1)}, bf16[128,640]{1,0:T(8,128)(2,1)S(1)}, u32[]{:S(2)}, u32[]{:S(2)}) collective-permute-start(bf16[128,640]{1,0:T(8,128)(2,1)S(1)} %get-tuple-element.39), channel_id=1, source_target_pairs={{2,0},{3,1},{4,2},{5,3},{6,4},{7,5},{0,6},{1,7},{10,8},{11,9},{12,... | collective-permute-start | bytes 491528 | tf_op jit(solution)/shard_map/ppermute | solution.py:49
  211.7 18.0 %collective-permute-start.8 = (bf16[4,128,640]{2,1,0:T(8,128)(2,1)S(1)}, bf16[4,128,640]{2,1,0:T(8,128)(2,1)S(1)}, u32[]{:S(2)}, u32[]{:S(2)}) collective-permute-start(bf16[4,128,640]{2,1,0:T(8,128)(2,1)S(1)} %get-tuple-element.29), channel_id=1, source_target_pairs={{8,0},{9,1},{10,2},{11,3},{12,4},{13,5},{14,6},{15,7},{16,8},{17,9... | collective-permute-start | bytes 1966088 | tf_op jit(solution)/shard_map/ppermute | solution.py:49
  215.8 19.0 %collective-permute-start.9 = (bf16[4,128,640]{2,1,0:T(8,128)(2,1)S(1)}, bf16[4,128,640]{2,1,0:T(8,128)(2,1)S(1)}, u32[]{:S(2)}, u32[]{:S(2)}) collective-permute-start(bf16[4,128,640]{2,1,0:T(8,128)(2,1)S(1)} %get-tuple-element.29), channel_id=1, source_target_pairs={{16,0},{17,1},{18,2},{19,3},{20,4},{21,5},{22,6},{23,7},{24,8},{25... | collective-permute-start | bytes 1966088 | tf_op jit(solution)/shard_map/ppermute | solution.py:49
  218.2 31.7 %collective-permute-start.10 = (bf16[4,128,640]{2,1,0:T(8,128)(2,1)S(1)}, bf16[4,128,640]{2,1,0:T(8,128)(2,1)S(1)}, u32[]{:S(2)}, u32[]{:S(2)}) collective-permute-start(bf16[4,128,640]{2,1,0:T(8,128)(2,1)S(1)} %get-tuple-element.29), channel_id=1, source_target_pairs={{24,0},{25,1},{26,2},{27,3},{28,4},{29,5},{30,6},{31,7},{0,8},{1,9... | collective-permute-start | bytes 1966088 | tf_op jit(solution)/shard_map/ppermute | solution.py:49
  249.9 4.7 %copy-start.25 = (f32[4]{0:T(128)S(1)}, f32[4]{0:T(128)}, u32[]{:S(2)}) copy-start(f32[4]{0:T(128)} %param.16) | copy-start | bytes 52
  251.6 14.4 %collective-permute-start.11 = (bf16[4,4,128,640]{3,2,1,0:T(8,128)(2,1)}, bf16[4,4,128,640]{3,2,1,0:T(8,128)(2,1)}, u32[]{:S(2)}, u32[]{:S(2)}) collective-permute-start(bf16[4,4,128,640]{3,2,1,0:T(8,128)(2,1)} %get-tuple-element.18), channel_id=1, source_target_pairs={{1,0},{0,1},{3,2},{2,3},{5,4},{4,5},{7,6},{6,7},{9,8},{8,9},{11,10... | collective-permute-start | bytes 7864328 | tf_op jit(solution)/shard_map/ppermute | solution.py:49
  268.3 6.1 %copy-start.2 = (bf16[2,4,4,128,640]{4,3,2,1,0:T(8,128)(2,1)}, bf16[2,4,4,128,640]{4,3,2,1,0:T(8,128)(2,1)S(1)}, u32[]{:S(2)}) copy-start(bf16[2,4,4,128,640]{4,3,2,1,0:T(8,128)(2,1)S(1)} %pad_maximum_fusion) | copy-start | bytes 15728644
  269.5 1.7 copy-start.9
  270.1 2.2 copy-start.10
  270.7 2.6 copy-start.11
  273.3 1.1 copy-start.17
  275.6 16.8 %copy-start.18 = (bf16[128,96]{0,1:T(8,128)(2,1)}, bf16[128,96]{0,1:T(8,128)(2,1)S(1)}, u32[]{:S(2)}) copy-start(bf16[128,96]{0,1:T(8,128)(2,1)S(1)} %get-tuple-element.40) | copy-start | bytes 73732
  275.6 16.8 %copy-start.19 = (bf16[128,96]{0,1:T(8,128)(2,1)}, bf16[128,96]{0,1:T(8,128)(2,1)S(1)}, u32[]{:S(2)}) copy-start(bf16[128,96]{0,1:T(8,128)(2,1)S(1)} %get-tuple-element.41) | copy-start | bytes 73732
  279.3 7.0 %copy-start.22 = (f32[128,64]{1,0:T(8,128)}, f32[128,64]{1,0:T(8,128)S(1)}, u32[]{:S(2)}) copy-start(f32[128,64]{1,0:T(8,128)S(1)} %fusion.22) | copy-start | bytes 98308
  282.9 3.5 copy-start.23
  282.9 3.5 copy-start.14
  286.3 3.1 copy-start.24
  289.4 2.9 copy-start.15
  289.4 2.9 copy-start.20
  289.4 2.9 copy-start.21
  297.7 4.6 %collective-permute-start.12 = (f32[4,4,15360]{2,1,0:T(4,128)S(1)}, f32[4,4,15360]{2,1,0:T(4,128)}, u32[]{:S(2)}, u32[]{:S(2)}) collective-permute-start(f32[4,4,15360]{2,1,0:T(4,128)S(1)} %dynamic-slice_bitcast_fusion), channel_id=1, source_target_pairs={{1,0},{0,1},{3,2},{2,3},{5,4},{4,5},{7,6},{6,7},{9,8},{8,9},{11,10... | collective-permute-start | bytes 2949128 | tf_op jit(solution)/shard_map/ppermute | solution.py:49
  303.9 14.6 %collective-permute-start.13 = (f32[4,15360]{1,0:T(4,128)S(1)}, f32[4,15360]{1,0:T(4,128)S(1)}, u32[]{:S(2)}, u32[]{:S(2)}) collective-permute-start(f32[4,15360]{1,0:T(4,128)S(1)} %get-tuple-element.19), channel_id=1, source_target_pairs={{32,0},{64,32},{96,64},{0,96},{160,128},{192,160},{224,192},{128,2... | collective-permute-start | bytes 737288 | tf_op jit(solution)/shard_map/ppermute | solution.py:49
  308.2 10.5 %collective-permute-start.14 = (f32[4,15360]{1,0:T(4,128)S(1)}, f32[4,15360]{1,0:T(4,128)S(1)}, u32[]{:S(2)}, u32[]{:S(2)}) collective-permute-start(f32[4,15360]{1,0:T(4,128)S(1)} %get-tuple-element.21), channel_id=1, source_target_pairs={{64,0},{96,32},{0,64},{32,96},{192,128},{224,160},{128,192},{160,2... | collective-permute-start | bytes 737288 | tf_op jit(solution)/shard_map/ppermute | solution.py:49
  310.7 14.1 %collective-permute-start.15 = (f32[4,15360]{1,0:T(4,128)S(1)}, f32[4,15360]{1,0:T(4,128)S(1)}, u32[]{:S(2)}, u32[]{:S(2)}) collective-permute-start(f32[4,15360]{1,0:T(4,128)S(1)} %get-tuple-element.20), channel_id=1, source_target_pairs={{96,0},{0,32},{32,64},{64,96},{224,128},{128,160},{160,192},{192,2... | collective-permute-start | bytes 737288 | tf_op jit(solution)/shard_map/ppermute | solution.py:49
  325.1 7.2 %collective-permute-start.16 = (f32[15360]{0:T(1024)S(1)}, f32[15360]{0:T(1024)S(1)}, u32[]{:S(2)}, u32[]{:S(2)}) collective-permute-start(f32[15360]{0:T(1024)S(1)} %bitcast.145), channel_id=1, source_target_pairs={{8,0},{9,1},{10,2},{11,3},{12,4},{13,5},{14,6},{15,7},{16,8},{17,9... | collective-permute-start | bytes 184328 | tf_op jit(solution)/shard_map/ppermute | solution.py:49
  327.3 6.5 %collective-permute-start.17 = (f32[15360]{0:T(1024)S(1)}, f32[15360]{0:T(1024)S(1)}, u32[]{:S(2)}, u32[]{:S(2)}) collective-permute-start(f32[15360]{0:T(1024)S(1)} %bitcast.144), channel_id=1, source_target_pairs={{16,0},{17,1},{18,2},{19,3},{20,4},{21,5},{22,6},{23,7},{24,8},{25... | collective-permute-start | bytes 184328 | tf_op jit(solution)/shard_map/ppermute | solution.py:49
  329.7 6.5 %collective-permute-start.18 = (f32[15360]{0:T(1024)S(1)}, f32[15360]{0:T(1024)S(1)}, u32[]{:S(2)}, u32[]{:S(2)}) collective-permute-start(f32[15360]{0:T(1024)S(1)} %bitcast.143), channel_id=1, source_target_pairs={{24,0},{25,1},{26,2},{27,3},{28,4},{29,5},{30,6},{31,7},{0,8},{1,9... | collective-permute-start | bytes 184328 | tf_op jit(solution)/shard_map/ppermute | solution.py:49
  336.3 8.4 %collective-permute-start.19 = (f32[15360]{0:T(1024)S(1)}, f32[15360]{0:T(1024)S(1)}, u32[]{:S(2)}, u32[]{:S(2)}) collective-permute-start(f32[15360]{0:T(1024)S(1)} %add_add_fusion), channel_id=1, source_target_pairs={{2,0},{3,1},{4,2},{5,3},{6,4},{7,5},{0,6},{1,7},{10,8},{11,9},{12,... | collective-permute-start | bytes 184328 | tf_op jit(solution)/shard_map/ppermute | solution.py:49
  338.8 5.9 %collective-permute-start.20 = (f32[15360]{0:T(1024)S(1)}, f32[15360]{0:T(1024)S(1)}, u32[]{:S(2)}, u32[]{:S(2)}) collective-permute-start(f32[15360]{0:T(1024)S(1)} %add_add_fusion), channel_id=1, source_target_pairs={{4,0},{5,1},{6,2},{7,3},{0,4},{1,5},{2,6},{3,7},{12,8},{13,9},{14,... | collective-permute-start | bytes 184328 | tf_op jit(solution)/shard_map/ppermute | solution.py:49
  341.7 6.9 %collective-permute-start.21 = (f32[15360]{0:T(1024)S(1)}, f32[15360]{0:T(1024)S(1)}, u32[]{:S(2)}, u32[]{:S(2)}) collective-permute-start(f32[15360]{0:T(1024)S(1)} %add_add_fusion), channel_id=1, source_target_pairs={{6,0},{7,1},{0,2},{1,3},{2,4},{3,5},{4,6},{5,7},{14,8},{15,9},{8,1... | collective-permute-start | bytes 184328 | tf_op jit(solution)/shard_map/ppermute | solution.py:49
  350.2 15.4 %collective-permute-start.22 = (f32[15360]{0:T(1024)S(1)}, f32[15360]{0:T(1024)S(1)}, u32[]{:S(2)}, u32[]{:S(2)}) collective-permute-start(f32[15360]{0:T(1024)S(1)} %bitcast.123), channel_id=1, source_target_pairs={{128,0},{160,32},{192,64},{224,96},{256,128},{288,160},{320,192},{... | collective-permute-start | bytes 184328 | tf_op jit(solution)/shard_map/ppermute | solution.py:49
  354.5 13.8 %collective-permute-start.23 = (f32[15360]{0:T(1024)S(1)}, f32[15360]{0:T(1024)S(1)}, u32[]{:S(2)}, u32[]{:S(2)}) collective-permute-start(f32[15360]{0:T(1024)S(1)} %bitcast.124), channel_id=1, source_target_pairs={{256,0},{288,32},{320,64},{352,96},{384,128},{416,160},{448,192},{... | collective-permute-start | bytes 184328 | tf_op jit(solution)/shard_map/ppermute | solution.py:49
  361.0 14.5 %collective-permute-start.24 = (f32[15360]{0:T(1024)S(1)}, f32[15360]{0:T(1024)S(1)}, u32[]{:S(2)}, u32[]{:S(2)}) collective-permute-start(f32[15360]{0:T(1024)S(1)} %bitcast.125), channel_id=1, source_target_pairs={{384,0},{416,32},{448,64},{480,96},{0,128},{32,160},{64,192},{96,2... | collective-permute-start | bytes 184328 | tf_op jit(solution)/shard_map/ppermute | solution.py:49
  377.1 7.3 %collective-permute-start.25 = (f32[15360]{0:T(1024)S(1)}, f32[15360]{0:T(1024)S(1)}, u32[]{:S(2)}, u32[]{:S(2)}) collective-permute-start(f32[15360]{0:T(1024)S(1)} %bitcast.127), channel_id=1, source_target_pairs={{8,0},{9,1},{10,2},{11,3},{12,4},{13,5},{14,6},{15,7},{16,8},{17,9... | collective-permute-start | bytes 184328 | tf_op jit(solution)/shard_map/ppermute | solution.py:49
  379.0 6.5 %collective-permute-start.26 = (f32[15360]{0:T(1024)S(1)}, f32[15360]{0:T(1024)S(1)}, u32[]{:S(2)}, u32[]{:S(2)}) collective-permute-start(f32[15360]{0:T(1024)S(1)} %bitcast.128), channel_id=1, source_target_pairs={{16,0},{17,1},{18,2},{19,3},{20,4},{21,5},{22,6},{23,7},{24,8},{25... | collective-permute-start | bytes 184328 | tf_op jit(solution)/shard_map/ppermute | solution.py:49
  382.1 6.2 %collective-permute-start.27 = (f32[15360]{0:T(1024)S(1)}, f32[15360]{0:T(1024)S(1)}, u32[]{:S(2)}, u32[]{:S(2)}) collective-permute-start(f32[15360]{0:T(1024)S(1)} %bitcast.129), channel_id=1, source_target_pairs={{24,0},{25,1},{26,2},{27,3},{28,4},{29,5},{30,6},{31,7},{0,8},{1,9... | collective-permute-start | bytes 184328 | tf_op jit(solution)/shard_map/ppermute | solution.py:49
  389.6 11.3 %collective-permute-start.28 = (f32[4,15360]{1,0:T(4,128)S(1)}, f32[4,15360]{1,0:T(4,128)S(1)}, u32[]{:S(2)}, u32[]{:S(2)}) collective-permute-start(f32[4,15360]{1,0:T(4,128)S(1)} %get-tuple-element.14), channel_id=1, source_target_pairs={{32,0},{64,32},{96,64},{0,96},{160,128},{192,160},{224,192},{128,2... | collective-permute-start | bytes 737288 | tf_op jit(solution)/shard_map/ppermute | solution.py:49
  393.4 8.4 %collective-permute-start.29 = (f32[4,15360]{1,0:T(4,128)S(1)}, f32[4,15360]{1,0:T(4,128)S(1)}, u32[]{:S(2)}, u32[]{:S(2)}) collective-permute-start(f32[4,15360]{1,0:T(4,128)S(1)} %get-tuple-element.14), channel_id=1, source_target_pairs={{64,0},{96,32},{0,64},{32,96},{192,128},{224,160},{128,192},{160,2... | collective-permute-start | bytes 737288 | tf_op jit(solution)/shard_map/ppermute | solution.py:49
  398.1 12.0 %collective-permute-start.30 = (f32[4,15360]{1,0:T(4,128)S(1)}, f32[4,15360]{1,0:T(4,128)S(1)}, u32[]{:S(2)}, u32[]{:S(2)}) collective-permute-start(f32[4,15360]{1,0:T(4,128)S(1)} %get-tuple-element.14), channel_id=1, source_target_pairs={{96,0},{0,32},{32,64},{64,96},{224,128},{128,160},{160,192},{192,2... | collective-permute-start | bytes 737288 | tf_op jit(solution)/shard_map/ppermute | solution.py:49
  410.4 6.0 %collective-permute-start.31 = (f32[4,4,15360]{2,1,0:T(4,128)S(1)}, f32[4,4,15360]{2,1,0:T(4,128)S(1)}, u32[]{:S(2)}, u32[]{:S(2)}) collective-permute-start(f32[4,4,15360]{2,1,0:T(4,128)S(1)} %constant_dynamic-slice_fusion), channel_id=1, source_target_pairs={{1,0},{0,1},{3,2},{2,3},{5,4},{4,5},{7,6},{6,7},{9,8},{8,9},{11,10... | collective-permute-start | bytes 2949128 | tf_op jit(solution)/shard_map/ppermute | solution.py:49
Sparse Core Ops, SparseCore 0:
  11.6 97.5 all-gather.1

commit v3 on v1

--- a/solution.py
+++ b/solution.py
@@ -30,7 +30,8 @@
     "x": ("dp", 1, 4),
     "zhi": ("dp", 4, 4),
 }
-RS_ORDER = ("core", "x", "y", "zlo", "zhi")
+RS_ORDER = ("core", "x", "y")
+SUM_ORDER = ("zlo", "zhi")
 
 
 def coord(dim):
@@ -62,8 +63,16 @@
     size = DIMS[dim][2]
     stacked = jnp.stack([array] + [shift(array, dim, step) for step in range(1, size)])
     if ordered:
-        stacked = jnp.roll(stacked, coord(dim), axis=0)
+        slots = (jnp.arange(size) - coord(dim)) % size
+        stacked = jnp.take(stacked, slots, axis=0)
     return stacked
+
+
+def sum_in_order(stacked):
+    total = stacked[0]
+    for index in range(1, stacked.shape[0]):
+        total = total + stacked[index]
+    return total
 
 
 def all_reduce_flat(flat):
@@ -71,6 +80,8 @@
     chunks = flat.reshape(*sizes, -1)
     for dim in RS_ORDER:
         chunks = reduce_scatter_dim(chunks, dim)
+    for dim in SUM_ORDER:
+        chunks = sum_in_order(gather_dim(chunks, dim))
     for dim in reversed(RS_ORDER):
         chunks = gather_dim(chunks, dim)
     return chunks.reshape(-1)

time: 443 us -> 411 us (0.928)
  starting transfers between devices: 129 us -> 102 us
  waiting for transfers between devices: 199 us -> 193 us
    ppermute x34 -> x28, starting transfers between devices: 124 us -> 98 us  [shift(): return lax.ppermute(array, axis, pairs)]
    ppermute x34 -> x28, waiting for transfers between devices: 81.4 us -> 75 us  [shift(): return lax.ppermute(array, axis, pairs)]
    gather x0 -> x5, local copies, waits for them, and re-layouts: none -> 6.15 us  [gather_dim(): stacked = jnp.take(stacked, slots, axis=0)]
    select_n x0 -> x2, local copies, waits for them, and re-layouts: none -> 4.57 us  [gather_dim(): stacked = jnp.take(stacked, slots, axis=0)]
  transfers between devices with their start and end apart: 37 -> 31, of which waited for: 21 -> 17; matrix products, arithmetic and copies ran while one was open for 7% -> 8% of each run, Pallas kernels for 0% -> 0%
where the time goes in v3:
time: 411 us; the launch traced here: 409 us
  waiting for transfers between devices  193 us (47%)
  starting transfers between devices  102 us (25%)
  matrix products  35.1 us (9%)
  local copies, waits for them, and re-layouts  34 us (8%)
  other arithmetic  27.2 us (7%)
  between operations  17.9 us (4%)
    all_gather x1, waiting for transfers between devices, on_device(): own_taps = lax.all_gather(own_half, 'dp', axis=1, tiled=True)  118 us
    ppermute x28, starting transfers between devices, shift(): return lax.ppermute(array, axis, pairs)  98 us
    ppermute x28, waiting for transfers between devices, shift(): return lax.ppermute(array, axis, pairs)  75 us
    dot_general x4, matrix products, on_device(): jnp.dot(score_grad, key_part, preferred_element_type=jnp.float32)  13.7 us
    dot_general x2, matrix products, stacked_conv(): return jnp.dot(windows, flat_taps, preferred_element_type=jnp.float32)  8.59 us
  transfers between devices with their start and end apart: 31, of which 17 were waited for; matrix products, arithmetic and copies ran while one was open for 8% of the time, Pallas kernels for 0%

profile of v3, /device:TPU:1, one launch (start us, length us, event | category | flops | bytes accessed | tf_op | source)
XLA Modules:
  0.0 409.4 jit_solution(905088614545148747)
XLA Ops:
  9.0 117.8 %all-gather.2.cloned.1.call-done = bf16[5,768,384]{2,1,0:T(8,128)(2,1)} async-done(((bf16[5,48,384]{2,1,0:T(8,128)(2,1)}), bf16[5,768,384]{2,1,0:T(8,128)(2,1)}) %all-gather.2.cloned.1.call-update) | async-done | bytes 2949136 | tf_op jit(solution)/shard_map/all_gather | solution.py:155
  126.8 3.1 collective-permute-start.2
  133.3 1.9 collective-permute-start
  135.3 2.4 collective-permute-start.1
  145.2 7.6 %dot_general.77 = bf16[128,4,3840]{2,1,0:T(4,128)(2,1)} reshape(bf16[512,3840]{1,0:T(8,128)(2,1)} %fusion.62) | data formatting | bytes 7864320 | tf_op jit(solution)/shard_map/dot_general | solution.py:128
  152.8 4.5 %fusion.14 = f32[128,4,384]{2,0,1:T(8,128)S(1)} fusion(bf16[3840,384,1]{1,0,2:T(8,128)(2,1)S(1)} %bitcast.146, bf16[128,4,3840]{2,1,0:T(4,128)(2,1)} %dot_general.77), kind=kOutput, calls=%fused_computation.28 | convolution fusion | flops 1509949440 | bytes 7667712 | tf_op jit(solution)/shard_map/dot_general | solution.py:128
  157.3 4.1 %fusion.12 = f32[128,4,384]{2,0,1:T(8,128)S(1)} fusion(bf16[3840,384,1]{1,0,2:T(8,128)(2,1)} %bitcast.4, bf16[128,4,3840]{2,1,0:T(4,128)(2,1)S(1)} %copy-done.5), kind=kOutput, calls=%fused_computation.26 | convolution fusion | flops 1509949440 | bytes 7667712 | tf_op jit(solution)/shard_map/dot_general | solution.py:128
  163.3 6.6 %collective-permute-start.3 = (bf16[128,640]{1,0:T(8,128)(2,1)S(1)}, bf16[128,640]{1,0:T(8,128)(2,1)S(1)}, u32[]{:S(2)}, u32[]{:S(2)}) collective-permute-start(bf16[128,640]{1,0:T(8,128)(2,1)S(1)} %get-tuple-element.33), channel_id=1, source_target_pairs={{2,0},{3,1},{4,2},{5,3},{6,4},{7,5},{0,6},{1,7},{10,8},{11,9},{12,... | collective-permute-start | bytes 491528 | tf_op jit(solution)/shard_map/ppermute | solution.py:49
  170.0 1.9 collective-permute-start.4
  171.9 2.2 collective-permute-start.5
  174.1 9.4 %collective-permute-done.4 = bf16[128,640]{1,0:T(8,128)(2,1)S(1)} collective-permute-done((bf16[128,640]{1,0:T(8,128)(2,1)S(1)}, bf16[128,640]{1,0:T(8,128)(2,1)S(1)}, u32[]{:S(2)}, u32[]{:S(2)}) %collective-permute-start.4) | collective-permute-done | bytes 163872 | tf_op jit(solution)/shard_map/ppermute | solution.py:49
  183.7 2.0 collective-permute-start.6
  185.7 5.2 %collective-permute-start.7 = (bf16[4,128,640]{2,1,0:T(8,128)(2,1)S(1)}, bf16[4,128,640]{2,1,0:T(8,128)(2,1)S(1)}, u32[]{:S(2)}, u32[]{:S(2)}) collective-permute-start(bf16[4,128,640]{2,1,0:T(8,128)(2,1)S(1)} %get-tuple-element.23), channel_id=1, source_target_pairs={{16,0},{17,1},{18,2},{19,3},{20,4},{21,5},{22,6},{23,7},{24,8},{25... | collective-permute-start | bytes 1966088 | tf_op jit(solution)/shard_map/ppermute | solution.py:49
  190.8 1.9 collective-permute-start.8
  192.8 8.7 %collective-permute-done.6 = bf16[4,128,640]{2,1,0:T(8,128)(2,1)S(1)} collective-permute-done((bf16[4,128,640]{2,1,0:T(8,128)(2,1)S(1)}, bf16[4,128,640]{2,1,0:T(8,128)(2,1)S(1)}, u32[]{:S(2)}, u32[]{:S(2)}) %collective-permute-start.6) | collective-permute-done | bytes 655392 | tf_op jit(solution)/shard_map/ppermute | solution.py:49
  201.5 2.5 collective-permute-done.7
  204.0 16.1 %collective-permute-done.8 = bf16[4,128,640]{2,1,0:T(8,128)(2,1)S(1)} collective-permute-done((bf16[4,128,640]{2,1,0:T(8,128)(2,1)S(1)}, bf16[4,128,640]{2,1,0:T(8,128)(2,1)S(1)}, u32[]{:S(2)}, u32[]{:S(2)}) %collective-permute-start.8) | collective-permute-done | bytes 655392 | tf_op jit(solution)/shard_map/ppermute | solution.py:49
  221.8 2.6 collective-permute-start.9
  227.6 1.9 convolution_convert_fusion
  229.4 2.0 fusion.121
  235.7 2.3 pad_maximum_fusion
  245.3 3.7 fusion.23
  249.0 3.5 fusion.24
  252.6 3.4 fusion.25
  256.0 3.0 multiply_reduce_fusion.4
  262.4 2.8 pad_maximum_fusion.2
  265.2 2.2 reshape.288
  267.5 1.9 collective-permute-start.10
  269.6 2.4 collective-permute-done.10
  273.6 4.3 %collective-permute-start.11 = (f32[4,15360]{1,0:T(4,128)S(1)}, f32[4,15360]{1,0:T(4,128)S(1)}, u32[]{:S(2)}, u32[]{:S(2)}) collective-permute-start(f32[4,15360]{1,0:T(4,128)S(1)} %get-tuple-element.17), channel_id=1, source_target_pairs={{32,0},{64,32},{96,64},{0,96},{160,128},{192,160},{224,192},{128,2... | collective-permute-start | bytes 737288 | tf_op jit(solution)/shard_map/ppermute | solution.py:49
  277.8 2.4 collective-permute-start.12
  280.2 2.4 collective-permute-start.13
  283.3 4.8 %collective-permute-done.11 = f32[4,15360]{1,0:T(4,128)S(1)} collective-permute-done((f32[4,15360]{1,0:T(4,128)S(1)}, f32[4,15360]{1,0:T(4,128)S(1)}, u32[]{:S(2)}, u32[]{:S(2)}) %collective-permute-start.11) | collective-permute-done | bytes 245792 | tf_op jit(solution)/shard_map/ppermute | solution.py:49
  288.4 6.0 %collective-permute-done.13 = f32[4,15360]{1,0:T(4,128)S(1)} collective-permute-done((f32[4,15360]{1,0:T(4,128)S(1)}, f32[4,15360]{1,0:T(4,128)S(1)}, u32[]{:S(2)}, u32[]{:S(2)}) %collective-permute-start.13) | collective-permute-done | bytes 245792 | tf_op jit(solution)/shard_map/ppermute | solution.py:49
  294.7 2.2 collective-permute-start.14
  297.0 4.9 %collective-permute-start.15 = (f32[15360]{0:T(1024)S(1)}, f32[15360]{0:T(1024)S(1)}, u32[]{:S(2)}, u32[]{:S(2)}) collective-permute-start(f32[15360]{0:T(1024)S(1)} %bitcast.135), channel_id=1, source_target_pairs={{16,0},{17,1},{18,2},{19,3},{20,4},{21,5},{22,6},{23,7},{24,8},{25... | collective-permute-start | bytes 184328 | tf_op jit(solution)/shard_map/ppermute | solution.py:49
  301.8 2.5 collective-permute-start.16
  304.3 3.7 collective-permute-done.16
  308.0 3.0 collective-permute-start.17
  311.1 4.5 %collective-permute-start.18 = (f32[15360]{0:T(1024)S(1)}, f32[15360]{0:T(1024)S(1)}, u32[]{:S(2)}, u32[]{:S(2)}) collective-permute-start(f32[15360]{0:T(1024)S(1)} %add_add_fusion), channel_id=1, source_target_pairs={{4,0},{5,1},{6,2},{7,3},{0,4},{1,5},{2,6},{3,7},{12,8},{13,9},{14,... | collective-permute-start | bytes 184328 | tf_op jit(solution)/shard_map/ppermute | solution.py:49
  315.6 3.4 collective-permute-start.19
  319.0 3.4 collective-permute-done.19
  323.6 4.4 %collective-permute-start.20 = (f32[15360]{0:T(1024)S(1)}, f32[15360]{0:T(1024)S(1)}, u32[]{:S(2)}, u32[]{:S(2)}) collective-permute-start(f32[15360]{0:T(1024)S(1)} %bitcast.125), channel_id=1, source_target_pairs={{128,0},{160,32},{192,64},{224,96},{256,128},{288,160},{320,192},{... | collective-permute-start | bytes 184328 | tf_op jit(solution)/shard_map/ppermute | solution.py:49
  328.0 7.6 %collective-permute-start.21 = (f32[15360]{0:T(1024)S(1)}, f32[15360]{0:T(1024)S(1)}, u32[]{:S(2)}, u32[]{:S(2)}) collective-permute-start(f32[15360]{0:T(1024)S(1)} %bitcast.126), channel_id=1, source_target_pairs={{256,0},{288,32},{320,64},{352,96},{384,128},{416,160},{448,192},{... | collective-permute-start | bytes 184328 | tf_op jit(solution)/shard_map/ppermute | solution.py:49
  335.6 3.8 collective-permute-start.22
  339.5 3.0 collective-permute-done.21
  342.5 4.7 %collective-permute-done.22 = f32[15360]{0:T(1024)S(1)} collective-permute-done((f32[15360]{0:T(1024)S(1)}, f32[15360]{0:T(1024)S(1)}, u32[]{:S(2)}, u32[]{:S(2)}) %collective-permute-start.22) | collective-permute-done | bytes 61472 | tf_op jit(solution)/shard_map/ppermute | solution.py:49
  348.4 1.9 collective-permute-start.23
  350.3 4.4 %collective-permute-start.24 = (f32[15360]{0:T(1024)S(1)}, f32[15360]{0:T(1024)S(1)}, u32[]{:S(2)}, u32[]{:S(2)}) collective-permute-start(f32[15360]{0:T(1024)S(1)} %bitcast.123), channel_id=1, source_target_pairs={{16,0},{17,1},{18,2},{19,3},{20,4},{21,5},{22,6},{23,7},{24,8},{25... | collective-permute-start | bytes 184328 | tf_op jit(solution)/shard_map/ppermute | solution.py:49
  354.7 2.8 collective-permute-start.25
  358.6 2.3 collective-permute-done.25
  361.9 1.9 collective-permute-start.26
  363.8 2.5 collective-permute-start.27
  366.3 2.8 collective-permute-start.28
  369.3 3.0 collective-permute-done.27
  372.3 2.8 collective-permute-done.28
  376.9 9.0 %collective-permute-start.29 = (f32[4,4,15360]{2,1,0:T(4,128)S(1)}, f32[4,4,15360]{2,1,0:T(4,128)S(1)}, u32[]{:S(2)}, u32[]{:S(2)}) collective-permute-start(f32[4,4,15360]{2,1,0:T(4,128)S(1)} %broadcast_select_fusion.1), channel_id=1, source_target_pairs={{1,0},{0,1},{3,2},{2,3},{5,4},{4,5},{7,6},{6,7},{9,8},{8,9},{11,10... | collective-permute-start | bytes 2949128 | tf_op jit(solution)/shard_map/ppermute | solution.py:49
  386.2 1.9 collective-permute-done.29
  388.6 2.9 gather_fusion.1
  391.5 2.1 broadcast_select_fusion
  393.5 2.3 select_n.277
  395.8 2.3 select_n.276
  398.1 2.4 slice.245
  400.5 2.1 slice.244
  (159 shorter events, 41.8 us)
Async XLA Ops:
  7.2 220.4 %copy-start = (bf16[384,768]{1,0:T(8,128)(2,1)S(1)}, bf16[384,768]{1,0:T(8,128)(2,1)}, u32[]{:S(2)}) copy-start(bf16[384,768]{1,0:T(8,128)(2,1)} %param.15) | copy-start | bytes 1769476
  7.2 125.5 %copy-start.1 = (bf16[1,512,768]{2,1,0:T(8,128)(2,1)S(1)}, bf16[1,512,768]{2,1,0:T(8,128)(2,1)}, u32[]{:S(2)}) copy-start(bf16[1,512,768]{2,1,0:T(8,128)(2,1)} %param.10) | copy-start | bytes 2359300
  7.2 119.6 %all-gather.2.cloned.1.call-start = ((), (), s32[]{:S(2)}) async-start(), calls=%async_computation | async-start | bytes 3133440 | tf_op jit(solution)/shard_map/all_gather | solution.py:155
  126.8 30.4 %collective-permute-start.2 = (bf16[5,768,384]{2,1,0:T(8,128)(2,1)}, bf16[5,768,384]{2,1,0:T(8,128)(2,1)}, u32[]{:S(2)}, u32[]{:S(2)}) collective-permute-start(bf16[5,768,384]{2,1,0:T(8,128)(2,1)} %all-gather.2.cloned.1.call-done), channel_id=1, source_target_pairs={{1,0},{0,1},{3,2},{2,3},{5,4},{4,5},{7,6},{6,7},{9,8},{8,9},{11,10... | collective-permute-start | bytes 8847368 | tf_op jit(solution)/shard_map/ppermute | solution.py:49
  133.3 5.9 %collective-permute-start = (bf16[2,768]{1,0:T(2,128)(2,1)S(1)}, bf16[2,768]{1,0:T(2,128)(2,1)S(1)}, u32[]{:S(2)}, u32[]{:S(2)}) collective-permute-start(bf16[2,768]{1,0:T(2,128)(2,1)S(1)} %get-tuple-element.21), channel_id=1, source_target_pairs={{0,1},{1,2},{2,3},{3,4},{4,5},{5,6},{6,7},{7,8},{8,9},{9,10},{10,1... | collective-permute-start | bytes 9224 | tf_op jit(solution)/shard_map/ppermute | solution.py:20
  135.3 7.7 %collective-permute-start.1 = (bf16[2,768]{1,0:T(2,128)(2,1)S(1)}, bf16[2,768]{1,0:T(2,128)(2,1)S(1)}, u32[]{:S(2)}, u32[]{:S(2)}) collective-permute-start(bf16[2,768]{1,0:T(2,128)(2,1)S(1)} %get-tuple-element.20), channel_id=1, source_target_pairs={{1,0},{2,1},{3,2},{4,3},{5,4},{6,5},{7,6},{8,7},{9,8},{10,9},{11,1... | collective-permute-start | bytes 9224 | tf_op jit(solution)/shard_map/ppermute | solution.py:21
  145.2 7.6 %copy-start.25 = (bf16[5,768,384]{2,1,0:T(8,128)(2,1)S(1)}, bf16[5,768,384]{2,1,0:T(8,128)(2,1)}, u32[]{:S(2)}) copy-start(bf16[5,768,384]{2,1,0:T(8,128)(2,1)} %all-gather.2.cloned.1.call-done) | copy-start | bytes 8847364
  152.8 4.5 %copy-start.5 = (bf16[128,4,3840]{2,1,0:T(4,128)(2,1)S(1)}, bf16[128,4,3840]{2,1,0:T(4,128)(2,1)}, u32[]{:S(2)}) copy-start(bf16[128,4,3840]{2,1,0:T(4,128)(2,1)} %dot_general.77) | copy-start | bytes 11796484
  157.3 4.2 %copy-start.4 = (f32[128,4,768]{2,1,0:T(4,128)S(1)}, f32[128,4,768]{2,1,0:T(4,128)}, u32[]{:S(2)}) copy-start(f32[128,4,768]{2,1,0:T(4,128)} %reshape.289) | copy-start | bytes 4718596
  161.4 1.0 copy-start.11
  161.4 1.5 copy-start.26
  162.0 98.3 %copy-start.3 = (bf16[128,768]{1,0:T(8,128)(2,1)}, bf16[128,768]{1,0:T(8,128)(2,1)S(1)}, u32[]{:S(2)}) copy-start(bf16[128,768]{1,0:T(8,128)(2,1)S(1)} %fusion.17) | copy-start | bytes 589828
  163.3 10.8 %collective-permute-start.3 = (bf16[128,640]{1,0:T(8,128)(2,1)S(1)}, bf16[128,640]{1,0:T(8,128)(2,1)S(1)}, u32[]{:S(2)}, u32[]{:S(2)}) collective-permute-start(bf16[128,640]{1,0:T(8,128)(2,1)S(1)} %get-tuple-element.33), channel_id=1, source_target_pairs={{2,0},{3,1},{4,2},{5,3},{6,4},{7,5},{0,6},{1,7},{10,8},{11,9},{12,... | collective-permute-start | bytes 491528 | tf_op jit(solution)/shard_map/ppermute | solution.py:49
  170.0 13.6 %collective-permute-start.4 = (bf16[128,640]{1,0:T(8,128)(2,1)S(1)}, bf16[128,640]{1,0:T(8,128)(2,1)S(1)}, u32[]{:S(2)}, u32[]{:S(2)}) collective-permute-start(bf16[128,640]{1,0:T(8,128)(2,1)S(1)} %get-tuple-element.33), channel_id=1, source_target_pairs={{4,0},{5,1},{6,2},{7,3},{0,4},{1,5},{2,6},{3,7},{12,8},{13,9},{14,... | collective-permute-start | bytes 491528 | tf_op jit(solution)/shard_map/ppermute | solution.py:49
  171.9 11.6 %collective-permute-start.5 = (bf16[128,640]{1,0:T(8,128)(2,1)S(1)}, bf16[128,640]{1,0:T(8,128)(2,1)S(1)}, u32[]{:S(2)}, u32[]{:S(2)}) collective-permute-start(bf16[128,640]{1,0:T(8,128)(2,1)S(1)} %get-tuple-element.33), channel_id=1, source_target_pairs={{6,0},{7,1},{0,2},{1,3},{2,4},{3,5},{4,6},{5,7},{14,8},{15,9},{8,1... | collective-permute-start | bytes 491528 | tf_op jit(solution)/shard_map/ppermute | solution.py:49
  183.7 17.8 %collective-permute-start.6 = (bf16[4,128,640]{2,1,0:T(8,128)(2,1)S(1)}, bf16[4,128,640]{2,1,0:T(8,128)(2,1)S(1)}, u32[]{:S(2)}, u32[]{:S(2)}) collective-permute-start(bf16[4,128,640]{2,1,0:T(8,128)(2,1)S(1)} %get-tuple-element.23), channel_id=1, source_target_pairs={{8,0},{9,1},{10,2},{11,3},{12,4},{13,5},{14,6},{15,7},{16,8},{17,9... | collective-permute-start | bytes 1966088 | tf_op jit(solution)/shard_map/ppermute | solution.py:49
  185.7 18.3 %collective-permute-start.7 = (bf16[4,128,640]{2,1,0:T(8,128)(2,1)S(1)}, bf16[4,128,640]{2,1,0:T(8,128)(2,1)S(1)}, u32[]{:S(2)}, u32[]{:S(2)}) collective-permute-start(bf16[4,128,640]{2,1,0:T(8,128)(2,1)S(1)} %get-tuple-element.23), channel_id=1, source_target_pairs={{16,0},{17,1},{18,2},{19,3},{20,4},{21,5},{22,6},{23,7},{24,8},{25... | collective-permute-start | bytes 1966088 | tf_op jit(solution)/shard_map/ppermute | solution.py:49
  190.8 29.2 %collective-permute-start.8 = (bf16[4,128,640]{2,1,0:T(8,128)(2,1)S(1)}, bf16[4,128,640]{2,1,0:T(8,128)(2,1)S(1)}, u32[]{:S(2)}, u32[]{:S(2)}) collective-permute-start(bf16[4,128,640]{2,1,0:T(8,128)(2,1)S(1)} %get-tuple-element.23), channel_id=1, source_target_pairs={{24,0},{25,1},{26,2},{27,3},{28,4},{29,5},{30,6},{31,7},{0,8},{1,9... | collective-permute-start | bytes 1966088 | tf_op jit(solution)/shard_map/ppermute | solution.py:49
  220.1 4.4 %copy-start.24 = (f32[4]{0:T(128)S(1)}, f32[4]{0:T(128)}, u32[]{:S(2)}) copy-start(f32[4]{0:T(128)} %param.16) | copy-start | bytes 52
  221.8 13.9 %collective-permute-start.9 = (bf16[4,4,128,640]{3,2,1,0:T(8,128)(2,1)}, bf16[4,4,128,640]{3,2,1,0:T(8,128)(2,1)}, u32[]{:S(2)}, u32[]{:S(2)}) collective-permute-start(bf16[4,4,128,640]{3,2,1,0:T(8,128)(2,1)} %get-tuple-element.16), channel_id=1, source_target_pairs={{1,0},{0,1},{3,2},{2,3},{5,4},{4,5},{7,6},{6,7},{9,8},{8,9},{11,10... | collective-permute-start | bytes 7864328 | tf_op jit(solution)/shard_map/ppermute | solution.py:49
  238.0 6.1 %copy-start.2 = (bf16[2,4,4,128,640]{4,3,2,1,0:T(8,128)(2,1)}, bf16[2,4,4,128,640]{4,3,2,1,0:T(8,128)(2,1)S(1)}, u32[]{:S(2)}) copy-start(bf16[2,4,4,128,640]{4,3,2,1,0:T(8,128)(2,1)S(1)} %pad_maximum_fusion) | copy-start | bytes 15728644
  239.2 1.7 copy-start.6
  239.7 2.2 copy-start.7
  240.4 2.6 copy-start.8
  243.0 1.1 copy-start.12
  245.3 16.8 %copy-start.13 = (bf16[128,96]{0,1:T(8,128)(2,1)}, bf16[128,96]{0,1:T(8,128)(2,1)S(1)}, u32[]{:S(2)}) copy-start(bf16[128,96]{0,1:T(8,128)(2,1)S(1)} %get-tuple-element.34) | copy-start | bytes 73732
  245.3 16.8 %copy-start.15 = (bf16[128,96]{0,1:T(8,128)(2,1)}, bf16[128,96]{0,1:T(8,128)(2,1)S(1)}, u32[]{:S(2)}) copy-start(bf16[128,96]{0,1:T(8,128)(2,1)S(1)} %get-tuple-element.35) | copy-start | bytes 73732
  249.0 7.0 %copy-start.21 = (f32[128,64]{1,0:T(8,128)}, f32[128,64]{1,0:T(8,128)S(1)}, u32[]{:S(2)}) copy-start(f32[128,64]{1,0:T(8,128)S(1)} %fusion.23) | copy-start | bytes 98308
  252.6 3.5 copy-start.22
  252.6 3.5 copy-start.9
  256.0 3.1 copy-start.23
  259.1 2.9 copy-start.10
  259.1 2.9 copy-start.17
  259.1 2.9 copy-start.19
  267.5 4.6 %collective-permute-start.10 = (f32[4,4,15360]{2,1,0:T(4,128)S(1)}, f32[4,4,15360]{2,1,0:T(4,128)}, u32[]{:S(2)}, u32[]{:S(2)}) collective-permute-start(f32[4,4,15360]{2,1,0:T(4,128)S(1)} %dynamic-slice_bitcast_fusion), channel_id=1, source_target_pairs={{1,0},{0,1},{3,2},{2,3},{5,4},{4,5},{7,6},{6,7},{9,8},{8,9},{11,10... | collective-permute-start | bytes 2949128 | tf_op jit(solution)/shard_map/ppermute | solution.py:49
  273.6 14.5 %collective-permute-start.11 = (f32[4,15360]{1,0:T(4,128)S(1)}, f32[4,15360]{1,0:T(4,128)S(1)}, u32[]{:S(2)}, u32[]{:S(2)}) collective-permute-start(f32[4,15360]{1,0:T(4,128)S(1)} %get-tuple-element.17), channel_id=1, source_target_pairs={{32,0},{64,32},{96,64},{0,96},{160,128},{192,160},{224,192},{128,2... | collective-permute-start | bytes 737288 | tf_op jit(solution)/shard_map/ppermute | solution.py:49
  277.8 10.5 %collective-permute-start.12 = (f32[4,15360]{1,0:T(4,128)S(1)}, f32[4,15360]{1,0:T(4,128)S(1)}, u32[]{:S(2)}, u32[]{:S(2)}) collective-permute-start(f32[4,15360]{1,0:T(4,128)S(1)} %get-tuple-element.19), channel_id=1, source_target_pairs={{64,0},{96,32},{0,64},{32,96},{192,128},{224,160},{128,192},{160,2... | collective-permute-start | bytes 737288 | tf_op jit(solution)/shard_map/ppermute | solution.py:49
  280.2 14.2 %collective-permute-start.13 = (f32[4,15360]{1,0:T(4,128)S(1)}, f32[4,15360]{1,0:T(4,128)S(1)}, u32[]{:S(2)}, u32[]{:S(2)}) collective-permute-start(f32[4,15360]{1,0:T(4,128)S(1)} %get-tuple-element.18), channel_id=1, source_target_pairs={{96,0},{0,32},{32,64},{64,96},{224,128},{128,160},{160,192},{192,2... | collective-permute-start | bytes 737288 | tf_op jit(solution)/shard_map/ppermute | solution.py:49
  294.7 9.6 %collective-permute-start.14 = (f32[15360]{0:T(1024)S(1)}, f32[15360]{0:T(1024)S(1)}, u32[]{:S(2)}, u32[]{:S(2)}) collective-permute-start(f32[15360]{0:T(1024)S(1)} %bitcast.136), channel_id=1, source_target_pairs={{8,0},{9,1},{10,2},{11,3},{12,4},{13,5},{14,6},{15,7},{16,8},{17,9... | collective-permute-start | bytes 184328 | tf_op jit(solution)/shard_map/ppermute | solution.py:49
  297.0 7.4 %collective-permute-start.15 = (f32[15360]{0:T(1024)S(1)}, f32[15360]{0:T(1024)S(1)}, u32[]{:S(2)}, u32[]{:S(2)}) collective-permute-start(f32[15360]{0:T(1024)S(1)} %bitcast.135), channel_id=1, source_target_pairs={{16,0},{17,1},{18,2},{19,3},{20,4},{21,5},{22,6},{23,7},{24,8},{25... | collective-permute-start | bytes 184328 | tf_op jit(solution)/shard_map/ppermute | solution.py:49
  301.8 6.2 %collective-permute-start.16 = (f32[15360]{0:T(1024)S(1)}, f32[15360]{0:T(1024)S(1)}, u32[]{:S(2)}, u32[]{:S(2)}) collective-permute-start(f32[15360]{0:T(1024)S(1)} %bitcast.134), channel_id=1, source_target_pairs={{24,0},{25,1},{26,2},{27,3},{28,4},{29,5},{30,6},{31,7},{0,8},{1,9... | collective-permute-start | bytes 184328 | tf_op jit(solution)/shard_map/ppermute | solution.py:49
  308.0 11.0 %collective-permute-start.17 = (f32[15360]{0:T(1024)S(1)}, f32[15360]{0:T(1024)S(1)}, u32[]{:S(2)}, u32[]{:S(2)}) collective-permute-start(f32[15360]{0:T(1024)S(1)} %add_add_fusion), channel_id=1, source_target_pairs={{2,0},{3,1},{4,2},{5,3},{6,4},{7,5},{0,6},{1,7},{10,8},{11,9},{12,... | collective-permute-start | bytes 184328 | tf_op jit(solution)/shard_map/ppermute | solution.py:49
  311.1 7.9 %collective-permute-start.18 = (f32[15360]{0:T(1024)S(1)}, f32[15360]{0:T(1024)S(1)}, u32[]{:S(2)}, u32[]{:S(2)}) collective-permute-start(f32[15360]{0:T(1024)S(1)} %add_add_fusion), channel_id=1, source_target_pairs={{4,0},{5,1},{6,2},{7,3},{0,4},{1,5},{2,6},{3,7},{12,8},{13,9},{14,... | collective-permute-start | bytes 184328 | tf_op jit(solution)/shard_map/ppermute | solution.py:49
  315.6 6.8 %collective-permute-start.19 = (f32[15360]{0:T(1024)S(1)}, f32[15360]{0:T(1024)S(1)}, u32[]{:S(2)}, u32[]{:S(2)}) collective-permute-start(f32[15360]{0:T(1024)S(1)} %add_add_fusion), channel_id=1, source_target_pairs={{6,0},{7,1},{0,2},{1,3},{2,4},{3,5},{4,6},{5,7},{14,8},{15,9},{8,1... | collective-permute-start | bytes 184328 | tf_op jit(solution)/shard_map/ppermute | solution.py:49
  323.3 34.2 %copy-start.14 = (bf16[128,96]{0,1:T(8,128)(2,1)S(1)}, bf16[128,96]{0,1:T(8,128)(2,1)}, u32[]{:S(2)}) copy-start(bf16[128,96]{0,1:T(8,128)(2,1)} %copy-done.13) | copy-start | bytes 73732
  323.3 34.2 %copy-start.16 = (bf16[128,96]{0,1:T(8,128)(2,1)S(1)}, bf16[128,96]{0,1:T(8,128)(2,1)}, u32[]{:S(2)}) copy-start(bf16[128,96]{0,1:T(8,128)(2,1)} %copy-done.15) | copy-start | bytes 73732
  323.3 34.2 %copy-start.18 = (bf16[128,96]{0,1:T(8,128)(2,1)S(1)}, bf16[128,96]{0,1:T(8,128)(2,1)}, u32[]{:S(2)}) copy-start(bf16[128,96]{0,1:T(8,128)(2,1)} %get-tuple-element.36) | copy-start | bytes 73732
  323.3 34.2 %copy-start.20 = (bf16[128,96]{0,1:T(8,128)(2,1)S(1)}, bf16[128,96]{0,1:T(8,128)(2,1)}, u32[]{:S(2)}) copy-start(bf16[128,96]{0,1:T(8,128)(2,1)} %get-tuple-element.37) | copy-start | bytes 73732
  323.6 15.9 %collective-permute-start.20 = (f32[15360]{0:T(1024)S(1)}, f32[15360]{0:T(1024)S(1)}, u32[]{:S(2)}, u32[]{:S(2)}) collective-permute-start(f32[15360]{0:T(1024)S(1)} %bitcast.125), channel_id=1, source_target_pairs={{128,0},{160,32},{192,64},{224,96},{256,128},{288,160},{320,192},{... | collective-permute-start | bytes 184328 | tf_op jit(solution)/shard_map/ppermute | solution.py:49
  328.0 14.4 %collective-permute-start.21 = (f32[15360]{0:T(1024)S(1)}, f32[15360]{0:T(1024)S(1)}, u32[]{:S(2)}, u32[]{:S(2)}) collective-permute-start(f32[15360]{0:T(1024)S(1)} %bitcast.126), channel_id=1, source_target_pairs={{256,0},{288,32},{320,64},{352,96},{384,128},{416,160},{448,192},{... | collective-permute-start | bytes 184328 | tf_op jit(solution)/shard_map/ppermute | solution.py:49
  335.6 11.6 %collective-permute-start.22 = (f32[15360]{0:T(1024)S(1)}, f32[15360]{0:T(1024)S(1)}, u32[]{:S(2)}, u32[]{:S(2)}) collective-permute-start(f32[15360]{0:T(1024)S(1)} %bitcast.127), channel_id=1, source_target_pairs={{384,0},{416,32},{448,64},{480,96},{0,128},{32,160},{64,192},{96,2... | collective-permute-start | bytes 184328 | tf_op jit(solution)/shard_map/ppermute | solution.py:49
  348.4 10.2 %collective-permute-start.23 = (f32[15360]{0:T(1024)S(1)}, f32[15360]{0:T(1024)S(1)}, u32[]{:S(2)}, u32[]{:S(2)}) collective-permute-start(f32[15360]{0:T(1024)S(1)} %bitcast.122), channel_id=1, source_target_pairs={{8,0},{9,1},{10,2},{11,3},{12,4},{13,5},{14,6},{15,7},{16,8},{17,9... | collective-permute-start | bytes 184328 | tf_op jit(solution)/shard_map/ppermute | solution.py:49
  350.3 8.2 %collective-permute-start.24 = (f32[15360]{0:T(1024)S(1)}, f32[15360]{0:T(1024)S(1)}, u32[]{:S(2)}, u32[]{:S(2)}) collective-permute-start(f32[15360]{0:T(1024)S(1)} %bitcast.123), channel_id=1, source_target_pairs={{16,0},{17,1},{18,2},{19,3},{20,4},{21,5},{22,6},{23,7},{24,8},{25... | collective-permute-start | bytes 184328 | tf_op jit(solution)/shard_map/ppermute | solution.py:49
  354.7 6.2 %collective-permute-start.25 = (f32[15360]{0:T(1024)S(1)}, f32[15360]{0:T(1024)S(1)}, u32[]{:S(2)}, u32[]{:S(2)}) collective-permute-start(f32[15360]{0:T(1024)S(1)} %bitcast.124), channel_id=1, source_target_pairs={{24,0},{25,1},{26,2},{27,3},{28,4},{29,5},{30,6},{31,7},{0,8},{1,9... | collective-permute-start | bytes 184328 | tf_op jit(solution)/shard_map/ppermute | solution.py:49
  361.9 7.4 %collective-permute-start.26 = (f32[4,15360]{1,0:T(4,128)S(1)}, f32[4,15360]{1,0:T(4,128)S(1)}, u32[]{:S(2)}, u32[]{:S(2)}) collective-permute-start(f32[4,15360]{1,0:T(4,128)S(1)} %broadcast_select_fusion.2), channel_id=1, source_target_pairs={{32,0},{64,32},{96,64},{0,96},{160,128},{192,160},{224,192},{128,2... | collective-permute-start | bytes 737288 | tf_op jit(solution)/shard_map/ppermute | solution.py:49
  363.8 8.4 %collective-permute-start.27 = (f32[4,15360]{1,0:T(4,128)S(1)}, f32[4,15360]{1,0:T(4,128)S(1)}, u32[]{:S(2)}, u32[]{:S(2)}) collective-permute-start(f32[4,15360]{1,0:T(4,128)S(1)} %broadcast_select_fusion.2), channel_id=1, source_target_pairs={{64,0},{96,32},{0,64},{32,96},{192,128},{224,160},{128,192},{160,2... | collective-permute-start | bytes 737288 | tf_op jit(solution)/shard_map/ppermute | solution.py:49
  366.3 8.8 %collective-permute-start.28 = (f32[4,15360]{1,0:T(4,128)S(1)}, f32[4,15360]{1,0:T(4,128)S(1)}, u32[]{:S(2)}, u32[]{:S(2)}) collective-permute-start(f32[4,15360]{1,0:T(4,128)S(1)} %broadcast_select_fusion.2), channel_id=1, source_target_pairs={{96,0},{0,32},{32,64},{64,96},{224,128},{128,160},{160,192},{192,2... | collective-permute-start | bytes 737288 | tf_op jit(solution)/shard_map/ppermute | solution.py:49
  376.9 11.2 %collective-permute-start.29 = (f32[4,4,15360]{2,1,0:T(4,128)S(1)}, f32[4,4,15360]{2,1,0:T(4,128)S(1)}, u32[]{:S(2)}, u32[]{:S(2)}) collective-permute-start(f32[4,4,15360]{2,1,0:T(4,128)S(1)} %broadcast_select_fusion.1), channel_id=1, source_target_pairs={{1,0},{0,1},{3,2},{2,3},{5,4},{4,5},{7,6},{6,7},{9,8},{8,9},{11,10... | collective-permute-start | bytes 2949128 | tf_op jit(solution)/shard_map/ppermute | solution.py:49
Sparse Core Ops, SparseCore 0:
  11.6 115.1 all-gather.1

commit v4 on v3

--- a/solution.py
+++ b/solution.py
@@ -64,7 +64,7 @@
     stacked = jnp.stack([array] + [shift(array, dim, step) for step in range(1, size)])
     if ordered:
         slots = (jnp.arange(size) - coord(dim)) % size
-        stacked = jnp.take(stacked, slots, axis=0)
+        stacked = jnp.take(stacked, slots, axis=0, mode="clip")
     return stacked
 
 
@@ -150,9 +150,17 @@
     activated = activate(layer_norm(incoming_tensor.astype(jnp.float32))).astype(jnp.bfloat16)
     padded = padded_2(activated, (("seq", 0),), margin)
     core = coord("core")
-    half_width = kernel_coefficients.shape[2] // 2
-    own_half = lax.dynamic_slice_in_dim(kernel_coefficients, core * half_width, half_width, axis=2)
-    own_taps = lax.all_gather(own_half, "dp", axis=1, tiled=True)
+    quarter = kernel_coefficients.shape[2] // 4
+    first_part = lax.dynamic_slice_in_dim(kernel_coefficients, 2 * core * quarter, quarter, axis=2)
+    second_part = lax.dynamic_slice_in_dim(
+        kernel_coefficients, (2 * core + 1) * quarter, quarter, axis=2
+    )
+    first_taps = lax.all_gather(first_part, "dp", axis=1, tiled=True)
+    routed = gather_dim(gather_dim(second_part, "x"), "zhi")
+    blocks = routed.shape[0] * routed.shape[1]
+    routed = routed.reshape(blocks, *second_part.shape)
+    second_taps = jnp.moveaxis(routed, 0, 1).reshape(first_taps.shape)
+    own_taps = jnp.concatenate([first_taps, second_taps], axis=2)
     other_taps = shift(own_taps, "core", 1)
     conv_own = stacked_conv(padded, own_taps, length_fine)
     conv_other = stacked_conv(padded, other_taps, length_fine)

time: 411 us -> 455 us (1.11)
  starting transfers between devices: 102 us -> 132 us
  local copies, waits for them, and re-layouts: 34 us -> 39.8 us
    ppermute x28 -> x34, waiting for transfers between devices: 75 us -> 131 us  [shift(): return lax.ppermute(array, axis, pairs)]
    all_gather x1, waiting for transfers between devices: 118 us -> 64.9 us  [on_device(): first_taps = lax.all_gather(first_part, 'dp', axis=1, tiled=True)]
    ppermute x28 -> x34, starting transfers between devices: 98 us -> 128 us  [shift(): return lax.ppermute(array, axis, pairs)]
    select_n x2 -> x0, local copies, waits for them, and re-layouts: 4.57 us -> none  [gather_dim(): stacked = jnp.take(stacked, slots, axis=0)]
  transfers between devices with their start and end apart: 31 -> 37, of which waited for: 17 -> 23; matrix products, arithmetic and copies ran while one was open for 8% -> 8% of each run, Pallas kernels for 0% -> 0%
where the time goes in v4:
time: 455 us; the launch traced here: 453 us
  waiting for transfers between devices  196 us (43%)
  starting transfers between devices  132 us (29%)
  local copies, waits for them, and re-layouts  39.8 us (9%)
  matrix products  37.9 us (8%)
  other arithmetic  28.6 us (6%)
  between operations  18 us (4%)
    ppermute x34, waiting for transfers between devices, shift(): return lax.ppermute(array, axis, pairs)  131 us
    ppermute x34, starting transfers between devices, shift(): return lax.ppermute(array, axis, pairs)  128 us
    all_gather x1, waiting for transfers between devices, on_device(): first_taps = lax.all_gather(first_part, 'dp', axis=1, tiled=True)  64.9 us
    dot_general x4, matrix products, on_device(): jnp.dot(score_grad, key_part, preferred_element_type=jnp.float32)  13.7 us
    dot_general x2, matrix products, stacked_conv(): return jnp.dot(windows, flat_taps, preferred_element_type=jnp.float32)  10.3 us
  transfers between devices with their start and end apart: 37, of which 23 were waited for; matrix products, arithmetic and copies ran while one was open for 8% of the time, Pallas kernels for 0%

profile of v4, /device:TPU:1, one launch (start us, length us, event | category | flops | bytes accessed | tf_op | source)
XLA Modules:
  0.0 452.9 jit_solution(15476751583919241479)
XLA Ops:
  9.1 5.2 %collective-permute-start.2 = (bf16[5,48,192]{2,1,0:T(8,128)(2,1)S(1)}, bf16[5,48,192]{2,1,0:T(8,128)(2,1)S(1)}, u32[]{:S(2)}, u32[]{:S(2)}) collective-permute-start(bf16[5,48,192]{2,1,0:T(8,128)(2,1)S(1)} %get-tuple-element.24), channel_id=1, source_target_pairs={{32,0},{64,32},{96,64},{0,96},{160,128},{192,160},{224,192},{128,2... | collective-permute-start | bytes 276488 | tf_op jit(solution)/shard_map/ppermute | solution.py:49
  14.3 2.4 collective-permute-start.3
  16.8 2.5 collective-permute-start.4
  19.3 2.1 collective-permute-done.3
  21.4 2.1 collective-permute-done.4
  24.3 10.1 %collective-permute-start.7 = (bf16[4,5,48,192]{3,2,1,0:T(8,128)(2,1)S(1)}, bf16[4,5,48,192]{3,2,1,0:T(8,128)(2,1)S(1)}, u32[]{:S(2)}, u32[]{:S(2)}) collective-permute-start(bf16[4,5,48,192]{3,2,1,0:T(8,128)(2,1)S(1)} %gather_fusion), channel_id=1, source_target_pairs={{384,0},{416,32},{448,64},{480,96},{0,128},{32,160},{64,192},{96,2... | collective-permute-start | bytes 1105928 | tf_op jit(solution)/shard_map/ppermute | solution.py:49
  34.5 5.6 %collective-permute-start.5 = (bf16[4,5,48,192]{3,2,1,0:T(8,128)(2,1)S(1)}, bf16[4,5,48,192]{3,2,1,0:T(8,128)(2,1)S(1)}, u32[]{:S(2)}, u32[]{:S(2)}) collective-permute-start(bf16[4,5,48,192]{3,2,1,0:T(8,128)(2,1)S(1)} %gather_fusion), channel_id=1, source_target_pairs={{128,0},{160,32},{192,64},{224,96},{256,128},{288,160},{320,192},{... | collective-permute-start | bytes 1105928 | tf_op jit(solution)/shard_map/ppermute | solution.py:49
  40.0 10.3 %collective-permute-start.6 = (bf16[4,5,48,192]{3,2,1,0:T(8,128)(2,1)S(1)}, bf16[4,5,48,192]{3,2,1,0:T(8,128)(2,1)S(1)}, u32[]{:S(2)}, u32[]{:S(2)}) collective-permute-start(bf16[4,5,48,192]{3,2,1,0:T(8,128)(2,1)S(1)} %gather_fusion), channel_id=1, source_target_pairs={{256,0},{288,32},{320,64},{352,96},{384,128},{416,160},{448,192},{... | collective-permute-start | bytes 1105928 | tf_op jit(solution)/shard_map/ppermute | solution.py:49
  50.3 5.8 %collective-permute-done.7 = bf16[4,5,48,192]{3,2,1,0:T(8,128)(2,1)S(1)} collective-permute-done((bf16[4,5,48,192]{3,2,1,0:T(8,128)(2,1)S(1)}, bf16[4,5,48,192]{3,2,1,0:T(8,128)(2,1)S(1)}, u32[]{:S(2)}, u32[]{:S(2)}) %collective-permute-start.7) | collective-permute-done | bytes 368672 | tf_op jit(solution)/shard_map/ppermute | solution.py:49
  56.2 42.0 %collective-permute-done.5 = bf16[4,5,48,192]{3,2,1,0:T(8,128)(2,1)S(1)} collective-permute-done((bf16[4,5,48,192]{3,2,1,0:T(8,128)(2,1)S(1)}, bf16[4,5,48,192]{3,2,1,0:T(8,128)(2,1)S(1)}, u32[]{:S(2)}, u32[]{:S(2)}) %collective-permute-start.5) | collective-permute-done | bytes 368672 | tf_op jit(solution)/shard_map/ppermute | solution.py:49
  104.5 64.9 %all-gather.2.cloned.1.call-done = bf16[5,768,192]{2,1,0:T(8,128)(2,1)} async-done(((bf16[5,48,192]{2,1,0:T(8,128)(2,1)}), bf16[5,768,192]{2,1,0:T(8,128)(2,1)}) %all-gather.2.cloned.1.call-update) | async-done | bytes 1474576 | tf_op jit(solution)/shard_map/all_gather | solution.py:158
  169.4 4.4 pad_maximum_fusion.1
  173.8 2.7 collective-permute-start.8
  179.6 2.4 collective-permute-start.1
  189.5 7.6 %dot_general.78 = bf16[128,4,3840]{2,1,0:T(4,128)(2,1)} reshape(bf16[512,3840]{1,0:T(8,128)(2,1)} %fusion.64) | data formatting | bytes 7864320 | tf_op jit(solution)/shard_map/dot_general | solution.py:128
  197.1 5.0 %fusion.14 = f32[512,384]{1,0:T(8,128)S(1)} fusion(bf16[512,3840]{1,0:T(8,128)(2,1)} %fusion.64, bf16[3840,192]{1,0:T(8,128)(2,1)S(1)} %bitcast.130, bf16[3840,192]{1,0:T(8,128)(2,1)} %bitcast.135), kind=kOutput, calls=%fused_computation.30 | convolution fusion | flops 1515847680 | bytes 7667712 | tf_op jit(solution)/shard_map/dot_general | solution.py:128
  202.4 5.3 %fusion.12 = f32[128,4,384]{2,0,1:T(8,128)S(1)} fusion(bf16[3840,384,1]{1,0,2:T(8,128)(2,1)} %bitcast.17, bf16[128,4,3840]{2,1,0:T(4,128)(2,1)} %dot_general.78), kind=kOutput, calls=%fused_computation.28 | convolution fusion | flops 1509949440 | bytes 7667712 | tf_op jit(solution)/shard_map/dot_general | solution.py:128
  210.7 7.5 %collective-permute-start.9 = (bf16[128,640]{1,0:T(8,128)(2,1)S(1)}, bf16[128,640]{1,0:T(8,128)(2,1)S(1)}, u32[]{:S(2)}, u32[]{:S(2)}) collective-permute-start(bf16[128,640]{1,0:T(8,128)(2,1)S(1)} %get-tuple-element.34), channel_id=1, source_target_pairs={{2,0},{3,1},{4,2},{5,3},{6,4},{7,5},{0,6},{1,7},{10,8},{11,9},{12,... | collective-permute-start | bytes 491528 | tf_op jit(solution)/shard_map/ppermute | solution.py:49
  220.1 2.2 collective-permute-start.11
  222.3 10.7 %collective-permute-done.10 = bf16[128,640]{1,0:T(8,128)(2,1)S(1)} collective-permute-done((bf16[128,640]{1,0:T(8,128)(2,1)S(1)}, bf16[128,640]{1,0:T(8,128)(2,1)S(1)}, u32[]{:S(2)}, u32[]{:S(2)}) %collective-permute-start.10) | collective-permute-done | bytes 163872 | tf_op jit(solution)/shard_map/ppermute | solution.py:49
  235.1 3.2 collective-permute-start.13
  238.3 2.8 collective-permute-start.14
  241.0 9.9 %collective-permute-done.12 = bf16[4,128,640]{2,1,0:T(8,128)(2,1)S(1)} collective-permute-done((bf16[4,128,640]{2,1,0:T(8,128)(2,1)S(1)}, bf16[4,128,640]{2,1,0:T(8,128)(2,1)S(1)}, u32[]{:S(2)}, u32[]{:S(2)}) %collective-permute-start.12) | collective-permute-done | bytes 655392 | tf_op jit(solution)/shard_map/ppermute | solution.py:49
  251.0 2.1 collective-permute-done.13
  253.1 16.1 %collective-permute-done.14 = bf16[4,128,640]{2,1,0:T(8,128)(2,1)S(1)} collective-permute-done((bf16[4,128,640]{2,1,0:T(8,128)(2,1)S(1)}, bf16[4,128,640]{2,1,0:T(8,128)(2,1)S(1)}, u32[]{:S(2)}, u32[]{:S(2)}) %collective-permute-start.14) | collective-permute-done | bytes 655392 | tf_op jit(solution)/shard_map/ppermute | solution.py:49
  270.9 2.6 collective-permute-start.15
  284.8 2.3 pad_maximum_fusion
  294.4 3.7 fusion.25
  298.1 3.5 fusion.26
  301.7 3.4 fusion.27
  305.2 3.0 multiply_reduce_fusion.4
  311.6 2.8 pad_maximum_fusion.4
  314.3 2.2 reshape.367
  318.6 2.6 collective-permute-done.16
  322.7 3.0 collective-permute-start.17
  325.7 2.7 collective-permute-start.18
  328.5 2.1 collective-permute-start.19
  332.0 4.3 collective-permute-done.18
  336.3 6.0 %collective-permute-done.19 = f32[4,15360]{1,0:T(4,128)S(1)} collective-permute-done((f32[4,15360]{1,0:T(4,128)S(1)}, f32[4,15360]{1,0:T(4,128)S(1)}, u32[]{:S(2)}, u32[]{:S(2)}) %collective-permute-start.19) | collective-permute-done | bytes 245792 | tf_op jit(solution)/shard_map/ppermute | solution.py:49
  342.6 2.2 collective-permute-start.20
  344.9 2.9 collective-permute-start.21
  347.7 2.4 collective-permute-start.22
  351.3 2.6 collective-permute-done.22
  355.8 3.8 collective-permute-start.24
  359.6 3.4 collective-permute-start.25
  363.0 3.4 collective-permute-done.25
  367.5 6.3 %collective-permute-start.26 = (f32[15360]{0:T(1024)S(1)}, f32[15360]{0:T(1024)S(1)}, u32[]{:S(2)}, u32[]{:S(2)}) collective-permute-start(f32[15360]{0:T(1024)S(1)} %bitcast.149), channel_id=1, source_target_pairs={{128,0},{160,32},{192,64},{224,96},{256,128},{288,160},{320,192},{... | collective-permute-start | bytes 184328 | tf_op jit(solution)/shard_map/ppermute | solution.py:49
  373.9 5.7 %collective-permute-start.27 = (f32[15360]{0:T(1024)S(1)}, f32[15360]{0:T(1024)S(1)}, u32[]{:S(2)}, u32[]{:S(2)}) collective-permute-start(f32[15360]{0:T(1024)S(1)} %bitcast.150), channel_id=1, source_target_pairs={{256,0},{288,32},{320,64},{352,96},{384,128},{416,160},{448,192},{... | collective-permute-start | bytes 184328 | tf_op jit(solution)/shard_map/ppermute | solution.py:49
  379.6 3.9 collective-permute-start.28
  383.5 4.9 %collective-permute-done.27 = f32[15360]{0:T(1024)S(1)} collective-permute-done((f32[15360]{0:T(1024)S(1)}, f32[15360]{0:T(1024)S(1)}, u32[]{:S(2)}, u32[]{:S(2)}) %collective-permute-start.27) | collective-permute-done | bytes 61472 | tf_op jit(solution)/shard_map/ppermute | solution.py:49
  388.4 2.5 collective-permute-done.28
  392.0 3.7 collective-permute-start.29
  395.7 3.5 collective-permute-start.30
  402.2 3.2 collective-permute-done.31
  408.4 3.3 collective-permute-start.33
  411.7 2.8 collective-permute-start.34
  414.5 2.3 collective-permute-done.33
  416.8 4.1 collective-permute-done.34
  422.3 7.5 %collective-permute-start.35 = (f32[4,4,15360]{2,1,0:T(4,128)S(1)}, f32[4,4,15360]{2,1,0:T(4,128)S(1)}, u32[]{:S(2)}, u32[]{:S(2)}) collective-permute-start(f32[4,4,15360]{2,1,0:T(4,128)S(1)} %gather_fusion.5), channel_id=1, source_target_pairs={{1,0},{0,1},{3,2},{2,3},{5,4},{4,5},{7,6},{6,7},{9,8},{8,9},{11,10... | collective-permute-start | bytes 2949128 | tf_op jit(solution)/shard_map/ppermute | solution.py:49
  433.8 3.3 gather_fusion.6
  437.0 2.3 slice.200
  439.3 2.3 slice.198
  441.6 2.4 slice.255
  444.0 2.1 slice.254
  (171 shorter events, 69.0 us)
Async XLA Ops:
  7.2 269.5 %copy-start = (bf16[384,768]{1,0:T(8,128)(2,1)S(1)}, bf16[384,768]{1,0:T(8,128)(2,1)}, u32[]{:S(2)}) copy-start(bf16[384,768]{1,0:T(8,128)(2,1)} %param.13) | copy-start | bytes 1769476
  7.2 162.2 %all-gather.2.cloned.1.call-start = ((), (), s32[]{:S(2)}) async-start(), calls=%async_computation | async-start | bytes 2088960 | tf_op jit(solution)/shard_map/all_gather | solution.py:158
  9.1 10.2 %collective-permute-start.2 = (bf16[5,48,192]{2,1,0:T(8,128)(2,1)S(1)}, bf16[5,48,192]{2,1,0:T(8,128)(2,1)S(1)}, u32[]{:S(2)}, u32[]{:S(2)}) collective-permute-start(bf16[5,48,192]{2,1,0:T(8,128)(2,1)S(1)} %get-tuple-element.24), channel_id=1, source_target_pairs={{32,0},{64,32},{96,64},{0,96},{160,128},{192,160},{224,192},{128,2... | collective-permute-start | bytes 276488 | tf_op jit(solution)/shard_map/ppermute | solution.py:49
  14.3 7.1 %collective-permute-start.3 = (bf16[5,48,192]{2,1,0:T(8,128)(2,1)S(1)}, bf16[5,48,192]{2,1,0:T(8,128)(2,1)S(1)}, u32[]{:S(2)}, u32[]{:S(2)}) collective-permute-start(bf16[5,48,192]{2,1,0:T(8,128)(2,1)S(1)} %get-tuple-element.24), channel_id=1, source_target_pairs={{64,0},{96,32},{0,64},{32,96},{192,128},{224,160},{128,192},{160,2... | collective-permute-start | bytes 276488 | tf_op jit(solution)/shard_map/ppermute | solution.py:49
  16.8 6.8 %collective-permute-start.4 = (bf16[5,48,192]{2,1,0:T(8,128)(2,1)S(1)}, bf16[5,48,192]{2,1,0:T(8,128)(2,1)S(1)}, u32[]{:S(2)}, u32[]{:S(2)}) collective-permute-start(bf16[5,48,192]{2,1,0:T(8,128)(2,1)S(1)} %get-tuple-element.24), channel_id=1, source_target_pairs={{96,0},{0,32},{32,64},{64,96},{224,128},{128,160},{160,192},{192,2... | collective-permute-start | bytes 276488 | tf_op jit(solution)/shard_map/ppermute | solution.py:49
  24.3 31.9 %collective-permute-start.7 = (bf16[4,5,48,192]{3,2,1,0:T(8,128)(2,1)S(1)}, bf16[4,5,48,192]{3,2,1,0:T(8,128)(2,1)S(1)}, u32[]{:S(2)}, u32[]{:S(2)}) collective-permute-start(bf16[4,5,48,192]{3,2,1,0:T(8,128)(2,1)S(1)} %gather_fusion), channel_id=1, source_target_pairs={{384,0},{416,32},{448,64},{480,96},{0,128},{32,160},{64,192},{96,2... | collective-permute-start | bytes 1105928 | tf_op jit(solution)/shard_map/ppermute | solution.py:49
  34.5 63.7 %collective-permute-start.5 = (bf16[4,5,48,192]{3,2,1,0:T(8,128)(2,1)S(1)}, bf16[4,5,48,192]{3,2,1,0:T(8,128)(2,1)S(1)}, u32[]{:S(2)}, u32[]{:S(2)}) collective-permute-start(bf16[4,5,48,192]{3,2,1,0:T(8,128)(2,1)S(1)} %gather_fusion), channel_id=1, source_target_pairs={{128,0},{160,32},{192,64},{224,96},{256,128},{288,160},{320,192},{... | collective-permute-start | bytes 1105928 | tf_op jit(solution)/shard_map/ppermute | solution.py:49
  40.0 58.2 %collective-permute-start.6 = (bf16[4,5,48,192]{3,2,1,0:T(8,128)(2,1)S(1)}, bf16[4,5,48,192]{3,2,1,0:T(8,128)(2,1)S(1)}, u32[]{:S(2)}, u32[]{:S(2)}) collective-permute-start(bf16[4,5,48,192]{3,2,1,0:T(8,128)(2,1)S(1)} %gather_fusion), channel_id=1, source_target_pairs={{256,0},{288,32},{320,64},{352,96},{384,128},{416,160},{448,192},{... | collective-permute-start | bytes 1105928 | tf_op jit(solution)/shard_map/ppermute | solution.py:49
  98.2 0.9 copy-start.13
  104.5 69.3 %copy-start.3 = (bf16[16,5,48,192]{3,2,0,1:T(8,128)(2,1)}, bf16[16,5,48,192]{3,2,0,1:T(8,128)(2,1)S(1)}, u32[]{:S(2)}) copy-start(bf16[16,5,48,192]{3,2,0,1:T(8,128)(2,1)S(1)} %copy.20) | copy-start | bytes 4423684
  169.4 7.1 %copy-start.1 = (bf16[1,512,768]{2,1,0:T(8,128)(2,1)S(1)}, bf16[1,512,768]{2,1,0:T(8,128)(2,1)}, u32[]{:S(2)}) copy-start(bf16[1,512,768]{2,1,0:T(8,128)(2,1)} %param.8) | copy-start | bytes 2359300
  173.8 28.6 %collective-permute-start.8 = (bf16[5,768,384]{2,1,0:T(8,128)(2,1)}, bf16[5,768,384]{2,1,0:T(8,128)(2,1)}, u32[]{:S(2)}, u32[]{:S(2)}) collective-permute-start(bf16[5,768,384]{2,1,0:T(8,128)(2,1)} %pad_maximum_fusion.1), channel_id=1, source_target_pairs={{1,0},{0,1},{3,2},{2,3},{5,4},{4,5},{7,6},{6,7},{9,8},{8,9},{11,10... | collective-permute-start | bytes 8847368 | tf_op jit(solution)/shard_map/ppermute | solution.py:49
  177.7 5.9 %collective-permute-start = (bf16[2,768]{1,0:T(2,128)(2,1)S(1)}, bf16[2,768]{1,0:T(2,128)(2,1)S(1)}, u32[]{:S(2)}, u32[]{:S(2)}) collective-permute-start(bf16[2,768]{1,0:T(2,128)(2,1)S(1)} %get-tuple-element.20), channel_id=1, source_target_pairs={{0,1},{1,2},{2,3},{3,4},{4,5},{5,6},{6,7},{7,8},{8,9},{9,10},{10,1... | collective-permute-start | bytes 9224 | tf_op jit(solution)/shard_map/ppermute | solution.py:20
  179.6 7.7 %collective-permute-start.1 = (bf16[2,768]{1,0:T(2,128)(2,1)S(1)}, bf16[2,768]{1,0:T(2,128)(2,1)S(1)}, u32[]{:S(2)}, u32[]{:S(2)}) collective-permute-start(bf16[2,768]{1,0:T(2,128)(2,1)S(1)} %get-tuple-element.19), channel_id=1, source_target_pairs={{1,0},{2,1},{3,2},{4,3},{5,4},{6,5},{7,6},{8,7},{9,8},{10,9},{11,1... | collective-permute-start | bytes 9224 | tf_op jit(solution)/shard_map/ppermute | solution.py:21
  189.5 7.6 %copy-start.4 = (bf16[16,5,48,192]{3,2,0,1:T(8,128)(2,1)S(1)}, bf16[16,5,48,192]{3,2,0,1:T(8,128)(2,1)}, u32[]{:S(2)}) copy-start(bf16[16,5,48,192]{3,2,0,1:T(8,128)(2,1)} %copy-done.3) | copy-start | bytes 4423684
  202.4 5.3 %copy-start.6 = (f32[128,4,768]{2,1,0:T(4,128)S(1)}, f32[128,4,768]{2,1,0:T(4,128)}, u32[]{:S(2)}) copy-start(f32[128,4,768]{2,1,0:T(4,128)} %reshape.368) | copy-start | bytes 4718596
  207.7 1.0 copy-start.14
  208.3 101.2 %copy-start.5 = (bf16[128,768]{1,0:T(8,128)(2,1)}, bf16[128,768]{1,0:T(8,128)(2,1)S(1)}, u32[]{:S(2)}) copy-start(bf16[128,768]{1,0:T(8,128)(2,1)S(1)} %fusion.19) | copy-start | bytes 589828
  210.7 11.6 %collective-permute-start.9 = (bf16[128,640]{1,0:T(8,128)(2,1)S(1)}, bf16[128,640]{1,0:T(8,128)(2,1)S(1)}, u32[]{:S(2)}, u32[]{:S(2)}) collective-permute-start(bf16[128,640]{1,0:T(8,128)(2,1)S(1)} %get-tuple-element.34), channel_id=1, source_target_pairs={{2,0},{3,1},{4,2},{5,3},{6,4},{7,5},{0,6},{1,7},{10,8},{11,9},{12,... | collective-permute-start | bytes 491528 | tf_op jit(solution)/shard_map/ppermute | solution.py:49
  218.2 14.9 %collective-permute-start.10 = (bf16[128,640]{1,0:T(8,128)(2,1)S(1)}, bf16[128,640]{1,0:T(8,128)(2,1)S(1)}, u32[]{:S(2)}, u32[]{:S(2)}) collective-permute-start(bf16[128,640]{1,0:T(8,128)(2,1)S(1)} %get-tuple-element.34), channel_id=1, source_target_pairs={{4,0},{5,1},{6,2},{7,3},{0,4},{1,5},{2,6},{3,7},{12,8},{13,9},{14,... | collective-permute-start | bytes 491528 | tf_op jit(solution)/shard_map/ppermute | solution.py:49
  220.1 12.9 %collective-permute-start.11 = (bf16[128,640]{1,0:T(8,128)(2,1)S(1)}, bf16[128,640]{1,0:T(8,128)(2,1)S(1)}, u32[]{:S(2)}, u32[]{:S(2)}) collective-permute-start(bf16[128,640]{1,0:T(8,128)(2,1)S(1)} %get-tuple-element.34), channel_id=1, source_target_pairs={{6,0},{7,1},{0,2},{1,3},{2,4},{3,5},{4,6},{5,7},{14,8},{15,9},{8,1... | collective-permute-start | bytes 491528 | tf_op jit(solution)/shard_map/ppermute | solution.py:49
  233.2 17.8 %collective-permute-start.12 = (bf16[4,128,640]{2,1,0:T(8,128)(2,1)S(1)}, bf16[4,128,640]{2,1,0:T(8,128)(2,1)S(1)}, u32[]{:S(2)}, u32[]{:S(2)}) collective-permute-start(bf16[4,128,640]{2,1,0:T(8,128)(2,1)S(1)} %get-tuple-element.22), channel_id=1, source_target_pairs={{8,0},{9,1},{10,2},{11,3},{12,4},{13,5},{14,6},{15,7},{16,8},{17,9... | collective-permute-start | bytes 1966088 | tf_op jit(solution)/shard_map/ppermute | solution.py:49
  235.1 18.0 %collective-permute-start.13 = (bf16[4,128,640]{2,1,0:T(8,128)(2,1)S(1)}, bf16[4,128,640]{2,1,0:T(8,128)(2,1)S(1)}, u32[]{:S(2)}, u32[]{:S(2)}) collective-permute-start(bf16[4,128,640]{2,1,0:T(8,128)(2,1)S(1)} %get-tuple-element.22), channel_id=1, source_target_pairs={{16,0},{17,1},{18,2},{19,3},{20,4},{21,5},{22,6},{23,7},{24,8},{25... | collective-permute-start | bytes 1966088 | tf_op jit(solution)/shard_map/ppermute | solution.py:49
  238.3 30.9 %collective-permute-start.14 = (bf16[4,128,640]{2,1,0:T(8,128)(2,1)S(1)}, bf16[4,128,640]{2,1,0:T(8,128)(2,1)S(1)}, u32[]{:S(2)}, u32[]{:S(2)}) collective-permute-start(bf16[4,128,640]{2,1,0:T(8,128)(2,1)S(1)} %get-tuple-element.22), channel_id=1, source_target_pairs={{24,0},{25,1},{26,2},{27,3},{28,4},{29,5},{30,6},{31,7},{0,8},{1,9... | collective-permute-start | bytes 1966088 | tf_op jit(solution)/shard_map/ppermute | solution.py:49
  269.2 4.3 copy-start.27
  270.9 13.9 %collective-permute-start.15 = (bf16[4,4,128,640]{3,2,1,0:T(8,128)(2,1)}, bf16[4,4,128,640]{3,2,1,0:T(8,128)(2,1)}, u32[]{:S(2)}, u32[]{:S(2)}) collective-permute-start(bf16[4,4,128,640]{3,2,1,0:T(8,128)(2,1)} %get-tuple-element.15), channel_id=1, source_target_pairs={{1,0},{0,1},{3,2},{2,3},{5,4},{4,5},{7,6},{6,7},{9,8},{8,9},{11,10... | collective-permute-start | bytes 7864328 | tf_op jit(solution)/shard_map/ppermute | solution.py:49
  287.1 6.1 %copy-start.2 = (bf16[2,4,4,128,640]{4,3,2,1,0:T(8,128)(2,1)}, bf16[2,4,4,128,640]{4,3,2,1,0:T(8,128)(2,1)S(1)}, u32[]{:S(2)}) copy-start(bf16[2,4,4,128,640]{4,3,2,1,0:T(8,128)(2,1)S(1)} %pad_maximum_fusion) | copy-start | bytes 15728644
  288.3 1.7 copy-start.7
  288.9 2.2 copy-start.8
  289.5 2.6 copy-start.9
  292.1 1.1 copy-start.15
  294.4 16.8 %copy-start.16 = (bf16[128,96]{0,1:T(8,128)(2,1)}, bf16[128,96]{0,1:T(8,128)(2,1)S(1)}, u32[]{:S(2)}) copy-start(bf16[128,96]{0,1:T(8,128)(2,1)S(1)} %get-tuple-element.35) | copy-start | bytes 73732
  294.4 16.8 %copy-start.18 = (bf16[128,96]{0,1:T(8,128)(2,1)}, bf16[128,96]{0,1:T(8,128)(2,1)S(1)}, u32[]{:S(2)}) copy-start(bf16[128,96]{0,1:T(8,128)(2,1)S(1)} %get-tuple-element.36) | copy-start | bytes 73732
  298.1 7.0 %copy-start.24 = (f32[128,64]{1,0:T(8,128)}, f32[128,64]{1,0:T(8,128)S(1)}, u32[]{:S(2)}) copy-start(f32[128,64]{1,0:T(8,128)S(1)} %fusion.25) | copy-start | bytes 98308
  301.7 3.5 copy-start.25
  301.7 3.5 copy-start.10
  305.1 3.1 copy-start.26
  308.2 2.9 copy-start.11
  308.2 2.9 copy-start.20
  308.2 2.9 copy-start.22
  316.6 4.6 %collective-permute-start.16 = (f32[4,4,15360]{2,1,0:T(4,128)S(1)}, f32[4,4,15360]{2,1,0:T(4,128)}, u32[]{:S(2)}, u32[]{:S(2)}) collective-permute-start(f32[4,4,15360]{2,1,0:T(4,128)S(1)} %dynamic-slice_bitcast_fusion), channel_id=1, source_target_pairs={{1,0},{0,1},{3,2},{2,3},{5,4},{4,5},{7,6},{6,7},{9,8},{8,9},{11,10... | collective-permute-start | bytes 2949128 | tf_op jit(solution)/shard_map/ppermute | solution.py:49
  322.7 9.3 %collective-permute-start.17 = (f32[4,15360]{1,0:T(4,128)S(1)}, f32[4,15360]{1,0:T(4,128)S(1)}, u32[]{:S(2)}, u32[]{:S(2)}) collective-permute-start(f32[4,15360]{1,0:T(4,128)S(1)} %get-tuple-element.16), channel_id=1, source_target_pairs={{32,0},{64,32},{96,64},{0,96},{160,128},{192,160},{224,192},{128,2... | collective-permute-start | bytes 737288 | tf_op jit(solution)/shard_map/ppermute | solution.py:49
  325.7 10.5 %collective-permute-start.18 = (f32[4,15360]{1,0:T(4,128)S(1)}, f32[4,15360]{1,0:T(4,128)S(1)}, u32[]{:S(2)}, u32[]{:S(2)}) collective-permute-start(f32[4,15360]{1,0:T(4,128)S(1)} %get-tuple-element.18), channel_id=1, source_target_pairs={{64,0},{96,32},{0,64},{32,96},{192,128},{224,160},{128,192},{160,2... | collective-permute-start | bytes 737288 | tf_op jit(solution)/shard_map/ppermute | solution.py:49
  328.5 13.8 %collective-permute-start.19 = (f32[4,15360]{1,0:T(4,128)S(1)}, f32[4,15360]{1,0:T(4,128)S(1)}, u32[]{:S(2)}, u32[]{:S(2)}) collective-permute-start(f32[4,15360]{1,0:T(4,128)S(1)} %get-tuple-element.17), channel_id=1, source_target_pairs={{96,0},{0,32},{32,64},{64,96},{224,128},{128,160},{160,192},{192,2... | collective-permute-start | bytes 737288 | tf_op jit(solution)/shard_map/ppermute | solution.py:49
  342.6 7.6 %collective-permute-start.20 = (f32[15360]{0:T(1024)S(1)}, f32[15360]{0:T(1024)S(1)}, u32[]{:S(2)}, u32[]{:S(2)}) collective-permute-start(f32[15360]{0:T(1024)S(1)} %bitcast.166), channel_id=1, source_target_pairs={{8,0},{9,1},{10,2},{11,3},{12,4},{13,5},{14,6},{15,7},{16,8},{17,9... | collective-permute-start | bytes 184328 | tf_op jit(solution)/shard_map/ppermute | solution.py:49
  344.9 6.5 %collective-permute-start.21 = (f32[15360]{0:T(1024)S(1)}, f32[15360]{0:T(1024)S(1)}, u32[]{:S(2)}, u32[]{:S(2)}) collective-permute-start(f32[15360]{0:T(1024)S(1)} %bitcast.165), channel_id=1, source_target_pairs={{16,0},{17,1},{18,2},{19,3},{20,4},{21,5},{22,6},{23,7},{24,8},{25... | collective-permute-start | bytes 184328 | tf_op jit(solution)/shard_map/ppermute | solution.py:49
  347.7 6.2 %collective-permute-start.22 = (f32[15360]{0:T(1024)S(1)}, f32[15360]{0:T(1024)S(1)}, u32[]{:S(2)}, u32[]{:S(2)}) collective-permute-start(f32[15360]{0:T(1024)S(1)} %bitcast.164), channel_id=1, source_target_pairs={{24,0},{25,1},{26,2},{27,3},{28,4},{29,5},{30,6},{31,7},{0,8},{1,9... | collective-permute-start | bytes 184328 | tf_op jit(solution)/shard_map/ppermute | solution.py:49
  353.9 9.1 %collective-permute-start.23 = (f32[15360]{0:T(1024)S(1)}, f32[15360]{0:T(1024)S(1)}, u32[]{:S(2)}, u32[]{:S(2)}) collective-permute-start(f32[15360]{0:T(1024)S(1)} %add_add_fusion), channel_id=1, source_target_pairs={{2,0},{3,1},{4,2},{5,3},{6,4},{7,5},{0,6},{1,7},{10,8},{11,9},{12,... | collective-permute-start | bytes 184328 | tf_op jit(solution)/shard_map/ppermute | solution.py:49
  355.8 7.2 %collective-permute-start.24 = (f32[15360]{0:T(1024)S(1)}, f32[15360]{0:T(1024)S(1)}, u32[]{:S(2)}, u32[]{:S(2)}) collective-permute-start(f32[15360]{0:T(1024)S(1)} %add_add_fusion), channel_id=1, source_target_pairs={{4,0},{5,1},{6,2},{7,3},{0,4},{1,5},{2,6},{3,7},{12,8},{13,9},{14,... | collective-permute-start | bytes 184328 | tf_op jit(solution)/shard_map/ppermute | solution.py:49
  359.6 6.8 %collective-permute-start.25 = (f32[15360]{0:T(1024)S(1)}, f32[15360]{0:T(1024)S(1)}, u32[]{:S(2)}, u32[]{:S(2)}) collective-permute-start(f32[15360]{0:T(1024)S(1)} %add_add_fusion), channel_id=1, source_target_pairs={{6,0},{7,1},{0,2},{1,3},{2,4},{3,5},{4,6},{5,7},{14,8},{15,9},{8,1... | collective-permute-start | bytes 184328 | tf_op jit(solution)/shard_map/ppermute | solution.py:49
  367.5 16.0 %collective-permute-start.26 = (f32[15360]{0:T(1024)S(1)}, f32[15360]{0:T(1024)S(1)}, u32[]{:S(2)}, u32[]{:S(2)}) collective-permute-start(f32[15360]{0:T(1024)S(1)} %bitcast.149), channel_id=1, source_target_pairs={{128,0},{160,32},{192,64},{224,96},{256,128},{288,160},{320,192},{... | collective-permute-start | bytes 184328 | tf_op jit(solution)/shard_map/ppermute | solution.py:49
  373.9 14.5 %collective-permute-start.27 = (f32[15360]{0:T(1024)S(1)}, f32[15360]{0:T(1024)S(1)}, u32[]{:S(2)}, u32[]{:S(2)}) collective-permute-start(f32[15360]{0:T(1024)S(1)} %bitcast.150), channel_id=1, source_target_pairs={{256,0},{288,32},{320,64},{352,96},{384,128},{416,160},{448,192},{... | collective-permute-start | bytes 184328 | tf_op jit(solution)/shard_map/ppermute | solution.py:49
  379.6 11.3 %collective-permute-start.28 = (f32[15360]{0:T(1024)S(1)}, f32[15360]{0:T(1024)S(1)}, u32[]{:S(2)}, u32[]{:S(2)}) collective-permute-start(f32[15360]{0:T(1024)S(1)} %bitcast.151), channel_id=1, source_target_pairs={{384,0},{416,32},{448,64},{480,96},{0,128},{32,160},{64,192},{96,2... | collective-permute-start | bytes 184328 | tf_op jit(solution)/shard_map/ppermute | solution.py:49
  392.0 9.2 %collective-permute-start.29 = (f32[15360]{0:T(1024)S(1)}, f32[15360]{0:T(1024)S(1)}, u32[]{:S(2)}, u32[]{:S(2)}) collective-permute-start(f32[15360]{0:T(1024)S(1)} %bitcast.152), channel_id=1, source_target_pairs={{8,0},{9,1},{10,2},{11,3},{12,4},{13,5},{14,6},{15,7},{16,8},{17,9... | collective-permute-start | bytes 184328 | tf_op jit(solution)/shard_map/ppermute | solution.py:49
  395.7 6.5 %collective-permute-start.30 = (f32[15360]{0:T(1024)S(1)}, f32[15360]{0:T(1024)S(1)}, u32[]{:S(2)}, u32[]{:S(2)}) collective-permute-start(f32[15360]{0:T(1024)S(1)} %bitcast.153), channel_id=1, source_target_pairs={{16,0},{17,1},{18,2},{19,3},{20,4},{21,5},{22,6},{23,7},{24,8},{25... | collective-permute-start | bytes 184328 | tf_op jit(solution)/shard_map/ppermute | solution.py:49
  399.2 6.2 %collective-permute-start.31 = (f32[15360]{0:T(1024)S(1)}, f32[15360]{0:T(1024)S(1)}, u32[]{:S(2)}, u32[]{:S(2)}) collective-permute-start(f32[15360]{0:T(1024)S(1)} %bitcast.154), channel_id=1, source_target_pairs={{24,0},{25,1},{26,2},{27,3},{28,4},{29,5},{30,6},{31,7},{0,8},{1,9... | collective-permute-start | bytes 184328 | tf_op jit(solution)/shard_map/ppermute | solution.py:49
  406.3 23.6 %copy-start.17 = (bf16[128,96]{0,1:T(8,128)(2,1)S(1)}, bf16[128,96]{0,1:T(8,128)(2,1)}, u32[]{:S(2)}) copy-start(bf16[128,96]{0,1:T(8,128)(2,1)} %copy-done.16) | copy-start | bytes 73732
  406.3 23.6 %copy-start.19 = (bf16[128,96]{0,1:T(8,128)(2,1)S(1)}, bf16[128,96]{0,1:T(8,128)(2,1)}, u32[]{:S(2)}) copy-start(bf16[128,96]{0,1:T(8,128)(2,1)} %copy-done.18) | copy-start | bytes 73732
  406.3 23.6 %copy-start.21 = (bf16[128,96]{0,1:T(8,128)(2,1)S(1)}, bf16[128,96]{0,1:T(8,128)(2,1)}, u32[]{:S(2)}) copy-start(bf16[128,96]{0,1:T(8,128)(2,1)} %get-tuple-element.37) | copy-start | bytes 73732
  406.3 23.6 %copy-start.23 = (bf16[128,96]{0,1:T(8,128)(2,1)S(1)}, bf16[128,96]{0,1:T(8,128)(2,1)}, u32[]{:S(2)}) copy-start(bf16[128,96]{0,1:T(8,128)(2,1)} %get-tuple-element.38) | copy-start | bytes 73732
  406.3 8.2 %collective-permute-start.32 = (f32[4,15360]{1,0:T(4,128)S(1)}, f32[4,15360]{1,0:T(4,128)S(1)}, u32[]{:S(2)}, u32[]{:S(2)}) collective-permute-start(f32[4,15360]{1,0:T(4,128)S(1)} %gather_fusion.4), channel_id=1, source_target_pairs={{32,0},{64,32},{96,64},{0,96},{160,128},{192,160},{224,192},{128,2... | collective-permute-start | bytes 737288 | tf_op jit(solution)/shard_map/ppermute | solution.py:49
  408.4 8.4 %collective-permute-start.33 = (f32[4,15360]{1,0:T(4,128)S(1)}, f32[4,15360]{1,0:T(4,128)S(1)}, u32[]{:S(2)}, u32[]{:S(2)}) collective-permute-start(f32[4,15360]{1,0:T(4,128)S(1)} %gather_fusion.4), channel_id=1, source_target_pairs={{64,0},{96,32},{0,64},{32,96},{192,128},{224,160},{128,192},{160,2... | collective-permute-start | bytes 737288 | tf_op jit(solution)/shard_map/ppermute | solution.py:49
  411.7 9.2 %collective-permute-start.34 = (f32[4,15360]{1,0:T(4,128)S(1)}, f32[4,15360]{1,0:T(4,128)S(1)}, u32[]{:S(2)}, u32[]{:S(2)}) collective-permute-start(f32[4,15360]{1,0:T(4,128)S(1)} %gather_fusion.4), channel_id=1, source_target_pairs={{96,0},{0,32},{32,64},{64,96},{224,128},{128,160},{160,192},{192,2... | collective-permute-start | bytes 737288 | tf_op jit(solution)/shard_map/ppermute | solution.py:49
  422.3 9.7 %collective-permute-start.35 = (f32[4,4,15360]{2,1,0:T(4,128)S(1)}, f32[4,4,15360]{2,1,0:T(4,128)S(1)}, u32[]{:S(2)}, u32[]{:S(2)}) collective-permute-start(f32[4,4,15360]{2,1,0:T(4,128)S(1)} %gather_fusion.5), channel_id=1, source_target_pairs={{1,0},{0,1},{3,2},{2,3},{5,4},{4,5},{7,6},{6,7},{9,8},{8,9},{11,10... | collective-permute-start | bytes 2949128 | tf_op jit(solution)/shard_map/ppermute | solution.py:49
  (1 other events, 0.8 us)
Sparse Core Ops, SparseCore 0:
  11.6 157.7 all-gather.1

commit v5 on v3

--- a/solution.py
+++ b/solution.py
@@ -64,7 +64,7 @@
     stacked = jnp.stack([array] + [shift(array, dim, step) for step in range(1, size)])
     if ordered:
         slots = (jnp.arange(size) - coord(dim)) % size
-        stacked = jnp.take(stacked, slots, axis=0)
+        stacked = jnp.take(stacked, slots, axis=0, mode="clip")
     return stacked
 
 
@@ -119,11 +119,14 @@
     )
 
 
-def stacked_conv(padded, all_taps, length_fine):
+def conv_windows(padded, tap_count, length_fine):
+    return jnp.concatenate(
+        [padded[tap_index : tap_index + length_fine] for tap_index in range(tap_count)], axis=1
+    )
+
+
+def stacked_conv(windows, all_taps):
     tap_count = all_taps.shape[0]
-    windows = jnp.concatenate(
-        [padded[tap_index : tap_index + length_fine] for tap_index in range(tap_count)], axis=1
-    )
     flat_taps = all_taps.reshape(tap_count * all_taps.shape[1], all_taps.shape[2])
     return jnp.dot(windows, flat_taps, preferred_element_type=jnp.float32)
 
@@ -147,15 +150,16 @@
     attender_total = logit_multipliers.shape[0]
     probe_extent = asking_projector.shape[1] // attender_total
     value_width = content_projector.shape[1] // attender_total
-    activated = activate(layer_norm(incoming_tensor.astype(jnp.float32))).astype(jnp.bfloat16)
-    padded = padded_2(activated, (("seq", 0),), margin)
+    raw_padded = padded_2(incoming_tensor, (("seq", 0),), margin)
+    padded = activate(layer_norm(raw_padded.astype(jnp.float32))).astype(jnp.bfloat16)
+    windows = conv_windows(padded, tap_count, length_fine)
     core = coord("core")
     half_width = kernel_coefficients.shape[2] // 2
     own_half = lax.dynamic_slice_in_dim(kernel_coefficients, core * half_width, half_width, axis=2)
     own_taps = lax.all_gather(own_half, "dp", axis=1, tiled=True)
     other_taps = shift(own_taps, "core", 1)
-    conv_own = stacked_conv(padded, own_taps, length_fine)
-    conv_other = stacked_conv(padded, other_taps, length_fine)
+    conv_own = stacked_conv(windows, own_taps)
+    conv_other = stacked_conv(windows, other_taps)
     conv_sum = jnp.where(
         core == 0,
         jnp.concatenate([conv_own, conv_other], axis=1),

time: 411 us -> 400 us (0.973)
  other arithmetic: 27.2 us -> 16.9 us
  local copies, waits for them, and re-layouts: 34 us -> 40.5 us
  waiting for transfers between devices: 193 us -> 188 us
    all_gather x1, waiting for transfers between devices: 118 us -> 105 us  [on_device(): own_taps = lax.all_gather(own_half, 'dp', axis=1, tiled=True)]
    ppermute x28, starting transfers between devices: 98 us -> 88.4 us  [shift(): return lax.ppermute(array, axis, pairs)]
    ppermute x28, waiting for transfers between devices: 75 us -> 82.9 us  [shift(): return lax.ppermute(array, axis, pairs)]
    unnamed x4 -> x0, other arithmetic: 4.85 us -> none
    select_n x2 -> x0, local copies, waits for them, and re-layouts: 4.57 us -> none  [gather_dim(): stacked = jnp.take(stacked, slots, axis=0)]
    unnamed x55, local copies, waits for them, and re-layouts: 1.96 us -> 6.38 us
  transfers between devices with their start and end apart: 31 -> 31, of which waited for: 17 -> 19; matrix products, arithmetic and copies ran while one was open for 8% -> 8% of each run, Pallas kernels for 0% -> 0%
where the time goes in v5:
time: 400 us; the launch traced here: 398 us
  waiting for transfers between devices  188 us (47%)
  starting transfers between devices  98.5 us (25%)
  local copies, waits for them, and re-layouts  40.5 us (10%)
  matrix products  35.9 us (9%)
  between operations  17.8 us (4%)
  other arithmetic  16.9 us (4%)
    all_gather x1, waiting for transfers between devices, on_device(): own_taps = lax.all_gather(own_half, 'dp', axis=1, tiled=True)  105 us
    ppermute x28, starting transfers between devices, shift(): return lax.ppermute(array, axis, pairs)  88.4 us
    ppermute x28, waiting for transfers between devices, shift(): return lax.ppermute(array, axis, pairs)  82.9 us
    dot_general x4, matrix products, on_device(): jnp.dot(score_grad, key_part, preferred_element_type=jnp.float32)  13.7 us
    dot_general x2, matrix products, stacked_conv(): return jnp.dot(windows, flat_taps, preferred_element_type=jnp.float32)  9.36 us
  transfers between devices with their start and end apart: 31, of which 19 were waited for; matrix products, arithmetic and copies ran while one was open for 8% of the time, Pallas kernels for 0%

profile of v5, /device:TPU:1, one launch (start us, length us, event | category | flops | bytes accessed | tf_op | source)
XLA Modules:
  0.0 397.9 jit_solution(7764278953751134092)
XLA Ops:
  9.7 4.9 %collective-permute-start = (bf16[2,768]{1,0:T(2,128)(2,1)S(1)}, bf16[2,768]{1,0:T(2,128)(2,1)S(1)}, u32[]{:S(2)}, u32[]{:S(2)}) collective-permute-start(bf16[2,768]{1,0:T(2,128)(2,1)S(1)} %get-tuple-element.19), channel_id=1, source_target_pairs={{0,1},{1,2},{2,3},{3,4},{4,5},{5,6},{6,7},{7,8},{8,9},{9,10},{10,1... | collective-permute-start | bytes 9224 | tf_op jit(solution)/shard_map/ppermute | solution.py:20
  14.7 5.1 %collective-permute-start.1 = (bf16[2,768]{1,0:T(2,128)(2,1)S(1)}, bf16[2,768]{1,0:T(2,128)(2,1)S(1)}, u32[]{:S(2)}, u32[]{:S(2)}) collective-permute-start(bf16[2,768]{1,0:T(2,128)(2,1)S(1)} %get-tuple-element.20), channel_id=1, source_target_pairs={{1,0},{2,1},{3,2},{4,3},{5,4},{6,5},{7,6},{8,7},{9,8},{10,9},{11,1... | collective-permute-start | bytes 9224 | tf_op jit(solution)/shard_map/ppermute | solution.py:21
  21.5 105.3 %all-gather.2.cloned.1.call-done = bf16[5,768,384]{2,1,0:T(8,128)(2,1)} async-done(((bf16[5,48,384]{2,1,0:T(8,128)(2,1)}), bf16[5,768,384]{2,1,0:T(8,128)(2,1)}) %all-gather.2.cloned.1.call-update) | async-done | bytes 2949136 | tf_op jit(solution)/shard_map/all_gather | solution.py:159
  126.8 3.1 collective-permute-start.2
  137.0 7.4 %dot_general.77 = bf16[128,4,3840]{2,1,0:T(4,128)(2,1)} reshape(bf16[512,3840]{1,0:T(8,128)(2,1)} %slice_dynamic-update-slice_fusion) | data formatting | bytes 7864320 | tf_op jit(solution)/shard_map/dot_general | solution.py:131
  144.4 5.3 %fusion.14 = f32[128,4,384]{2,0,1:T(8,128)S(1)} fusion(bf16[3840,384,1]{1,0,2:T(8,128)(2,1)} %bitcast.152, bf16[128,4,3840]{2,1,0:T(4,128)(2,1)} %dot_general.77), kind=kOutput, calls=%fused_computation.28 | convolution fusion | flops 1509949440 | bytes 7667712 | tf_op jit(solution)/shard_map/dot_general | solution.py:131
  149.8 4.0 %fusion.12 = f32[128,4,384]{2,0,1:T(8,128)S(1)} fusion(bf16[3840,384,1]{1,0,2:T(8,128)(2,1)} %bitcast.6, bf16[128,4,3840]{2,1,0:T(4,128)(2,1)S(1)} %copy-done.4), kind=kOutput, calls=%fused_computation.26 | convolution fusion | flops 1509949440 | bytes 7667712 | tf_op jit(solution)/shard_map/dot_general | solution.py:131
  155.7 3.6 collective-permute-start.3
  159.3 1.9 collective-permute-start.4
  161.3 2.2 collective-permute-start.5
  163.5 11.3 %collective-permute-done.4 = bf16[128,640]{1,0:T(8,128)(2,1)S(1)} collective-permute-done((bf16[128,640]{1,0:T(8,128)(2,1)S(1)}, bf16[128,640]{1,0:T(8,128)(2,1)S(1)}, u32[]{:S(2)}, u32[]{:S(2)}) %collective-permute-start.4) | collective-permute-done | bytes 163872 | tf_op jit(solution)/shard_map/ppermute | solution.py:49
  174.9 3.7 collective-permute-start.6
  178.6 2.4 collective-permute-start.7
  181.1 2.3 collective-permute-start.8
  183.4 9.2 %collective-permute-done.6 = bf16[4,128,640]{2,1,0:T(8,128)(2,1)S(1)} collective-permute-done((bf16[4,128,640]{2,1,0:T(8,128)(2,1)S(1)}, bf16[4,128,640]{2,1,0:T(8,128)(2,1)S(1)}, u32[]{:S(2)}, u32[]{:S(2)}) %collective-permute-start.6) | collective-permute-done | bytes 655392 | tf_op jit(solution)/shard_map/ppermute | solution.py:49
  192.6 4.3 %collective-permute-done.7 = bf16[4,128,640]{2,1,0:T(8,128)(2,1)S(1)} collective-permute-done((bf16[4,128,640]{2,1,0:T(8,128)(2,1)S(1)}, bf16[4,128,640]{2,1,0:T(8,128)(2,1)S(1)}, u32[]{:S(2)}, u32[]{:S(2)}) %collective-permute-start.7) | collective-permute-done | bytes 655392 | tf_op jit(solution)/shard_map/ppermute | solution.py:49
  196.9 15.8 %collective-permute-done.8 = bf16[4,128,640]{2,1,0:T(8,128)(2,1)S(1)} collective-permute-done((bf16[4,128,640]{2,1,0:T(8,128)(2,1)S(1)}, bf16[4,128,640]{2,1,0:T(8,128)(2,1)S(1)}, u32[]{:S(2)}, u32[]{:S(2)}) %collective-permute-start.8) | collective-permute-done | bytes 655392 | tf_op jit(solution)/shard_map/ppermute | solution.py:49
  212.7 1.8 fusion.121
  214.5 2.6 collective-permute-start.9
  220.2 1.9 convolution_convert_fusion
  222.1 2.0 fusion.125
  228.4 2.3 pad_maximum_fusion
  237.9 3.7 fusion.33
  241.7 3.5 fusion.34
  245.3 3.4 fusion.35
  248.7 3.0 multiply_reduce_fusion.3
  255.1 2.8 pad_maximum_fusion.2
  257.9 2.2 reshape.361
  260.1 1.9 collective-permute-start.10
  262.2 2.6 collective-permute-done.10
  266.2 4.1 %collective-permute-start.11 = (f32[4,15360]{1,0:T(4,128)S(1)}, f32[4,15360]{1,0:T(4,128)S(1)}, u32[]{:S(2)}, u32[]{:S(2)}) collective-permute-start(f32[4,15360]{1,0:T(4,128)S(1)} %get-tuple-element.16), channel_id=1, source_target_pairs={{32,0},{64,32},{96,64},{0,96},{160,128},{192,160},{224,192},{128,2... | collective-permute-start | bytes 737288 | tf_op jit(solution)/shard_map/ppermute | solution.py:49
  270.4 2.7 collective-permute-start.12
  273.1 2.3 collective-permute-start.13
  276.0 4.9 %collective-permute-done.12 = f32[4,15360]{1,0:T(4,128)S(1)} collective-permute-done((f32[4,15360]{1,0:T(4,128)S(1)}, f32[4,15360]{1,0:T(4,128)S(1)}, u32[]{:S(2)}, u32[]{:S(2)}) %collective-permute-start.12) | collective-permute-done | bytes 245792 | tf_op jit(solution)/shard_map/ppermute | solution.py:49
  280.9 6.0 %collective-permute-done.13 = f32[4,15360]{1,0:T(4,128)S(1)} collective-permute-done((f32[4,15360]{1,0:T(4,128)S(1)}, f32[4,15360]{1,0:T(4,128)S(1)}, u32[]{:S(2)}, u32[]{:S(2)}) %collective-permute-start.13) | collective-permute-done | bytes 245792 | tf_op jit(solution)/shard_map/ppermute | solution.py:49
  287.2 2.2 collective-permute-start.14
  289.5 2.5 collective-permute-start.15
  291.9 2.5 collective-permute-start.16
  296.0 2.5 collective-permute-done.16
  298.5 2.4 collective-permute-start.17
  300.8 3.8 collective-permute-start.18
  304.6 3.4 collective-permute-start.19
  308.0 3.4 collective-permute-done.19
  312.5 4.2 %collective-permute-start.20 = (f32[15360]{0:T(1024)S(1)}, f32[15360]{0:T(1024)S(1)}, u32[]{:S(2)}, u32[]{:S(2)}) collective-permute-start(f32[15360]{0:T(1024)S(1)} %bitcast.128), channel_id=1, source_target_pairs={{128,0},{160,32},{192,64},{224,96},{256,128},{288,160},{320,192},{... | collective-permute-start | bytes 184328 | tf_op jit(solution)/shard_map/ppermute | solution.py:49
  316.7 7.8 %collective-permute-start.21 = (f32[15360]{0:T(1024)S(1)}, f32[15360]{0:T(1024)S(1)}, u32[]{:S(2)}, u32[]{:S(2)}) collective-permute-start(f32[15360]{0:T(1024)S(1)} %bitcast.129), channel_id=1, source_target_pairs={{256,0},{288,32},{320,64},{352,96},{384,128},{416,160},{448,192},{... | collective-permute-start | bytes 184328 | tf_op jit(solution)/shard_map/ppermute | solution.py:49
  324.4 4.3 %collective-permute-start.22 = (f32[15360]{0:T(1024)S(1)}, f32[15360]{0:T(1024)S(1)}, u32[]{:S(2)}, u32[]{:S(2)}) collective-permute-start(f32[15360]{0:T(1024)S(1)} %bitcast.130), channel_id=1, source_target_pairs={{384,0},{416,32},{448,64},{480,96},{0,128},{32,160},{64,192},{96,2... | collective-permute-start | bytes 184328 | tf_op jit(solution)/shard_map/ppermute | solution.py:49
  328.8 1.7 collective-permute-done.21
  330.5 7.6 %collective-permute-done.22 = f32[15360]{0:T(1024)S(1)} collective-permute-done((f32[15360]{0:T(1024)S(1)}, f32[15360]{0:T(1024)S(1)}, u32[]{:S(2)}, u32[]{:S(2)}) %collective-permute-start.22) | collective-permute-done | bytes 61472 | tf_op jit(solution)/shard_map/ppermute | solution.py:49
  339.2 1.9 collective-permute-start.23
  341.1 1.9 collective-permute-start.24
  343.1 3.4 collective-permute-start.25
  347.6 2.8 collective-permute-done.25
  351.4 2.1 collective-permute-start.26
  353.4 2.1 collective-permute-start.27
  355.5 3.2 collective-permute-start.28
  358.8 3.1 collective-permute-done.27
  361.9 3.5 collective-permute-done.28
  366.7 8.1 %collective-permute-start.29 = (f32[4,4,15360]{2,1,0:T(4,128)S(1)}, f32[4,4,15360]{2,1,0:T(4,128)S(1)}, u32[]{:S(2)}, u32[]{:S(2)}) collective-permute-start(f32[4,4,15360]{2,1,0:T(4,128)S(1)} %gather_fusion.3), channel_id=1, source_target_pairs={{1,0},{0,1},{3,2},{2,3},{5,4},{4,5},{7,6},{6,7},{9,8},{8,9},{11,10... | collective-permute-start | bytes 2949128 | tf_op jit(solution)/shard_map/ppermute | solution.py:49
  377.0 1.7 pad_maximum_fusion.3
  378.7 3.3 gather_fusion.4
  382.0 2.3 slice.204
  384.3 2.3 slice.202
  386.6 2.4 slice.254
  389.0 2.1 slice.253
  (145 shorter events, 40.2 us)
Async XLA Ops:
  7.2 213.0 %copy-start = (bf16[384,768]{1,0:T(8,128)(2,1)S(1)}, bf16[384,768]{1,0:T(8,128)(2,1)}, u32[]{:S(2)}) copy-start(bf16[384,768]{1,0:T(8,128)(2,1)} %param.13) | copy-start | bytes 1769476
  7.2 122.7 %copy-start.2 = (bf16[1,512,768]{2,1,0:T(8,128)(2,1)S(1)}, bf16[1,512,768]{2,1,0:T(8,128)(2,1)}, u32[]{:S(2)}) copy-start(bf16[1,512,768]{2,1,0:T(8,128)(2,1)} %param.8) | copy-start | bytes 2359300
  7.2 119.6 %all-gather.2.cloned.1.call-start = ((), (), s32[]{:S(2)}) async-start(), calls=%async_computation | async-start | bytes 3133440 | tf_op jit(solution)/shard_map/all_gather | solution.py:159
  9.7 120.2 %collective-permute-start = (bf16[2,768]{1,0:T(2,128)(2,1)S(1)}, bf16[2,768]{1,0:T(2,128)(2,1)S(1)}, u32[]{:S(2)}, u32[]{:S(2)}) collective-permute-start(bf16[2,768]{1,0:T(2,128)(2,1)S(1)} %get-tuple-element.19), channel_id=1, source_target_pairs={{0,1},{1,2},{2,3},{3,4},{4,5},{5,6},{6,7},{7,8},{8,9},{9,10},{10,1... | collective-permute-start | bytes 9224 | tf_op jit(solution)/shard_map/ppermute | solution.py:20
  14.7 115.2 %collective-permute-start.1 = (bf16[2,768]{1,0:T(2,128)(2,1)S(1)}, bf16[2,768]{1,0:T(2,128)(2,1)S(1)}, u32[]{:S(2)}, u32[]{:S(2)}) collective-permute-start(bf16[2,768]{1,0:T(2,128)(2,1)S(1)} %get-tuple-element.20), channel_id=1, source_target_pairs={{1,0},{2,1},{3,2},{4,3},{5,4},{6,5},{7,6},{8,7},{9,8},{10,9},{11,1... | collective-permute-start | bytes 9224 | tf_op jit(solution)/shard_map/ppermute | solution.py:21
  126.8 22.9 %collective-permute-start.2 = (bf16[5,768,384]{2,1,0:T(8,128)(2,1)}, bf16[5,768,384]{2,1,0:T(8,128)(2,1)}, u32[]{:S(2)}, u32[]{:S(2)}) collective-permute-start(bf16[5,768,384]{2,1,0:T(8,128)(2,1)} %all-gather.2.cloned.1.call-done), channel_id=1, source_target_pairs={{1,0},{0,1},{3,2},{2,3},{5,4},{4,5},{7,6},{6,7},{9,8},{8,9},{11,10... | collective-permute-start | bytes 8847368 | tf_op jit(solution)/shard_map/ppermute | solution.py:49
  144.4 5.4 %copy-start.4 = (bf16[128,4,3840]{2,1,0:T(4,128)(2,1)S(1)}, bf16[128,4,3840]{2,1,0:T(4,128)(2,1)}, u32[]{:S(2)}) copy-start(bf16[128,4,3840]{2,1,0:T(4,128)(2,1)} %dot_general.77) | copy-start | bytes 11796484
  153.8 1.0 copy-start.10
  153.8 1.5 copy-start.24
  154.4 98.6 %copy-start.3 = (bf16[128,768]{1,0:T(8,128)(2,1)}, bf16[128,768]{1,0:T(8,128)(2,1)S(1)}, u32[]{:S(2)}) copy-start(bf16[128,768]{1,0:T(8,128)(2,1)S(1)} %fusion.27) | copy-start | bytes 589828
  155.7 7.7 %collective-permute-start.3 = (bf16[128,640]{1,0:T(8,128)(2,1)S(1)}, bf16[128,640]{1,0:T(8,128)(2,1)S(1)}, u32[]{:S(2)}, u32[]{:S(2)}) collective-permute-start(bf16[128,640]{1,0:T(8,128)(2,1)S(1)} %get-tuple-element.32), channel_id=1, source_target_pairs={{2,0},{3,1},{4,2},{5,3},{6,4},{7,5},{0,6},{1,7},{10,8},{11,9},{12,... | collective-permute-start | bytes 491528 | tf_op jit(solution)/shard_map/ppermute | solution.py:49
  159.3 15.5 %collective-permute-start.4 = (bf16[128,640]{1,0:T(8,128)(2,1)S(1)}, bf16[128,640]{1,0:T(8,128)(2,1)S(1)}, u32[]{:S(2)}, u32[]{:S(2)}) collective-permute-start(bf16[128,640]{1,0:T(8,128)(2,1)S(1)} %get-tuple-element.32), channel_id=1, source_target_pairs={{4,0},{5,1},{6,2},{7,3},{0,4},{1,5},{2,6},{3,7},{12,8},{13,9},{14,... | collective-permute-start | bytes 491528 | tf_op jit(solution)/shard_map/ppermute | solution.py:49
  161.3 13.5 %collective-permute-start.5 = (bf16[128,640]{1,0:T(8,128)(2,1)S(1)}, bf16[128,640]{1,0:T(8,128)(2,1)S(1)}, u32[]{:S(2)}, u32[]{:S(2)}) collective-permute-start(bf16[128,640]{1,0:T(8,128)(2,1)S(1)} %get-tuple-element.32), channel_id=1, source_target_pairs={{6,0},{7,1},{0,2},{1,3},{2,4},{3,5},{4,6},{5,7},{14,8},{15,9},{8,1... | collective-permute-start | bytes 491528 | tf_op jit(solution)/shard_map/ppermute | solution.py:49
  174.9 17.7 %collective-permute-start.6 = (bf16[4,128,640]{2,1,0:T(8,128)(2,1)S(1)}, bf16[4,128,640]{2,1,0:T(8,128)(2,1)S(1)}, u32[]{:S(2)}, u32[]{:S(2)}) collective-permute-start(bf16[4,128,640]{2,1,0:T(8,128)(2,1)S(1)} %get-tuple-element.22), channel_id=1, source_target_pairs={{8,0},{9,1},{10,2},{11,3},{12,4},{13,5},{14,6},{15,7},{16,8},{17,9... | collective-permute-start | bytes 1966088 | tf_op jit(solution)/shard_map/ppermute | solution.py:49
  178.6 18.3 %collective-permute-start.7 = (bf16[4,128,640]{2,1,0:T(8,128)(2,1)S(1)}, bf16[4,128,640]{2,1,0:T(8,128)(2,1)S(1)}, u32[]{:S(2)}, u32[]{:S(2)}) collective-permute-start(bf16[4,128,640]{2,1,0:T(8,128)(2,1)S(1)} %get-tuple-element.22), channel_id=1, source_target_pairs={{16,0},{17,1},{18,2},{19,3},{20,4},{21,5},{22,6},{23,7},{24,8},{25... | collective-permute-start | bytes 1966088 | tf_op jit(solution)/shard_map/ppermute | solution.py:49
  181.1 31.6 %collective-permute-start.8 = (bf16[4,128,640]{2,1,0:T(8,128)(2,1)S(1)}, bf16[4,128,640]{2,1,0:T(8,128)(2,1)S(1)}, u32[]{:S(2)}, u32[]{:S(2)}) collective-permute-start(bf16[4,128,640]{2,1,0:T(8,128)(2,1)S(1)} %get-tuple-element.22), channel_id=1, source_target_pairs={{24,0},{25,1},{26,2},{27,3},{28,4},{29,5},{30,6},{31,7},{0,8},{1,9... | collective-permute-start | bytes 1966088 | tf_op jit(solution)/shard_map/ppermute | solution.py:49
  212.7 4.4 %copy-start.23 = (f32[4]{0:T(128)S(1)}, f32[4]{0:T(128)}, u32[]{:S(2)}) copy-start(f32[4]{0:T(128)} %param.14) | copy-start | bytes 52
  214.5 13.9 %collective-permute-start.9 = (bf16[4,4,128,640]{3,2,1,0:T(8,128)(2,1)}, bf16[4,4,128,640]{3,2,1,0:T(8,128)(2,1)}, u32[]{:S(2)}, u32[]{:S(2)}) collective-permute-start(bf16[4,4,128,640]{3,2,1,0:T(8,128)(2,1)} %get-tuple-element.15), channel_id=1, source_target_pairs={{1,0},{0,1},{3,2},{2,3},{5,4},{4,5},{7,6},{6,7},{9,8},{8,9},{11,10... | collective-permute-start | bytes 7864328 | tf_op jit(solution)/shard_map/ppermute | solution.py:49
  230.6 6.1 %copy-start.1 = (bf16[2,4,4,128,640]{4,3,2,1,0:T(8,128)(2,1)}, bf16[2,4,4,128,640]{4,3,2,1,0:T(8,128)(2,1)S(1)}, u32[]{:S(2)}) copy-start(bf16[2,4,4,128,640]{4,3,2,1,0:T(8,128)(2,1)S(1)} %pad_maximum_fusion) | copy-start | bytes 15728644
  231.8 1.8 copy-start.5
  232.4 2.2 copy-start.6
  233.1 2.6 copy-start.7
  235.7 1.1 copy-start.11
  237.9 16.8 %copy-start.12 = (bf16[128,96]{0,1:T(8,128)(2,1)}, bf16[128,96]{0,1:T(8,128)(2,1)S(1)}, u32[]{:S(2)}) copy-start(bf16[128,96]{0,1:T(8,128)(2,1)S(1)} %get-tuple-element.33) | copy-start | bytes 73732
  237.9 16.8 %copy-start.14 = (bf16[128,96]{0,1:T(8,128)(2,1)}, bf16[128,96]{0,1:T(8,128)(2,1)S(1)}, u32[]{:S(2)}) copy-start(bf16[128,96]{0,1:T(8,128)(2,1)S(1)} %get-tuple-element.34) | copy-start | bytes 73732
  241.7 7.0 %copy-start.20 = (f32[128,64]{1,0:T(8,128)}, f32[128,64]{1,0:T(8,128)S(1)}, u32[]{:S(2)}) copy-start(f32[128,64]{1,0:T(8,128)S(1)} %fusion.33) | copy-start | bytes 98308
  245.2 3.5 copy-start.21
  245.2 3.5 copy-start.8
  248.7 3.1 copy-start.22
  251.8 2.9 copy-start.9
  251.8 2.9 copy-start.16
  251.8 2.9 copy-start.18
  260.1 4.6 %collective-permute-start.10 = (f32[4,4,15360]{2,1,0:T(4,128)S(1)}, f32[4,4,15360]{2,1,0:T(4,128)}, u32[]{:S(2)}, u32[]{:S(2)}) collective-permute-start(f32[4,4,15360]{2,1,0:T(4,128)S(1)} %dynamic-slice_bitcast_fusion), channel_id=1, source_target_pairs={{1,0},{0,1},{3,2},{2,3},{5,4},{4,5},{7,6},{6,7},{9,8},{8,9},{11,10... | collective-permute-start | bytes 2949128 | tf_op jit(solution)/shard_map/ppermute | solution.py:49
  266.2 9.7 %collective-permute-start.11 = (f32[4,15360]{1,0:T(4,128)S(1)}, f32[4,15360]{1,0:T(4,128)S(1)}, u32[]{:S(2)}, u32[]{:S(2)}) collective-permute-start(f32[4,15360]{1,0:T(4,128)S(1)} %get-tuple-element.16), channel_id=1, source_target_pairs={{32,0},{64,32},{96,64},{0,96},{160,128},{192,160},{224,192},{128,2... | collective-permute-start | bytes 737288 | tf_op jit(solution)/shard_map/ppermute | solution.py:49
  270.4 10.5 %collective-permute-start.12 = (f32[4,15360]{1,0:T(4,128)S(1)}, f32[4,15360]{1,0:T(4,128)S(1)}, u32[]{:S(2)}, u32[]{:S(2)}) collective-permute-start(f32[4,15360]{1,0:T(4,128)S(1)} %get-tuple-element.18), channel_id=1, source_target_pairs={{64,0},{96,32},{0,64},{32,96},{192,128},{224,160},{128,192},{160,2... | collective-permute-start | bytes 737288 | tf_op jit(solution)/shard_map/ppermute | solution.py:49
  273.1 13.8 %collective-permute-start.13 = (f32[4,15360]{1,0:T(4,128)S(1)}, f32[4,15360]{1,0:T(4,128)S(1)}, u32[]{:S(2)}, u32[]{:S(2)}) collective-permute-start(f32[4,15360]{1,0:T(4,128)S(1)} %get-tuple-element.17), channel_id=1, source_target_pairs={{96,0},{0,32},{32,64},{64,96},{224,128},{128,160},{160,192},{192,2... | collective-permute-start | bytes 737288 | tf_op jit(solution)/shard_map/ppermute | solution.py:49
  287.2 7.2 %collective-permute-start.14 = (f32[15360]{0:T(1024)S(1)}, f32[15360]{0:T(1024)S(1)}, u32[]{:S(2)}, u32[]{:S(2)}) collective-permute-start(f32[15360]{0:T(1024)S(1)} %bitcast.142), channel_id=1, source_target_pairs={{8,0},{9,1},{10,2},{11,3},{12,4},{13,5},{14,6},{15,7},{16,8},{17,9... | collective-permute-start | bytes 184328 | tf_op jit(solution)/shard_map/ppermute | solution.py:49
  289.5 6.5 %collective-permute-start.15 = (f32[15360]{0:T(1024)S(1)}, f32[15360]{0:T(1024)S(1)}, u32[]{:S(2)}, u32[]{:S(2)}) collective-permute-start(f32[15360]{0:T(1024)S(1)} %bitcast.141), channel_id=1, source_target_pairs={{16,0},{17,1},{18,2},{19,3},{20,4},{21,5},{22,6},{23,7},{24,8},{25... | collective-permute-start | bytes 184328 | tf_op jit(solution)/shard_map/ppermute | solution.py:49
  291.9 6.5 %collective-permute-start.16 = (f32[15360]{0:T(1024)S(1)}, f32[15360]{0:T(1024)S(1)}, u32[]{:S(2)}, u32[]{:S(2)}) collective-permute-start(f32[15360]{0:T(1024)S(1)} %bitcast.140), channel_id=1, source_target_pairs={{24,0},{25,1},{26,2},{27,3},{28,4},{29,5},{30,6},{31,7},{0,8},{1,9... | collective-permute-start | bytes 184328 | tf_op jit(solution)/shard_map/ppermute | solution.py:49
  298.5 9.6 %collective-permute-start.17 = (f32[15360]{0:T(1024)S(1)}, f32[15360]{0:T(1024)S(1)}, u32[]{:S(2)}, u32[]{:S(2)}) collective-permute-start(f32[15360]{0:T(1024)S(1)} %add_add_fusion), channel_id=1, source_target_pairs={{2,0},{3,1},{4,2},{5,3},{6,4},{7,5},{0,6},{1,7},{10,8},{11,9},{12,... | collective-permute-start | bytes 184328 | tf_op jit(solution)/shard_map/ppermute | solution.py:49
  300.8 7.2 %collective-permute-start.18 = (f32[15360]{0:T(1024)S(1)}, f32[15360]{0:T(1024)S(1)}, u32[]{:S(2)}, u32[]{:S(2)}) collective-permute-start(f32[15360]{0:T(1024)S(1)} %add_add_fusion), channel_id=1, source_target_pairs={{4,0},{5,1},{6,2},{7,3},{0,4},{1,5},{2,6},{3,7},{12,8},{13,9},{14,... | collective-permute-start | bytes 184328 | tf_op jit(solution)/shard_map/ppermute | solution.py:49
  304.6 6.8 %collective-permute-start.19 = (f32[15360]{0:T(1024)S(1)}, f32[15360]{0:T(1024)S(1)}, u32[]{:S(2)}, u32[]{:S(2)}) collective-permute-start(f32[15360]{0:T(1024)S(1)} %add_add_fusion), channel_id=1, source_target_pairs={{6,0},{7,1},{0,2},{1,3},{2,4},{3,5},{4,6},{5,7},{14,8},{15,9},{8,1... | collective-permute-start | bytes 184328 | tf_op jit(solution)/shard_map/ppermute | solution.py:49
  312.5 16.3 %collective-permute-start.20 = (f32[15360]{0:T(1024)S(1)}, f32[15360]{0:T(1024)S(1)}, u32[]{:S(2)}, u32[]{:S(2)}) collective-permute-start(f32[15360]{0:T(1024)S(1)} %bitcast.128), channel_id=1, source_target_pairs={{128,0},{160,32},{192,64},{224,96},{256,128},{288,160},{320,192},{... | collective-permute-start | bytes 184328 | tf_op jit(solution)/shard_map/ppermute | solution.py:49
  316.7 13.8 %collective-permute-start.21 = (f32[15360]{0:T(1024)S(1)}, f32[15360]{0:T(1024)S(1)}, u32[]{:S(2)}, u32[]{:S(2)}) collective-permute-start(f32[15360]{0:T(1024)S(1)} %bitcast.129), channel_id=1, source_target_pairs={{256,0},{288,32},{320,64},{352,96},{384,128},{416,160},{448,192},{... | collective-permute-start | bytes 184328 | tf_op jit(solution)/shard_map/ppermute | solution.py:49
  324.4 13.7 %collective-permute-start.22 = (f32[15360]{0:T(1024)S(1)}, f32[15360]{0:T(1024)S(1)}, u32[]{:S(2)}, u32[]{:S(2)}) collective-permute-start(f32[15360]{0:T(1024)S(1)} %bitcast.130), channel_id=1, source_target_pairs={{384,0},{416,32},{448,64},{480,96},{0,128},{32,160},{64,192},{96,2... | collective-permute-start | bytes 184328 | tf_op jit(solution)/shard_map/ppermute | solution.py:49
  339.2 7.2 %collective-permute-start.23 = (f32[15360]{0:T(1024)S(1)}, f32[15360]{0:T(1024)S(1)}, u32[]{:S(2)}, u32[]{:S(2)}) collective-permute-start(f32[15360]{0:T(1024)S(1)} %bitcast.131), channel_id=1, source_target_pairs={{8,0},{9,1},{10,2},{11,3},{12,4},{13,5},{14,6},{15,7},{16,8},{17,9... | collective-permute-start | bytes 184328 | tf_op jit(solution)/shard_map/ppermute | solution.py:49
  341.1 6.5 %collective-permute-start.24 = (f32[15360]{0:T(1024)S(1)}, f32[15360]{0:T(1024)S(1)}, u32[]{:S(2)}, u32[]{:S(2)}) collective-permute-start(f32[15360]{0:T(1024)S(1)} %bitcast.132), channel_id=1, source_target_pairs={{16,0},{17,1},{18,2},{19,3},{20,4},{21,5},{22,6},{23,7},{24,8},{25... | collective-permute-start | bytes 184328 | tf_op jit(solution)/shard_map/ppermute | solution.py:49
  343.1 7.3 %collective-permute-start.25 = (f32[15360]{0:T(1024)S(1)}, f32[15360]{0:T(1024)S(1)}, u32[]{:S(2)}, u32[]{:S(2)}) collective-permute-start(f32[15360]{0:T(1024)S(1)} %bitcast.133), channel_id=1, source_target_pairs={{24,0},{25,1},{26,2},{27,3},{28,4},{29,5},{30,6},{31,7},{0,8},{1,9... | collective-permute-start | bytes 184328 | tf_op jit(solution)/shard_map/ppermute | solution.py:49
  351.3 23.5 %copy-start.13 = (bf16[128,96]{0,1:T(8,128)(2,1)S(1)}, bf16[128,96]{0,1:T(8,128)(2,1)}, u32[]{:S(2)}) copy-start(bf16[128,96]{0,1:T(8,128)(2,1)} %copy-done.12) | copy-start | bytes 73732
  351.3 23.5 %copy-start.15 = (bf16[128,96]{0,1:T(8,128)(2,1)S(1)}, bf16[128,96]{0,1:T(8,128)(2,1)}, u32[]{:S(2)}) copy-start(bf16[128,96]{0,1:T(8,128)(2,1)} %copy-done.14) | copy-start | bytes 73732
  351.3 23.5 %copy-start.17 = (bf16[128,96]{0,1:T(8,128)(2,1)S(1)}, bf16[128,96]{0,1:T(8,128)(2,1)}, u32[]{:S(2)}) copy-start(bf16[128,96]{0,1:T(8,128)(2,1)} %get-tuple-element.35) | copy-start | bytes 73732
  351.4 23.5 %copy-start.19 = (bf16[128,96]{0,1:T(8,128)(2,1)S(1)}, bf16[128,96]{0,1:T(8,128)(2,1)}, u32[]{:S(2)}) copy-start(bf16[128,96]{0,1:T(8,128)(2,1)} %get-tuple-element.36) | copy-start | bytes 73732
  351.4 7.4 %collective-permute-start.26 = (f32[4,15360]{1,0:T(4,128)S(1)}, f32[4,15360]{1,0:T(4,128)S(1)}, u32[]{:S(2)}, u32[]{:S(2)}) collective-permute-start(f32[4,15360]{1,0:T(4,128)S(1)} %gather_fusion.2), channel_id=1, source_target_pairs={{32,0},{64,32},{96,64},{0,96},{160,128},{192,160},{224,192},{128,2... | collective-permute-start | bytes 737288 | tf_op jit(solution)/shard_map/ppermute | solution.py:49
  353.4 8.4 %collective-permute-start.27 = (f32[4,15360]{1,0:T(4,128)S(1)}, f32[4,15360]{1,0:T(4,128)S(1)}, u32[]{:S(2)}, u32[]{:S(2)}) collective-permute-start(f32[4,15360]{1,0:T(4,128)S(1)} %gather_fusion.2), channel_id=1, source_target_pairs={{64,0},{96,32},{0,64},{32,96},{192,128},{224,160},{128,192},{160,2... | collective-permute-start | bytes 737288 | tf_op jit(solution)/shard_map/ppermute | solution.py:49
  355.5 9.9 %collective-permute-start.28 = (f32[4,15360]{1,0:T(4,128)S(1)}, f32[4,15360]{1,0:T(4,128)S(1)}, u32[]{:S(2)}, u32[]{:S(2)}) collective-permute-start(f32[4,15360]{1,0:T(4,128)S(1)} %gather_fusion.2), channel_id=1, source_target_pairs={{96,0},{0,32},{32,64},{64,96},{224,128},{128,160},{160,192},{192,2... | collective-permute-start | bytes 737288 | tf_op jit(solution)/shard_map/ppermute | solution.py:49
  366.7 10.3 %collective-permute-start.29 = (f32[4,4,15360]{2,1,0:T(4,128)S(1)}, f32[4,4,15360]{2,1,0:T(4,128)S(1)}, u32[]{:S(2)}, u32[]{:S(2)}) collective-permute-start(f32[4,4,15360]{2,1,0:T(4,128)S(1)} %gather_fusion.3), channel_id=1, source_target_pairs={{1,0},{0,1},{3,2},{2,3},{5,4},{4,5},{7,6},{6,7},{9,8},{8,9},{11,10... | collective-permute-start | bytes 2949128 | tf_op jit(solution)/shard_map/ppermute | solution.py:49
Sparse Core Ops, SparseCore 0:
  11.6 115.1 all-gather.1
